TPU v7x, 512 devices: a whole 4x4x16 slice. The times are simulated.
512 devices in a mesh: row: 16 (over x_hi, y, core), col: 32 (over z, x_lo).
Axes of the slice: x: 4 (x_hi: 2, x_lo: 2; x = x_hi * 2 + x_lo), y: 4, z: 16, core: 2. Of those that a mesh axis runs over, the one named last changes fastest.
Arguments:
- probes: bfloat16 [512, 262144], P(None, ('row', 'col')), may hold values from -6 to 6
- own_blocks: bfloat16 [3, 262144, 512], P(None, ('row', 'col')), may hold values from -0.1875 to 0.1875
- cross_blocks: bfloat16 [3, 262144, 512], P(None, ('row', 'col')), may hold values from -0.1875 to 0.1875
- level_perm: int32 [3, 262144], P(None, ('row', 'col')), may hold values from 0 to 511, as said below
Outputs:
- mixed: bfloat16 [512, 262144], P(None, ('row', 'col'))
Inputs may be any that keep to these rules, and one draw needn't show every extreme that they name: `level_perm`: each aligned run of 512 entries of a level is a permutation of 0 to 511.
All inputs are finite; a program needn't handle non-finite values.
Results may differ from a plain program's by a relative error of at most 0.0057.
Values may be sent and summed in bfloat16 or wider, within the bound.
No kernel may reach another device: no remote copies, remote signals or barrier semaphores. Data moves between devices by JAX's collectives and lax.ppermute only.
A program may use at most 64 MiB of HBM per device.

v0:
```python
import jax
import jax.numpy as jnp
from jax import lax
from jax.sharding import PartitionSpec as P


def from_partner(value, axis, distance):
    mask = 2**distance
    pairs = [(source, source ^ mask) for source in range(lax.axis_size(axis))]
    return lax.ppermute(value, axis, pairs)


def combine(panel, partner, own, cross):
    total = jnp.dot(panel, own, preferred_element_type=jnp.float32)
    return total + jnp.dot(partner, cross, preferred_element_type=jnp.float32)


def across_col(panel, own, cross, bit):
    other = from_partner(panel, "col", bit)
    return combine(panel, other, own, cross)


def across_row(panel, own, cross, bit):
    other = from_partner(panel, "row", bit)
    return combine(panel, other, own, cross)


def per_device(probes, own_blocks, cross_blocks, level_perm):
    col_bits = lax.axis_size("col").bit_length() - 1
    row_bits = lax.axis_size("row").bit_length() - 1
    panel = probes
    for level in range(3):
        own = own_blocks[level]
        cross = cross_blocks[level]
        order = level_perm[level]
        if level == 0:
            total = across_col(panel, own, cross, col_bits - 1)
        elif level == 1:
            total = across_row(panel, own, cross, row_bits - 1)
        else:
            total = across_col(panel, own, cross, 0)
        total = jnp.take(total, order, axis=1)
        panel = total.astype(jnp.bfloat16)
    return panel


def solution(mesh):
    placed = (
        P(None, ("row", "col")),
        P(None, ("row", "col"), None),
        P(None, ("row", "col"), None),
        P(None, ("row", "col")),
    )
    return jax.shard_map(
        per_device, mesh=mesh, in_specs=placed, out_specs=P(None, ("row", "col")), check_vma=False
    )
```

profile of v0, /device:TPU:34, one launch (start us, length us, event | category | flops | bytes accessed | tf_op | source)
XLA Modules:
  0.0 100.8 jit_solution(5631016557990575474)
XLA Ops:
  0.0 0.0 copy-start
  0.0 14.9 %collective-permute-start = (bf16[512,512]{1,0:T(8,128)(2,1)}, bf16[512,512]{1,0:T(8,128)(2,1)S(1)}, u32[]{:S(2)}, u32[]{:S(2)}) collective-permute-start(bf16[512,512]{1,0:T(8,128)(2,1)} %param.6), channel_id=1, source_target_pairs={{0,16},{1,17},{2,18},{3,19},{4,20},{5,21},{6,22},{7,23},{8,24},{9,... | collective-permute-start | bytes 1572872 | tf_op jit(solution)/shard_map/ppermute | solution.py:10
  15.0 0.8 fusion.15
  15.8 1.6 %fusion.7 = f32[512,512]{1,0:T(8,128)S(1)} fusion(bf16[512,512]{1,0:T(8,128)(2,1)} %param.6, bf16[3,512,512]{2,1,0:T(8,128)(2,1)} %param.7), kind=kOutput, calls=%fused_computation.16 | convolution fusion | flops 268435456 | bytes 2097152 | tf_op jit(solution)/shard_map/dot_general | solution.py:14
  17.5 43.7 %collective-permute-done = bf16[512,512]{1,0:T(8,128)(2,1)S(1)} collective-permute-done((bf16[512,512]{1,0:T(8,128)(2,1)}, bf16[512,512]{1,0:T(8,128)(2,1)S(1)}, u32[]{:S(2)}, u32[]{:S(2)}) %collective-permute-start) | collective-permute-done | bytes 524320 | tf_op jit(solution)/shard_map/ppermute | solution.py:10
  61.2 0.0 copy-done
  61.2 0.4 convolution_add_fusion.2
  61.6 0.2 copy.5
  61.8 2.0 %gather_fusion = bf16[512,512]{1,0:T(8,128)(2,1)S(1)} fusion(bf16[512,512]{0,1:T(8,128)(2,1)S(1)} %copy.5, s32[1024]{0:T(1024)S(1)} %pad_clamp_fusion.2), kind=kCustom, calls=%fused_computation.clone | custom fusion | bytes 1050624 | tf_op jit(solution)/shard_map/jit(_take)/gather | solution.py:42
  63.8 0.2 bitcast_convert_fusion.2
  64.0 4.0 %collective-permute-start.1 = (bf16[512,512]{0,1:T(8,128)(2,1)S(1)}, bf16[512,512]{0,1:T(8,128)(2,1)S(1)}, u32[]{:S(2)}, u32[]{:S(2)}) collective-permute-start(bf16[512,512]{0,1:T(8,128)(2,1)S(1)} %bitcast_convert_fusion.2), channel_id=1, source_target_pairs={{0,256},{32,288},{64,320},{96,352},{128,384},{160,416},{192,448},{... | collective-permute-start | bytes 1572872 | tf_op jit(solution)/shard_map/ppermute | solution.py:10
  68.1 1.5 %fusion.4 = f32[512,512]{1,0:T(8,128)S(1)} fusion(bf16[512,512]{0,1:T(8,128)(2,1)S(1)} %bitcast_convert_fusion.2, bf16[3,512,512]{2,1,0:T(8,128)(2,1)} %param.7), kind=kOutput, calls=%fused_computation.13 | convolution fusion | flops 268435456 | bytes 2097152 | tf_op jit(solution)/shard_map/dot_general | solution.py:14
  69.6 10.6 %collective-permute-done.1 = bf16[512,512]{0,1:T(8,128)(2,1)S(1)} collective-permute-done((bf16[512,512]{0,1:T(8,128)(2,1)S(1)}, bf16[512,512]{0,1:T(8,128)(2,1)S(1)}, u32[]{:S(2)}, u32[]{:S(2)}) %collective-permute-start.1) | collective-permute-done | bytes 524320 | tf_op jit(solution)/shard_map/ppermute | solution.py:10
  80.2 0.5 convolution_add_fusion.1
  80.7 0.2 copy.6
  80.9 2.0 %gather_fusion.1 = bf16[512,512]{1,0:T(8,128)(2,1)S(1)} fusion(bf16[512,512]{0,1:T(8,128)(2,1)S(1)} %copy.6, s32[1024]{0:T(1024)S(1)} %pad_clamp_fusion.1), kind=kCustom, calls=%fused_computation.1.clone | custom fusion | bytes 1050624 | tf_op jit(solution)/shard_map/jit(_take)/gather | solution.py:42
  82.9 0.2 bitcast_convert_fusion.1
  83.1 2.4 %collective-permute-start.2 = (bf16[512,512]{0,1:T(8,128)(2,1)S(1)}, bf16[512,512]{0,1:T(8,128)(2,1)S(1)}, u32[]{:S(2)}, u32[]{:S(2)}) collective-permute-start(bf16[512,512]{0,1:T(8,128)(2,1)S(1)} %bitcast_convert_fusion.1), channel_id=1, source_target_pairs={{0,1},{1,0},{2,3},{3,2},{4,5},{5,4},{6,7},{7,6},{8,9},{9,8},{10,11... | collective-permute-start | bytes 1572872 | tf_op jit(solution)/shard_map/ppermute | solution.py:10
  85.5 1.5 %fusion.1 = f32[512,512]{1,0:T(8,128)S(1)} fusion(bf16[512,512]{0,1:T(8,128)(2,1)S(1)} %bitcast_convert_fusion.1, bf16[3,512,512]{2,1,0:T(8,128)(2,1)} %param.7), kind=kOutput, calls=%fused_computation.10 | convolution fusion | flops 268435456 | bytes 2097152 | tf_op jit(solution)/shard_map/dot_general | solution.py:14
  87.0 9.8 %collective-permute-done.2 = bf16[512,512]{0,1:T(8,128)(2,1)S(1)} collective-permute-done((bf16[512,512]{0,1:T(8,128)(2,1)S(1)}, bf16[512,512]{0,1:T(8,128)(2,1)S(1)}, u32[]{:S(2)}, u32[]{:S(2)}) %collective-permute-start.2) | collective-permute-done | bytes 524320 | tf_op jit(solution)/shard_map/ppermute | solution.py:10
  96.9 0.5 convolution_add_fusion
  97.4 0.2 copy.7
  97.6 2.0 %gather_fusion.2 = bf16[512,512]{1,0:T(8,128)(2,1)S(1)} fusion(bf16[512,512]{0,1:T(8,128)(2,1)S(1)} %copy.7, s32[1024]{0:T(1024)S(1)} %pad_clamp_fusion), kind=kCustom, calls=%fused_computation.2.clone | custom fusion | bytes 1050624 | tf_op jit(solution)/shard_map/jit(_take)/gather | solution.py:42
  99.6 0.2 bitcast_convert_fusion
  99.8 1.0 copy.8
  (9 shorter events, 0.1 us)
Async XLA Ops:
  0.0 61.2 %copy-start = (bf16[3,512,512]{2,1,0:T(8,128)(2,1)S(1)}, bf16[3,512,512]{2,1,0:T(8,128)(2,1)}, u32[]{:S(2)}) copy-start(bf16[3,512,512]{2,1,0:T(8,128)(2,1)} %param.8) | copy-start | bytes 4718596
  0.0 61.2 %collective-permute-start = (bf16[512,512]{1,0:T(8,128)(2,1)}, bf16[512,512]{1,0:T(8,128)(2,1)S(1)}, u32[]{:S(2)}, u32[]{:S(2)}) collective-permute-start(bf16[512,512]{1,0:T(8,128)(2,1)} %param.6), channel_id=1, source_target_pairs={{0,16},{1,17},{2,18},{3,19},{4,20},{5,21},{6,22},{7,23},{8,24},{9,... | collective-permute-start | bytes 1572872 | tf_op jit(solution)/shard_map/ppermute | solution.py:10
  64.0 16.2 %collective-permute-start.1 = (bf16[512,512]{0,1:T(8,128)(2,1)S(1)}, bf16[512,512]{0,1:T(8,128)(2,1)S(1)}, u32[]{:S(2)}, u32[]{:S(2)}) collective-permute-start(bf16[512,512]{0,1:T(8,128)(2,1)S(1)} %bitcast_convert_fusion.2), channel_id=1, source_target_pairs={{0,256},{32,288},{64,320},{96,352},{128,384},{160,416},{192,448},{... | collective-permute-start | bytes 1572872 | tf_op jit(solution)/shard_map/ppermute | solution.py:10
  83.1 13.8 %collective-permute-start.2 = (bf16[512,512]{0,1:T(8,128)(2,1)S(1)}, bf16[512,512]{0,1:T(8,128)(2,1)S(1)}, u32[]{:S(2)}, u32[]{:S(2)}) collective-permute-start(bf16[512,512]{0,1:T(8,128)(2,1)S(1)} %bitcast_convert_fusion.1), channel_id=1, source_target_pairs={{0,1},{1,0},{2,3},{3,2},{4,5},{5,4},{6,7},{7,6},{8,9},{9,8},{10,11... | collective-permute-start | bytes 1572872 | tf_op jit(solution)/shard_map/ppermute | solution.py:10
where the time goes:
time: 101 us
  waiting for transfers between devices  64.2 us (64%)
  starting transfers between devices  21.4 us (21%)
  local copies, waits for them, and re-layouts  8.38 us (8%)
  matrix products  6.01 us (6%)
    ppermute x3, waiting for transfers between devices, from_partner(): return lax.ppermute(value, axis, pairs)  64.2 us
    ppermute x3, starting transfers between devices, from_partner(): return lax.ppermute(value, axis, pairs)  21.4 us
    gather x3, local copies, waits for them, and re-layouts, per_device(): total = jnp.take(total, order, axis=1)  5.91 us
    dot_general x3, matrix products, combine(): total = jnp.dot(panel, own, preferred_element_type=jnp.float32)  4.64 us
  transfers between devices with their start and end apart: 3, of which 3 were waited for; matrix products, arithmetic and copies ran while one was open for 5% of the time, Pallas kernels for 0%

commit v1 on v0

v1 whole, which is shorter than its diff:
```python
import jax
import jax.numpy as jnp
from jax import lax
from jax.sharding import PartitionSpec as P

CHUNKS = 2


def from_partner(value, axis, distance):
    mask = 2**distance
    pairs = [(source, source ^ mask) for source in range(lax.axis_size(axis))]
    return lax.ppermute(value, axis, pairs)


def permuted_columns(weights, order):
    n = weights.shape[-1]
    onehot = (lax.broadcasted_iota(jnp.int32, (n, n), 0) == order[None, :]).astype(weights.dtype)
    return jnp.dot(weights, onehot, preferred_element_type=jnp.float32).astype(weights.dtype)


def per_device(probes, own_blocks, cross_blocks, level_perm):
    col_bits = lax.axis_size("col").bit_length() - 1
    row_bits = lax.axis_size("row").bit_length() - 1
    plan = [("col", col_bits - 1), ("row", row_bits - 1), ("col", 0)]
    br = own_blocks.shape[1]
    weights = []
    for level in range(3):
        both = jnp.concatenate([own_blocks[level], cross_blocks[level]], axis=0)
        both = permuted_columns(both, level_perm[level])
        weights.append((both[:br], both[br:]))
    rows = probes.shape[0] // CHUNKS
    outs = []
    for chunk in range(CHUNKS):
        panel = probes[chunk * rows:(chunk + 1) * rows]
        for level, (axis, bit) in enumerate(plan):
            own, cross = weights[level]
            other = from_partner(panel, axis, bit)
            total = jnp.dot(panel, own, preferred_element_type=jnp.float32)
            total = total + jnp.dot(other, cross, preferred_element_type=jnp.float32)
            panel = total.astype(jnp.bfloat16)
        outs.append(panel)
    return jnp.concatenate(outs, axis=0)


def solution(mesh):
    placed = (
        P(None, ("row", "col")),
        P(None, ("row", "col"), None),
        P(None, ("row", "col"), None),
        P(None, ("row", "col")),
    )
    return jax.shard_map(
        per_device, mesh=mesh, in_specs=placed, out_specs=P(None, ("row", "col")), check_vma=False
    )
```

time: 101 us -> 86 us (0.85)
  the two profiles are of different devices: /device:TPU:34 before, /device:TPU:48 now
where the time goes in v1:
time: 86 us; the launch traced here: 85.6 us
  waiting for transfers between devices  41.3 us (48%)
  starting transfers between devices  33 us (38%)
  matrix products  6.1 us (7%)
  local copies, waits for them, and re-layouts  4.19 us (5%)
    ppermute x6, waiting for transfers between devices, from_partner(): return lax.ppermute(value, axis, pairs)  41.3 us
    ppermute x6, starting transfers between devices, from_partner(): return lax.ppermute(value, axis, pairs)  33 us
    dot_general x3, matrix products, permuted_columns(): jnp.dot(weights, onehot, preferred_element_type=jnp.float32)  2.27 us
    squeeze x1, local copies, waits for them, and re-layouts, per_device(): both = jnp.concatenate([own_blocks[level], cross_blocks[level]], axis=0)  2.03 us
    dot_general x6, matrix products, per_device(): total = total + jnp.dot(other, cross, preferred_element_type=jnp.float32)  1.93 us
    dot_general x6, matrix products, per_device(): total = jnp.dot(panel, own, preferred_element_type=jnp.float32)  1.89 us
  transfers between devices with their start and end apart: 6, of which 4 were waited for; matrix products, arithmetic and copies ran while one was open for 10% of the time, Pallas kernels for 0%

profile of v1, /device:TPU:48, one launch (start us, length us, event | category | flops | bytes accessed | tf_op | source)
XLA Modules:
  0.0 85.6 jit_solution(12104345492733114622)
XLA Ops:
  0.0 1.1 %fusion.41 = (bf16[256,512]{1,0:T(8,128)(2,1)S(1)}, bf16[256,512]{1,0:T(8,128)(2,1)S(1)}) fusion(bf16[512,512]{1,0:T(8,128)(2,1)} %param.4), kind=kLoop, calls=%fused_computation.60 | loop fusion | bytes 1048576 | tf_op jit(solution)/shard_map/slice | solution.py:34
  1.1 14.8 %collective-permute-start = (bf16[256,512]{1,0:T(8,128)(2,1)S(1)}, bf16[256,512]{1,0:T(8,128)(2,1)S(1)}, u32[]{:S(2)}, u32[]{:S(2)}) collective-permute-start(bf16[256,512]{1,0:T(8,128)(2,1)S(1)} %get-tuple-element.11), channel_id=1, source_target_pairs={{0,16},{1,17},{2,18},{3,19},{4,20},{5,21},{6,22},{7,23},{8,24},{9,... | collective-permute-start | bytes 786440 | tf_op jit(solution)/shard_map/ppermute | solution.py:12
  15.9 1.9 %collective-permute-start.3 = (bf16[256,512]{1,0:T(8,128)(2,1)S(1)}, bf16[256,512]{1,0:T(8,128)(2,1)S(1)}, u32[]{:S(2)}, u32[]{:S(2)}) collective-permute-start(bf16[256,512]{1,0:T(8,128)(2,1)S(1)} %get-tuple-element.12), channel_id=1, source_target_pairs={{0,16},{1,17},{2,18},{3,19},{4,20},{5,21},{6,22},{7,23},{8,24},{9,... | collective-permute-start | bytes 786440 | tf_op jit(solution)/shard_map/ppermute | solution.py:12
  17.8 0.8 fusion.42
  18.6 2.0 %slice_bitcast_fusion = (bf16[512,512]{1,0:T(8,128)(2,1)S(1)}, bf16[512,512]{1,0:T(8,128)(2,1)S(1)}, bf16[512,512]{1,0:T(8,128)(2,1)S(1)}, bf16[512,512]{1,0:T(8...) fusion(bf16[3,512,512]{2,1,0:T(8,128)(2,1)} %param.6, bf16[3,512,512]{2,1,0:T(8,128)(2,1)} %param.5), kind=kLoop, calls=%fused_computation.29 | loop fusion | bytes 6291456 | tf_op jit(solution)/shard_map/squeeze | solution.py:28
  20.7 0.0 copy-start
  20.7 0.8 convolution_convert_fusion.2
  21.5 0.3 copy-done
  21.7 0.3 fusion.34
  22.1 0.8 convolution_convert_fusion.1
  22.8 0.8 convolution_convert_fusion
  23.6 0.3 fusion.32
  24.0 33.0 %collective-permute-done = bf16[256,512]{1,0:T(8,128)(2,1)S(1)} collective-permute-done((bf16[256,512]{1,0:T(8,128)(2,1)S(1)}, bf16[256,512]{1,0:T(8,128)(2,1)S(1)}, u32[]{:S(2)}, u32[]{:S(2)}) %collective-permute-start) | collective-permute-done | bytes 262176 | tf_op jit(solution)/shard_map/ppermute | solution.py:12
  56.9 0.3 fusion
  57.3 4.9 %collective-permute-start.1 = (bf16[256,512]{0,1:T(8,128)(2,1)S(1)}, bf16[256,512]{0,1:T(8,128)(2,1)S(1)}, u32[]{:S(2)}, u32[]{:S(2)}) collective-permute-start(bf16[256,512]{0,1:T(8,128)(2,1)S(1)} %bitcast.27), channel_id=1, source_target_pairs={{0,256},{32,288},{64,320},{96,352},{128,384},{160,416},{192,448},{... | collective-permute-start | bytes 786440 | tf_op jit(solution)/shard_map/ppermute | solution.py:12
  62.2 0.0 collective-permute-done.3
  62.2 0.3 fusion.3
  62.6 0.3 fusion.28
  62.9 4.6 %collective-permute-start.4 = (bf16[256,512]{0,1:T(8,128)(2,1)S(1)}, bf16[256,512]{0,1:T(8,128)(2,1)S(1)}, u32[]{:S(2)}, u32[]{:S(2)}) collective-permute-start(bf16[256,512]{0,1:T(8,128)(2,1)S(1)} %bitcast.28), channel_id=1, source_target_pairs={{0,256},{32,288},{64,320},{96,352},{128,384},{160,416},{192,448},{... | collective-permute-start | bytes 786440 | tf_op jit(solution)/shard_map/ppermute | solution.py:12
  67.5 0.3 fusion.26
  67.8 0.3 fusion.1
  68.2 2.6 %collective-permute-start.2 = (bf16[256,512]{1,0:T(8,128)(2,1)S(1)}, bf16[256,512]{1,0:T(8,128)(2,1)S(1)}, u32[]{:S(2)}, u32[]{:S(2)}) collective-permute-start(bf16[256,512]{1,0:T(8,128)(2,1)S(1)} %fusion.1), channel_id=1, source_target_pairs={{0,1},{1,0},{2,3},{3,2},{4,5},{5,4},{6,7},{7,6},{8,9},{9,8},{10,11... | collective-permute-start | bytes 786440 | tf_op jit(solution)/shard_map/ppermute | solution.py:12
  70.8 3.6 %collective-permute-done.4 = bf16[256,512]{0,1:T(8,128)(2,1)S(1)} collective-permute-done((bf16[256,512]{0,1:T(8,128)(2,1)S(1)}, bf16[256,512]{0,1:T(8,128)(2,1)S(1)}, u32[]{:S(2)}, u32[]{:S(2)}) %collective-permute-start.4) | collective-permute-done | bytes 262176 | tf_op jit(solution)/shard_map/ppermute | solution.py:12
  74.4 0.3 fusion.4
  74.7 0.3 fusion.22
  75.0 4.2 %collective-permute-start.5 = (bf16[256,512]{1,0:T(8,128)(2,1)S(1)}, bf16[256,512]{1,0:T(8,128)(2,1)S(1)}, u32[]{:S(2)}, u32[]{:S(2)}) collective-permute-start(bf16[256,512]{1,0:T(8,128)(2,1)S(1)} %fusion.4), channel_id=1, source_target_pairs={{0,1},{1,0},{2,3},{3,2},{4,5},{5,4},{6,7},{7,6},{8,9},{9,8},{10,11... | collective-permute-start | bytes 786440 | tf_op jit(solution)/shard_map/ppermute | solution.py:12
  79.2 0.3 fusion.20
  79.5 1.3 %collective-permute-done.2 = bf16[256,512]{1,0:T(8,128)(2,1)S(1)} collective-permute-done((bf16[256,512]{1,0:T(8,128)(2,1)S(1)}, bf16[256,512]{1,0:T(8,128)(2,1)S(1)}, u32[]{:S(2)}, u32[]{:S(2)}) %collective-permute-start.2) | collective-permute-done | bytes 262176 | tf_op jit(solution)/shard_map/ppermute | solution.py:12
  80.7 0.3 fusion.2
  81.1 3.4 %collective-permute-done.5 = bf16[256,512]{1,0:T(8,128)(2,1)S(1)} collective-permute-done((bf16[256,512]{1,0:T(8,128)(2,1)S(1)}, bf16[256,512]{1,0:T(8,128)(2,1)S(1)}, u32[]{:S(2)}, u32[]{:S(2)}) %collective-permute-start.5) | collective-permute-done | bytes 262176 | tf_op jit(solution)/shard_map/ppermute | solution.py:12
  84.5 0.3 fusion.5
  84.8 0.8 pad_maximum_fusion
  (1 shorter events, 0.0 us)
Async XLA Ops:
  1.1 55.9 %collective-permute-start = (bf16[256,512]{1,0:T(8,128)(2,1)S(1)}, bf16[256,512]{1,0:T(8,128)(2,1)S(1)}, u32[]{:S(2)}, u32[]{:S(2)}) collective-permute-start(bf16[256,512]{1,0:T(8,128)(2,1)S(1)} %get-tuple-element.11), channel_id=1, source_target_pairs={{0,16},{1,17},{2,18},{3,19},{4,20},{5,21},{6,22},{7,23},{8,24},{9,... | collective-permute-start | bytes 786440 | tf_op jit(solution)/shard_map/ppermute | solution.py:12
  15.9 46.3 %collective-permute-start.3 = (bf16[256,512]{1,0:T(8,128)(2,1)S(1)}, bf16[256,512]{1,0:T(8,128)(2,1)S(1)}, u32[]{:S(2)}, u32[]{:S(2)}) collective-permute-start(bf16[256,512]{1,0:T(8,128)(2,1)S(1)} %get-tuple-element.12), channel_id=1, source_target_pairs={{0,16},{1,17},{2,18},{3,19},{4,20},{5,21},{6,22},{7,23},{8,24},{9,... | collective-permute-start | bytes 786440 | tf_op jit(solution)/shard_map/ppermute | solution.py:12
  20.7 1.0 %copy-start = (bf16[512,512]{1,0:T(8,128)(2,1)S(1)}, bf16[512,512]{1,0:T(8,128)(2,1)}, u32[]{:S(2)}) copy-start(bf16[512,512]{1,0:T(8,128)(2,1)} %param.4) | copy-start | bytes 1572868
  57.3 10.5 %collective-permute-start.1 = (bf16[256,512]{0,1:T(8,128)(2,1)S(1)}, bf16[256,512]{0,1:T(8,128)(2,1)S(1)}, u32[]{:S(2)}, u32[]{:S(2)}) collective-permute-start(bf16[256,512]{0,1:T(8,128)(2,1)S(1)} %bitcast.27), channel_id=1, source_target_pairs={{0,256},{32,288},{64,320},{96,352},{128,384},{160,416},{192,448},{... | collective-permute-start | bytes 786440 | tf_op jit(solution)/shard_map/ppermute | solution.py:12
  62.9 11.5 %collective-permute-start.4 = (bf16[256,512]{0,1:T(8,128)(2,1)S(1)}, bf16[256,512]{0,1:T(8,128)(2,1)S(1)}, u32[]{:S(2)}, u32[]{:S(2)}) collective-permute-start(bf16[256,512]{0,1:T(8,128)(2,1)S(1)} %bitcast.28), channel_id=1, source_target_pairs={{0,256},{32,288},{64,320},{96,352},{128,384},{160,416},{192,448},{... | collective-permute-start | bytes 786440 | tf_op jit(solution)/shard_map/ppermute | solution.py:12
  68.2 12.6 %collective-permute-start.2 = (bf16[256,512]{1,0:T(8,128)(2,1)S(1)}, bf16[256,512]{1,0:T(8,128)(2,1)S(1)}, u32[]{:S(2)}, u32[]{:S(2)}) collective-permute-start(bf16[256,512]{1,0:T(8,128)(2,1)S(1)} %fusion.1), channel_id=1, source_target_pairs={{0,1},{1,0},{2,3},{3,2},{4,5},{5,4},{6,7},{7,6},{8,9},{9,8},{10,11... | collective-permute-start | bytes 786440 | tf_op jit(solution)/shard_map/ppermute | solution.py:12
  75.0 9.5 %collective-permute-start.5 = (bf16[256,512]{1,0:T(8,128)(2,1)S(1)}, bf16[256,512]{1,0:T(8,128)(2,1)S(1)}, u32[]{:S(2)}, u32[]{:S(2)}) collective-permute-start(bf16[256,512]{1,0:T(8,128)(2,1)S(1)} %fusion.4), channel_id=1, source_target_pairs={{0,1},{1,0},{2,3},{3,2},{4,5},{5,4},{6,7},{7,6},{8,9},{9,8},{10,11... | collective-permute-start | bytes 786440 | tf_op jit(solution)/shard_map/ppermute | solution.py:12

commit v2 on v1

--- a/solution.py
+++ b/solution.py
@@ -9,6 +9,12 @@
 def from_partner(value, axis, distance):
     mask = 2**distance
     pairs = [(source, source ^ mask) for source in range(lax.axis_size(axis))]
+    return lax.ppermute(value, axis, pairs)
+
+
+def shifted(value, axis, step):
+    size = lax.axis_size(axis)
+    pairs = [(source, (source + step) % size) for source in range(size)]
     return lax.ppermute(value, axis, pairs)
 
 
@@ -34,7 +40,11 @@
         panel = probes[chunk * rows:(chunk + 1) * rows]
         for level, (axis, bit) in enumerate(plan):
             own, cross = weights[level]
-            other = from_partner(panel, axis, bit)
+            if level == 0:
+                step = (2**bit // 2) * (1 if chunk % 2 == 0 else -1)
+                other = shifted(shifted(panel, axis, step), axis, step)
+            else:
+                other = from_partner(panel, axis, bit)
             total = jnp.dot(panel, own, preferred_element_type=jnp.float32)
             total = total + jnp.dot(other, cross, preferred_element_type=jnp.float32)
             panel = total.astype(jnp.bfloat16)

time: 86 us -> 95.9 us (1.12)
  the two profiles are of different devices: /device:TPU:48 before, /device:TPU:120 now
where the time goes in v2:
time: 95.9 us; the launch traced here: 95.5 us
  waiting for transfers between devices  46.7 us (49%)
  starting transfers between devices  37.5 us (39%)
  matrix products  6.11 us (6%)
  local copies, waits for them, and re-layouts  4.19 us (4%)
    ppermute x4, waiting for transfers between devices, shifted(): return lax.ppermute(value, axis, pairs)  36.5 us
    ppermute x4, starting transfers between devices, shifted(): return lax.ppermute(value, axis, pairs)  21.7 us
    ppermute x4, starting transfers between devices, from_partner(): return lax.ppermute(value, axis, pairs)  15.8 us
    ppermute x4, waiting for transfers between devices, from_partner(): return lax.ppermute(value, axis, pairs)  10.2 us
    dot_general x3, matrix products, permuted_columns(): jnp.dot(weights, onehot, preferred_element_type=jnp.float32)  2.28 us
    squeeze x1, local copies, waits for them, and re-layouts, per_device(): both = jnp.concatenate([own_blocks[level], cross_blocks[level]], axis=0)  2.03 us
    dot_general x6, matrix products, per_device(): total = total + jnp.dot(other, cross, preferred_element_type=jnp.float32)  1.93 us
  transfers between devices with their start and end apart: 8, of which 6 were waited for; matrix products, arithmetic and copies ran while one was open for 9% of the time, Pallas kernels for 0%

profile of v2, /device:TPU:120, one launch (start us, length us, event | category | flops | bytes accessed | tf_op | source)
XLA Modules:
  0.0 95.5 jit_solution(11169363916489904260)
XLA Ops:
  0.0 1.1 %fusion.41 = (bf16[256,512]{1,0:T(8,128)(2,1)S(1)}, bf16[256,512]{1,0:T(8,128)(2,1)S(1)}) fusion(bf16[512,512]{1,0:T(8,128)(2,1)} %param.4), kind=kLoop, calls=%fused_computation.60 | loop fusion | bytes 1048576 | tf_op jit(solution)/shard_map/slice | solution.py:40
  1.1 9.1 %collective-permute-start = (bf16[256,512]{1,0:T(8,128)(2,1)S(1)}, bf16[256,512]{1,0:T(8,128)(2,1)S(1)}, u32[]{:S(2)}, u32[]{:S(2)}) collective-permute-start(bf16[256,512]{1,0:T(8,128)(2,1)S(1)} %get-tuple-element.11), channel_id=1, source_target_pairs={{0,8},{1,9},{2,10},{3,11},{4,12},{5,13},{6,14},{7,15},{8,16},{9,17... | collective-permute-start | bytes 786440 | tf_op jit(solution)/shard_map/ppermute | solution.py:18
  10.2 2.9 %collective-permute-start.4 = (bf16[256,512]{1,0:T(8,128)(2,1)S(1)}, bf16[256,512]{1,0:T(8,128)(2,1)S(1)}, u32[]{:S(2)}, u32[]{:S(2)}) collective-permute-start(bf16[256,512]{1,0:T(8,128)(2,1)S(1)} %get-tuple-element.12), channel_id=1, source_target_pairs={{0,24},{1,25},{2,26},{3,27},{4,28},{5,29},{6,30},{7,31},{8,0},{9,1... | collective-permute-start | bytes 786440 | tf_op jit(solution)/shard_map/ppermute | solution.py:18
  13.0 0.8 fusion.42
  13.9 2.0 %slice_bitcast_fusion = (bf16[512,512]{1,0:T(8,128)(2,1)S(1)}, bf16[512,512]{1,0:T(8,128)(2,1)S(1)}, bf16[512,512]{1,0:T(8,128)(2,1)S(1)}, bf16[512,512]{1,0:T(8...) fusion(bf16[3,512,512]{2,1,0:T(8,128)(2,1)} %param.6, bf16[3,512,512]{2,1,0:T(8,128)(2,1)} %param.5), kind=kLoop, calls=%fused_computation.29 | loop fusion | bytes 6291456 | tf_op jit(solution)/shard_map/squeeze | solution.py:34
  15.9 0.8 convolution_convert_fusion.2
  16.7 0.8 convolution_convert_fusion.1
  17.7 0.3 fusion.34
  18.1 16.4 %collective-permute-done = bf16[256,512]{1,0:T(8,128)(2,1)S(1)} collective-permute-done((bf16[256,512]{1,0:T(8,128)(2,1)S(1)}, bf16[256,512]{1,0:T(8,128)(2,1)S(1)}, u32[]{:S(2)}, u32[]{:S(2)}) %collective-permute-start) | collective-permute-done | bytes 262176 | tf_op jit(solution)/shard_map/ppermute | solution.py:18
  34.4 5.2 %collective-permute-start.1 = (bf16[256,512]{1,0:T(8,128)(2,1)S(1)}, bf16[256,512]{1,0:T(8,128)(2,1)S(1)}, u32[]{:S(2)}, u32[]{:S(2)}) collective-permute-start(bf16[256,512]{1,0:T(8,128)(2,1)S(1)} %collective-permute-done), channel_id=1, source_target_pairs={{0,8},{1,9},{2,10},{3,11},{4,12},{5,13},{6,14},{7,15},{8,16},{9,17... | collective-permute-start | bytes 786440 | tf_op jit(solution)/shard_map/ppermute | solution.py:18
  39.6 0.8 convolution_convert_fusion
  40.4 0.3 fusion.32
  40.8 4.5 %collective-permute-start.5 = (bf16[256,512]{1,0:T(8,128)(2,1)S(1)}, bf16[256,512]{1,0:T(8,128)(2,1)S(1)}, u32[]{:S(2)}, u32[]{:S(2)}) collective-permute-start(bf16[256,512]{1,0:T(8,128)(2,1)S(1)} %collective-permute-done.4), channel_id=1, source_target_pairs={{0,24},{1,25},{2,26},{3,27},{4,28},{5,29},{6,30},{7,31},{8,0},{9,1... | collective-permute-start | bytes 786440 | tf_op jit(solution)/shard_map/ppermute | solution.py:18
  45.3 15.0 %collective-permute-done.1 = bf16[256,512]{1,0:T(8,128)(2,1)S(1)} collective-permute-done((bf16[256,512]{1,0:T(8,128)(2,1)S(1)}, bf16[256,512]{1,0:T(8,128)(2,1)S(1)}, u32[]{:S(2)}, u32[]{:S(2)}) %collective-permute-start.1) | collective-permute-done | bytes 262176 | tf_op jit(solution)/shard_map/ppermute | solution.py:18
  60.3 0.3 fusion
  60.6 4.9 %collective-permute-start.2 = (bf16[256,512]{0,1:T(8,128)(2,1)S(1)}, bf16[256,512]{0,1:T(8,128)(2,1)S(1)}, u32[]{:S(2)}, u32[]{:S(2)}) collective-permute-start(bf16[256,512]{0,1:T(8,128)(2,1)S(1)} %bitcast.27), channel_id=1, source_target_pairs={{0,256},{32,288},{64,320},{96,352},{128,384},{160,416},{192,448},{... | collective-permute-start | bytes 786440 | tf_op jit(solution)/shard_map/ppermute | solution.py:12
  65.6 5.1 %collective-permute-done.5 = bf16[256,512]{1,0:T(8,128)(2,1)S(1)} collective-permute-done((bf16[256,512]{1,0:T(8,128)(2,1)S(1)}, bf16[256,512]{1,0:T(8,128)(2,1)S(1)}, u32[]{:S(2)}, u32[]{:S(2)}) %collective-permute-start.5) | collective-permute-done | bytes 262176 | tf_op jit(solution)/shard_map/ppermute | solution.py:18
  70.7 0.3 fusion.3
  71.1 0.3 fusion.28
  71.4 4.9 %collective-permute-start.6 = (bf16[256,512]{0,1:T(8,128)(2,1)S(1)}, bf16[256,512]{0,1:T(8,128)(2,1)S(1)}, u32[]{:S(2)}, u32[]{:S(2)}) collective-permute-start(bf16[256,512]{0,1:T(8,128)(2,1)S(1)} %bitcast.28), channel_id=1, source_target_pairs={{0,256},{32,288},{64,320},{96,352},{128,384},{160,416},{192,448},{... | collective-permute-start | bytes 786440 | tf_op jit(solution)/shard_map/ppermute | solution.py:12
  76.3 0.3 fusion.26
  76.7 0.3 fusion.1
  77.0 2.5 %collective-permute-start.3 = (bf16[256,512]{1,0:T(8,128)(2,1)S(1)}, bf16[256,512]{1,0:T(8,128)(2,1)S(1)}, u32[]{:S(2)}, u32[]{:S(2)}) collective-permute-start(bf16[256,512]{1,0:T(8,128)(2,1)S(1)} %fusion.1), channel_id=1, source_target_pairs={{0,1},{1,0},{2,3},{3,2},{4,5},{5,4},{6,7},{7,6},{8,9},{9,8},{10,11... | collective-permute-start | bytes 786440 | tf_op jit(solution)/shard_map/ppermute | solution.py:12
  79.5 4.5 %collective-permute-done.6 = bf16[256,512]{0,1:T(8,128)(2,1)S(1)} collective-permute-done((bf16[256,512]{0,1:T(8,128)(2,1)S(1)}, bf16[256,512]{0,1:T(8,128)(2,1)S(1)}, u32[]{:S(2)}, u32[]{:S(2)}) %collective-permute-start.6) | collective-permute-done | bytes 262176 | tf_op jit(solution)/shard_map/ppermute | solution.py:12
  84.0 0.3 fusion.4
  84.3 0.3 fusion.22
  84.6 3.4 %collective-permute-start.7 = (bf16[256,512]{1,0:T(8,128)(2,1)S(1)}, bf16[256,512]{1,0:T(8,128)(2,1)S(1)}, u32[]{:S(2)}, u32[]{:S(2)}) collective-permute-start(bf16[256,512]{1,0:T(8,128)(2,1)S(1)} %fusion.4), channel_id=1, source_target_pairs={{0,1},{1,0},{2,3},{3,2},{4,5},{5,4},{6,7},{7,6},{8,9},{9,8},{10,11... | collective-permute-start | bytes 786440 | tf_op jit(solution)/shard_map/ppermute | solution.py:12
  88.3 1.4 %collective-permute-done.3 = bf16[256,512]{1,0:T(8,128)(2,1)S(1)} collective-permute-done((bf16[256,512]{1,0:T(8,128)(2,1)S(1)}, bf16[256,512]{1,0:T(8,128)(2,1)S(1)}, u32[]{:S(2)}, u32[]{:S(2)}) %collective-permute-start.3) | collective-permute-done | bytes 262176 | tf_op jit(solution)/shard_map/ppermute | solution.py:12
  89.7 0.3 fusion.2
  90.0 4.4 %collective-permute-done.7 = bf16[256,512]{1,0:T(8,128)(2,1)S(1)} collective-permute-done((bf16[256,512]{1,0:T(8,128)(2,1)S(1)}, bf16[256,512]{1,0:T(8,128)(2,1)S(1)}, u32[]{:S(2)}, u32[]{:S(2)}) %collective-permute-start.7) | collective-permute-done | bytes 262176 | tf_op jit(solution)/shard_map/ppermute | solution.py:12
  94.3 0.3 fusion.5
  94.6 0.8 pad_maximum_fusion
  (5 shorter events, 0.6 us)
Async XLA Ops:
  1.1 33.4 %collective-permute-start = (bf16[256,512]{1,0:T(8,128)(2,1)S(1)}, bf16[256,512]{1,0:T(8,128)(2,1)S(1)}, u32[]{:S(2)}, u32[]{:S(2)}) collective-permute-start(bf16[256,512]{1,0:T(8,128)(2,1)S(1)} %get-tuple-element.11), channel_id=1, source_target_pairs={{0,8},{1,9},{2,10},{3,11},{4,12},{5,13},{6,14},{7,15},{8,16},{9,17... | collective-permute-start | bytes 786440 | tf_op jit(solution)/shard_map/ppermute | solution.py:18
  10.2 30.6 %collective-permute-start.4 = (bf16[256,512]{1,0:T(8,128)(2,1)S(1)}, bf16[256,512]{1,0:T(8,128)(2,1)S(1)}, u32[]{:S(2)}, u32[]{:S(2)}) collective-permute-start(bf16[256,512]{1,0:T(8,128)(2,1)S(1)} %get-tuple-element.12), channel_id=1, source_target_pairs={{0,24},{1,25},{2,26},{3,27},{4,28},{5,29},{6,30},{7,31},{8,0},{9,1... | collective-permute-start | bytes 786440 | tf_op jit(solution)/shard_map/ppermute | solution.py:18
  16.7 1.0 %copy-start = (bf16[512,512]{1,0:T(8,128)(2,1)S(1)}, bf16[512,512]{1,0:T(8,128)(2,1)}, u32[]{:S(2)}) copy-start(bf16[512,512]{1,0:T(8,128)(2,1)} %param.4) | copy-start | bytes 1572868
  34.4 25.8 %collective-permute-start.1 = (bf16[256,512]{1,0:T(8,128)(2,1)S(1)}, bf16[256,512]{1,0:T(8,128)(2,1)S(1)}, u32[]{:S(2)}, u32[]{:S(2)}) collective-permute-start(bf16[256,512]{1,0:T(8,128)(2,1)S(1)} %collective-permute-done), channel_id=1, source_target_pairs={{0,8},{1,9},{2,10},{3,11},{4,12},{5,13},{6,14},{7,15},{8,16},{9,17... | collective-permute-start | bytes 786440 | tf_op jit(solution)/shard_map/ppermute | solution.py:18
  40.8 30.0 %collective-permute-start.5 = (bf16[256,512]{1,0:T(8,128)(2,1)S(1)}, bf16[256,512]{1,0:T(8,128)(2,1)S(1)}, u32[]{:S(2)}, u32[]{:S(2)}) collective-permute-start(bf16[256,512]{1,0:T(8,128)(2,1)S(1)} %collective-permute-done.4), channel_id=1, source_target_pairs={{0,24},{1,25},{2,26},{3,27},{4,28},{5,29},{6,30},{7,31},{8,0},{9,1... | collective-permute-start | bytes 786440 | tf_op jit(solution)/shard_map/ppermute | solution.py:18
  60.6 16.0 %collective-permute-start.2 = (bf16[256,512]{0,1:T(8,128)(2,1)S(1)}, bf16[256,512]{0,1:T(8,128)(2,1)S(1)}, u32[]{:S(2)}, u32[]{:S(2)}) collective-permute-start(bf16[256,512]{0,1:T(8,128)(2,1)S(1)} %bitcast.27), channel_id=1, source_target_pairs={{0,256},{32,288},{64,320},{96,352},{128,384},{160,416},{192,448},{... | collective-permute-start | bytes 786440 | tf_op jit(solution)/shard_map/ppermute | solution.py:12
  71.4 12.6 %collective-permute-start.6 = (bf16[256,512]{0,1:T(8,128)(2,1)S(1)}, bf16[256,512]{0,1:T(8,128)(2,1)S(1)}, u32[]{:S(2)}, u32[]{:S(2)}) collective-permute-start(bf16[256,512]{0,1:T(8,128)(2,1)S(1)} %bitcast.28), channel_id=1, source_target_pairs={{0,256},{32,288},{64,320},{96,352},{128,384},{160,416},{192,448},{... | collective-permute-start | bytes 786440 | tf_op jit(solution)/shard_map/ppermute | solution.py:12
  77.0 12.7 %collective-permute-start.3 = (bf16[256,512]{1,0:T(8,128)(2,1)S(1)}, bf16[256,512]{1,0:T(8,128)(2,1)S(1)}, u32[]{:S(2)}, u32[]{:S(2)}) collective-permute-start(bf16[256,512]{1,0:T(8,128)(2,1)S(1)} %fusion.1), channel_id=1, source_target_pairs={{0,1},{1,0},{2,3},{3,2},{4,5},{5,4},{6,7},{7,6},{8,9},{9,8},{10,11... | collective-permute-start | bytes 786440 | tf_op jit(solution)/shard_map/ppermute | solution.py:12
  84.6 9.7 %collective-permute-start.7 = (bf16[256,512]{1,0:T(8,128)(2,1)S(1)}, bf16[256,512]{1,0:T(8,128)(2,1)S(1)}, u32[]{:S(2)}, u32[]{:S(2)}) collective-permute-start(bf16[256,512]{1,0:T(8,128)(2,1)S(1)} %fusion.4), channel_id=1, source_target_pairs={{0,1},{1,0},{2,3},{3,2},{4,5},{5,4},{6,7},{7,6},{8,9},{9,8},{10,11... | collective-permute-start | bytes 786440 | tf_op jit(solution)/shard_map/ppermute | solution.py:12

commit v3 on v1

--- a/solution.py
+++ b/solution.py
@@ -29,17 +29,28 @@
         both = permuted_columns(both, level_perm[level])
         weights.append((both[:br], both[br:]))
     rows = probes.shape[0] // CHUNKS
-    outs = []
+    arrived = from_partner(probes, *plan[0])
+    panels, others = [], []
     for chunk in range(CHUNKS):
-        panel = probes[chunk * rows:(chunk + 1) * rows]
+        part = slice(chunk * rows, (chunk + 1) * rows)
+        panel = probes[part]
         for level, (axis, bit) in enumerate(plan):
             own, cross = weights[level]
-            other = from_partner(panel, axis, bit)
+            if level == 0:
+                other = arrived[part]
+            else:
+                other = from_partner(panel, axis, bit)
+            if level == 2:
+                break
             total = jnp.dot(panel, own, preferred_element_type=jnp.float32)
             total = total + jnp.dot(other, cross, preferred_element_type=jnp.float32)
             panel = total.astype(jnp.bfloat16)
-        outs.append(panel)
-    return jnp.concatenate(outs, axis=0)
+        panels.append(panel)
+        others.append(other)
+    own, cross = weights[2]
+    total = jnp.dot(jnp.concatenate(panels), own, preferred_element_type=jnp.float32)
+    total = total + jnp.dot(jnp.concatenate(others), cross, preferred_element_type=jnp.float32)
+    return total.astype(jnp.bfloat16)
 
 
 def solution(mesh):

time: 86 us -> 90.5 us (1.052)
  the two profiles are of different devices: /device:TPU:48 before, /device:TPU:32 now
where the time goes in v3:
time: 90.5 us; the launch traced here: 90.2 us
  waiting for transfers between devices  51 us (56%)
  starting transfers between devices  29.3 us (32%)
  matrix products  6.58 us (7%)
  local copies, waits for them, and re-layouts  3.12 us (3%)
    ppermute x5, waiting for transfers between devices, from_partner(): return lax.ppermute(value, axis, pairs)  51 us
    ppermute x5, starting transfers between devices, from_partner(): return lax.ppermute(value, axis, pairs)  29.3 us
    dot_general x3, matrix products, permuted_columns(): jnp.dot(weights, onehot, preferred_element_type=jnp.float32)  2.27 us
    squeeze x1, local copies, waits for them, and re-layouts, per_device(): both = jnp.concatenate([own_blocks[level], cross_blocks[level]], axis=0)  2.03 us
  transfers between devices with their start and end apart: 5, of which 5 were waited for; matrix products, arithmetic and copies ran while one was open for 9% of the time, Pallas kernels for 0%

profile of v3, /device:TPU:32, one launch (start us, length us, event | category | flops | bytes accessed | tf_op | source)
XLA Modules:
  0.0 90.2 jit_solution(12137641932542016784)
XLA Ops:
  0.0 14.8 %collective-permute-start = (bf16[512,512]{1,0:T(8,128)(2,1)}, bf16[512,512]{1,0:T(8,128)(2,1)S(1)}, u32[]{:S(2)}, u32[]{:S(2)}) collective-permute-start(bf16[512,512]{1,0:T(8,128)(2,1)} %param.4), channel_id=1, source_target_pairs={{0,16},{1,17},{2,18},{3,19},{4,20},{5,21},{6,22},{7,23},{8,24},{9,... | collective-permute-start | bytes 1572872 | tf_op jit(solution)/shard_map/ppermute | solution.py:12
  14.8 0.8 fusion.47
  15.6 2.0 %slice_bitcast_fusion.2 = (bf16[512,512]{1,0:T(8,128)(2,1)S(1)}, bf16[512,512]{1,0:T(8,128)(2,1)S(1)}, bf16[512,512]{1,0:T(8,128)(2,1)S(1)}, bf16[512,512]{1,0:T...) fusion(bf16[3,512,512]{2,1,0:T(8,128)(2,1)} %param.6, bf16[3,512,512]{2,1,0:T(8,128)(2,1)} %param.5), kind=kLoop, calls=%fused_computation.38 | loop fusion | bytes 6291456 | tf_op jit(solution)/shard_map/squeeze | solution.py:28
  17.7 0.8 convolution_convert_fusion.1
  18.4 0.8 convolution_convert_fusion.2
  19.2 0.0 copy-start
  19.2 0.8 convolution_convert_fusion
  20.0 0.3 copy-done
  20.2 0.3 fusion.34
  20.6 0.3 fusion.36
  20.9 40.1 %collective-permute-done = bf16[512,512]{1,0:T(8,128)(2,1)S(1)} collective-permute-done((bf16[512,512]{1,0:T(8,128)(2,1)}, bf16[512,512]{1,0:T(8,128)(2,1)S(1)}, u32[]{:S(2)}, u32[]{:S(2)}) %collective-permute-start) | collective-permute-done | bytes 524320 | tf_op jit(solution)/shard_map/ppermute | solution.py:12
  61.0 0.3 fusion.3
  61.4 4.9 %collective-permute-start.2 = (bf16[256,512]{0,1:T(8,128)(2,1)S(1)}, bf16[256,512]{0,1:T(8,128)(2,1)S(1)}, u32[]{:S(2)}, u32[]{:S(2)}) collective-permute-start(bf16[256,512]{0,1:T(8,128)(2,1)S(1)} %bitcast.22), channel_id=1, source_target_pairs={{0,256},{32,288},{64,320},{96,352},{128,384},{160,416},{192,448},{... | collective-permute-start | bytes 786440 | tf_op jit(solution)/shard_map/ppermute | solution.py:12
  66.3 0.3 fusion.1
  66.7 0.3 fusion.28
  67.0 2.4 %collective-permute-start.1 = (bf16[256,512]{0,1:T(8,128)(2,1)S(1)}, bf16[256,512]{0,1:T(8,128)(2,1)S(1)}, u32[]{:S(2)}, u32[]{:S(2)}) collective-permute-start(bf16[256,512]{0,1:T(8,128)(2,1)S(1)} %bitcast.21), channel_id=1, source_target_pairs={{0,256},{32,288},{64,320},{96,352},{128,384},{160,416},{192,448},{... | collective-permute-start | bytes 786440 | tf_op jit(solution)/shard_map/ppermute | solution.py:12
  69.4 0.3 fusion.30
  69.7 3.3 %collective-permute-done.2 = bf16[256,512]{0,1:T(8,128)(2,1)S(1)} collective-permute-done((bf16[256,512]{0,1:T(8,128)(2,1)S(1)}, bf16[256,512]{0,1:T(8,128)(2,1)S(1)}, u32[]{:S(2)}, u32[]{:S(2)}) %collective-permute-start.2) | collective-permute-done | bytes 262176 | tf_op jit(solution)/shard_map/ppermute | solution.py:12
  73.0 0.3 fusion.4
  73.3 3.5 %collective-permute-start.4 = (bf16[256,512]{1,0:T(8,128)(2,1)S(1)}, bf16[256,512]{1,0:T(8,128)(2,1)S(1)}, u32[]{:S(2)}, u32[]{:S(2)}) collective-permute-start(bf16[256,512]{1,0:T(8,128)(2,1)S(1)} %fusion.4), channel_id=1, source_target_pairs={{0,1},{1,0},{2,3},{3,2},{4,5},{5,4},{6,7},{7,6},{8,9},{9,8},{10,11... | collective-permute-start | bytes 786440 | tf_op jit(solution)/shard_map/ppermute | solution.py:12
  76.9 1.7 %collective-permute-done.1 = bf16[256,512]{0,1:T(8,128)(2,1)S(1)} collective-permute-done((bf16[256,512]{0,1:T(8,128)(2,1)S(1)}, bf16[256,512]{0,1:T(8,128)(2,1)S(1)}, u32[]{:S(2)}, u32[]{:S(2)}) %collective-permute-start.1) | collective-permute-done | bytes 262176 | tf_op jit(solution)/shard_map/ppermute | solution.py:12
  78.6 0.3 fusion.2
  78.9 3.5 %collective-permute-start.3 = (bf16[256,512]{1,0:T(8,128)(2,1)S(1)}, bf16[256,512]{1,0:T(8,128)(2,1)S(1)}, u32[]{:S(2)}, u32[]{:S(2)}) collective-permute-start(bf16[256,512]{1,0:T(8,128)(2,1)S(1)} %fusion.2), channel_id=1, source_target_pairs={{0,1},{1,0},{2,3},{3,2},{4,5},{5,4},{6,7},{7,6},{8,9},{9,8},{10,11... | collective-permute-start | bytes 786440 | tf_op jit(solution)/shard_map/ppermute | solution.py:12
  82.5 0.4 fusion.15
  82.9 2.3 %collective-permute-done.4 = bf16[256,512]{1,0:T(8,128)(2,1)S(1)} collective-permute-done((bf16[256,512]{1,0:T(8,128)(2,1)S(1)}, bf16[256,512]{1,0:T(8,128)(2,1)S(1)}, u32[]{:S(2)}, u32[]{:S(2)}) %collective-permute-start.4) | collective-permute-done | bytes 262176 | tf_op jit(solution)/shard_map/ppermute | solution.py:12
  85.2 3.7 %collective-permute-done.3 = bf16[256,512]{1,0:T(8,128)(2,1)S(1)} collective-permute-done((bf16[256,512]{1,0:T(8,128)(2,1)S(1)}, bf16[256,512]{1,0:T(8,128)(2,1)S(1)}, u32[]{:S(2)}, u32[]{:S(2)}) %collective-permute-start.3) | collective-permute-done | bytes 262176 | tf_op jit(solution)/shard_map/ppermute | solution.py:12
  88.9 1.2 %fusion = bf16[512,512]{1,0:T(8,128)(2,1)} fusion(f32[512,512]{1,0:T(8,128)S(1)} %fusion.15, bf16[1024,512]{1,0:T(8,128)(2,1)S(1)} %convolution_convert_fusion, bf16[256,512]{1,0:T(8,128)(2,1)S(1)} %collective-permute-done.4, bf16[256,512]{1,0:T(8,128)(2,1)S(1)} %collective-permute-done.3), kind=kOutput, calls=%fused_computation.4 | convolution fusion | flops 270008320 | bytes 2621440 | tf_op jit(solution)/shard_map/dot_general | solution.py:52
Async XLA Ops:
  0.0 61.0 %collective-permute-start = (bf16[512,512]{1,0:T(8,128)(2,1)}, bf16[512,512]{1,0:T(8,128)(2,1)S(1)}, u32[]{:S(2)}, u32[]{:S(2)}) collective-permute-start(bf16[512,512]{1,0:T(8,128)(2,1)} %param.4), channel_id=1, source_target_pairs={{0,16},{1,17},{2,18},{3,19},{4,20},{5,21},{6,22},{7,23},{8,24},{9,... | collective-permute-start | bytes 1572872 | tf_op jit(solution)/shard_map/ppermute | solution.py:12
  19.2 1.0 %copy-start = (bf16[512,512]{1,0:T(8,128)(2,1)S(1)}, bf16[512,512]{1,0:T(8,128)(2,1)}, u32[]{:S(2)}) copy-start(bf16[512,512]{1,0:T(8,128)(2,1)} %param.4) | copy-start | bytes 1572868
  61.4 11.6 %collective-permute-start.2 = (bf16[256,512]{0,1:T(8,128)(2,1)S(1)}, bf16[256,512]{0,1:T(8,128)(2,1)S(1)}, u32[]{:S(2)}, u32[]{:S(2)}) collective-permute-start(bf16[256,512]{0,1:T(8,128)(2,1)S(1)} %bitcast.22), channel_id=1, source_target_pairs={{0,256},{32,288},{64,320},{96,352},{128,384},{160,416},{192,448},{... | collective-permute-start | bytes 786440 | tf_op jit(solution)/shard_map/ppermute | solution.py:12
  67.0 11.6 %collective-permute-start.1 = (bf16[256,512]{0,1:T(8,128)(2,1)S(1)}, bf16[256,512]{0,1:T(8,128)(2,1)S(1)}, u32[]{:S(2)}, u32[]{:S(2)}) collective-permute-start(bf16[256,512]{0,1:T(8,128)(2,1)S(1)} %bitcast.21), channel_id=1, source_target_pairs={{0,256},{32,288},{64,320},{96,352},{128,384},{160,416},{192,448},{... | collective-permute-start | bytes 786440 | tf_op jit(solution)/shard_map/ppermute | solution.py:12
  73.3 11.9 %collective-permute-start.4 = (bf16[256,512]{1,0:T(8,128)(2,1)S(1)}, bf16[256,512]{1,0:T(8,128)(2,1)S(1)}, u32[]{:S(2)}, u32[]{:S(2)}) collective-permute-start(bf16[256,512]{1,0:T(8,128)(2,1)S(1)} %fusion.4), channel_id=1, source_target_pairs={{0,1},{1,0},{2,3},{3,2},{4,5},{5,4},{6,7},{7,6},{8,9},{9,8},{10,11... | collective-permute-start | bytes 786440 | tf_op jit(solution)/shard_map/ppermute | solution.py:12
  78.9 10.0 %collective-permute-start.3 = (bf16[256,512]{1,0:T(8,128)(2,1)S(1)}, bf16[256,512]{1,0:T(8,128)(2,1)S(1)}, u32[]{:S(2)}, u32[]{:S(2)}) collective-permute-start(bf16[256,512]{1,0:T(8,128)(2,1)S(1)} %fusion.2), channel_id=1, source_target_pairs={{0,1},{1,0},{2,3},{3,2},{4,5},{5,4},{6,7},{7,6},{8,9},{9,8},{10,11... | collective-permute-start | bytes 786440 | tf_op jit(solution)/shard_map/ppermute | solution.py:12

commit v4 on v1

--- a/solution.py
+++ b/solution.py
@@ -29,15 +29,25 @@
         both = permuted_columns(both, level_perm[level])
         weights.append((both[:br], both[br:]))
     rows = probes.shape[0] // CHUNKS
+    panels = [probes[chunk * rows:(chunk + 1) * rows] for chunk in range(CHUNKS)]
+    arrived = [from_partner(panels[0], *plan[0])]
     outs = []
     for chunk in range(CHUNKS):
-        panel = probes[chunk * rows:(chunk + 1) * rows]
+        panel = panels[chunk]
         for level, (axis, bit) in enumerate(plan):
             own, cross = weights[level]
-            other = from_partner(panel, axis, bit)
+            if level == 0:
+                other = arrived[chunk]
+            else:
+                other = from_partner(panel, axis, bit)
+            if level == 2 and chunk + 1 < CHUNKS:
+                other, arrived[chunk + 1] = lax.optimization_barrier((other, arrived[chunk + 1]))
             total = jnp.dot(panel, own, preferred_element_type=jnp.float32)
             total = total + jnp.dot(other, cross, preferred_element_type=jnp.float32)
             panel = total.astype(jnp.bfloat16)
+            if level == 0 and chunk + 1 < CHUNKS:
+                panel, after = lax.optimization_barrier((panel, panels[chunk + 1]))
+                arrived.append(from_partner(after, *plan[0]))
         outs.append(panel)
     return jnp.concatenate(outs, axis=0)
 

time: 86 us -> 94.3 us (1.097)
  the two profiles are of different devices: /device:TPU:48 before, /device:TPU:46 now
where the time goes in v4:
time: 94.3 us; the launch traced here: 94 us
  waiting for transfers between devices  44.5 us (47%)
  starting transfers between devices  38.1 us (40%)
  matrix products  6.1 us (6%)
  local copies, waits for them, and re-layouts  4.19 us (4%)
    ppermute x6, waiting for transfers between devices, from_partner(): return lax.ppermute(value, axis, pairs)  44.5 us
    ppermute x6, starting transfers between devices, from_partner(): return lax.ppermute(value, axis, pairs)  38.1 us
    dot_general x3, matrix products, permuted_columns(): jnp.dot(weights, onehot, preferred_element_type=jnp.float32)  2.27 us
    squeeze x1, local copies, waits for them, and re-layouts, per_device(): both = jnp.concatenate([own_blocks[level], cross_blocks[level]], axis=0)  2.03 us
    dot_general x6, matrix products, per_device(): total = total + jnp.dot(other, cross, preferred_element_type=jnp.float32)  1.92 us
    dot_general x6, matrix products, per_device(): total = jnp.dot(panel, own, preferred_element_type=jnp.float32)  1.9 us
  transfers between devices with their start and end apart: 6, of which 4 were waited for; matrix products, arithmetic and copies ran while one was open for 8% of the time, Pallas kernels for 0%

profile of v4, /device:TPU:46, one launch (start us, length us, event | category | flops | bytes accessed | tf_op | source)
XLA Modules:
  0.0 94.0 jit_solution(4002173914444558036)
XLA Ops:
  0.0 1.1 %fusion.41 = (bf16[256,512]{1,0:T(8,128)(2,1)S(1)}, bf16[256,512]{1,0:T(8,128)(2,1)S(1)}) fusion(bf16[512,512]{1,0:T(8,128)(2,1)} %param.4), kind=kLoop, calls=%fused_computation.61 | loop fusion | bytes 1048576 | tf_op jit(solution)/shard_map/slice | solution.py:32
  1.1 14.8 %collective-permute-start = (bf16[256,512]{1,0:T(8,128)(2,1)S(1)}, bf16[256,512]{1,0:T(8,128)(2,1)S(1)}, u32[]{:S(2)}, u32[]{:S(2)}) collective-permute-start(bf16[256,512]{1,0:T(8,128)(2,1)S(1)} %get-tuple-element.20), channel_id=1, source_target_pairs={{0,16},{1,17},{2,18},{3,19},{4,20},{5,21},{6,22},{7,23},{8,24},{9,... | collective-permute-start | bytes 786440 | tf_op jit(solution)/shard_map/ppermute | solution.py:12
  15.9 0.8 fusion.42
  16.7 2.0 %slice_bitcast_fusion = (bf16[512,512]{1,0:T(8,128)(2,1)S(1)}, bf16[512,512]{1,0:T(8,128)(2,1)S(1)}, bf16[512,512]{1,0:T(8,128)(2,1)S(1)}, bf16[512,512]{1,0:T(8...) fusion(bf16[3,512,512]{2,1,0:T(8,128)(2,1)} %param.6, bf16[3,512,512]{2,1,0:T(8,128)(2,1)} %param.5), kind=kLoop, calls=%fused_computation.31 | loop fusion | bytes 6291456 | tf_op jit(solution)/shard_map/squeeze | solution.py:28
  18.8 0.0 copy-start
  18.8 0.8 convolution_convert_fusion.2
  19.5 0.3 copy-done
  19.8 0.3 fusion.34
  20.1 19.1 %collective-permute-done = bf16[256,512]{1,0:T(8,128)(2,1)S(1)} collective-permute-done((bf16[256,512]{1,0:T(8,128)(2,1)S(1)}, bf16[256,512]{1,0:T(8,128)(2,1)S(1)}, u32[]{:S(2)}, u32[]{:S(2)}) %collective-permute-start) | collective-permute-done | bytes 262176 | tf_op jit(solution)/shard_map/ppermute | solution.py:12
  39.3 0.3 fusion.6
  39.6 3.3 %collective-permute-start.1 = (bf16[256,512]{0,1:T(8,128)(2,1)S(1)}, bf16[256,512]{0,1:T(8,128)(2,1)S(1)}, u32[]{:S(2)}, u32[]{:S(2)}) collective-permute-start(bf16[256,512]{0,1:T(8,128)(2,1)S(1)} %fusion.6), channel_id=1, source_target_pairs={{0,256},{32,288},{64,320},{96,352},{128,384},{160,416},{192,448},{... | collective-permute-start | bytes 786440 | tf_op jit(solution)/shard_map/ppermute | solution.py:12
  42.9 0.8 convolution_convert_fusion.1
  43.7 12.2 %collective-permute-start.3 = (bf16[256,512]{1,0:T(8,128)(2,1)S(1)}, bf16[256,512]{1,0:T(8,128)(2,1)S(1)}, u32[]{:S(2)}, u32[]{:S(2)}) collective-permute-start(bf16[256,512]{1,0:T(8,128)(2,1)S(1)} %get-tuple-element.10), channel_id=1, source_target_pairs={{0,16},{1,17},{2,18},{3,19},{4,20},{5,21},{6,22},{7,23},{8,24},{9,... | collective-permute-start | bytes 786440 | tf_op jit(solution)/shard_map/ppermute | solution.py:12
  55.9 0.3 fusion.29
  56.3 0.0 collective-permute-done.1
  56.3 0.3 fusion.1
  56.6 1.9 %collective-permute-start.2 = (bf16[256,512]{1,0:T(8,128)(2,1)S(1)}, bf16[256,512]{1,0:T(8,128)(2,1)S(1)}, u32[]{:S(2)}, u32[]{:S(2)}) collective-permute-start(bf16[256,512]{1,0:T(8,128)(2,1)S(1)} %fusion.1), channel_id=1, source_target_pairs={{0,1},{1,0},{2,3},{3,2},{4,5},{5,4},{6,7},{7,6},{8,9},{9,8},{10,11... | collective-permute-start | bytes 786440 | tf_op jit(solution)/shard_map/ppermute | solution.py:12
  58.5 0.8 convolution_convert_fusion
  59.3 0.3 convolution_bitcast_fusion
  59.6 11.9 %collective-permute-done.3 = bf16[256,512]{1,0:T(8,128)(2,1)S(1)} collective-permute-done((bf16[256,512]{1,0:T(8,128)(2,1)S(1)}, bf16[256,512]{1,0:T(8,128)(2,1)S(1)}, u32[]{:S(2)}, u32[]{:S(2)}) %collective-permute-start.3) | collective-permute-done | bytes 262176 | tf_op jit(solution)/shard_map/ppermute | solution.py:12
  71.6 0.3 fusion.3
  71.9 3.5 %collective-permute-start.4 = (bf16[256,512]{0,1:T(8,128)(2,1)S(1)}, bf16[256,512]{0,1:T(8,128)(2,1)S(1)}, u32[]{:S(2)}, u32[]{:S(2)}) collective-permute-start(bf16[256,512]{0,1:T(8,128)(2,1)S(1)} %fusion.3), channel_id=1, source_target_pairs={{0,256},{32,288},{64,320},{96,352},{128,384},{160,416},{192,448},{... | collective-permute-start | bytes 786440 | tf_op jit(solution)/shard_map/ppermute | solution.py:12
  75.5 0.3 fusion.23
  75.8 0.3 fusion.27
  76.1 7.3 %collective-permute-done.4 = bf16[256,512]{0,1:T(8,128)(2,1)S(1)} collective-permute-done((bf16[256,512]{0,1:T(8,128)(2,1)S(1)}, bf16[256,512]{0,1:T(8,128)(2,1)S(1)}, u32[]{:S(2)}, u32[]{:S(2)}) %collective-permute-start.4) | collective-permute-done | bytes 262176 | tf_op jit(solution)/shard_map/ppermute | solution.py:12
  83.4 0.3 fusion.4
  83.7 2.3 %collective-permute-start.5 = (bf16[256,512]{1,0:T(8,128)(2,1)S(1)}, bf16[256,512]{1,0:T(8,128)(2,1)S(1)}, u32[]{:S(2)}, u32[]{:S(2)}) collective-permute-start(bf16[256,512]{1,0:T(8,128)(2,1)S(1)} %fusion.4), channel_id=1, source_target_pairs={{0,1},{1,0},{2,3},{3,2},{4,5},{5,4},{6,7},{7,6},{8,9},{9,8},{10,11... | collective-permute-start | bytes 786440 | tf_op jit(solution)/shard_map/ppermute | solution.py:12
  86.1 0.3 fusion.2
  86.4 0.3 fusion.21
  86.7 6.2 %collective-permute-done.5 = bf16[256,512]{1,0:T(8,128)(2,1)S(1)} collective-permute-done((bf16[256,512]{1,0:T(8,128)(2,1)S(1)}, bf16[256,512]{1,0:T(8,128)(2,1)S(1)}, u32[]{:S(2)}, u32[]{:S(2)}) %collective-permute-start.5) | collective-permute-done | bytes 262176 | tf_op jit(solution)/shard_map/ppermute | solution.py:12
  92.8 0.3 fusion.5
  93.1 0.8 pad_maximum_fusion
  (1 shorter events, 0.0 us)
Async XLA Ops:
  1.1 38.2 %collective-permute-start = (bf16[256,512]{1,0:T(8,128)(2,1)S(1)}, bf16[256,512]{1,0:T(8,128)(2,1)S(1)}, u32[]{:S(2)}, u32[]{:S(2)}) collective-permute-start(bf16[256,512]{1,0:T(8,128)(2,1)S(1)} %get-tuple-element.20), channel_id=1, source_target_pairs={{0,16},{1,17},{2,18},{3,19},{4,20},{5,21},{6,22},{7,23},{8,24},{9,... | collective-permute-start | bytes 786440 | tf_op jit(solution)/shard_map/ppermute | solution.py:12
  18.8 1.0 %copy-start = (bf16[512,512]{1,0:T(8,128)(2,1)S(1)}, bf16[512,512]{1,0:T(8,128)(2,1)}, u32[]{:S(2)}) copy-start(bf16[512,512]{1,0:T(8,128)(2,1)} %param.4) | copy-start | bytes 1572868
  39.6 16.6 %collective-permute-start.1 = (bf16[256,512]{0,1:T(8,128)(2,1)S(1)}, bf16[256,512]{0,1:T(8,128)(2,1)S(1)}, u32[]{:S(2)}, u32[]{:S(2)}) collective-permute-start(bf16[256,512]{0,1:T(8,128)(2,1)S(1)} %fusion.6), channel_id=1, source_target_pairs={{0,256},{32,288},{64,320},{96,352},{128,384},{160,416},{192,448},{... | collective-permute-start | bytes 786440 | tf_op jit(solution)/shard_map/ppermute | solution.py:12
  43.7 27.9 %collective-permute-start.3 = (bf16[256,512]{1,0:T(8,128)(2,1)S(1)}, bf16[256,512]{1,0:T(8,128)(2,1)S(1)}, u32[]{:S(2)}, u32[]{:S(2)}) collective-permute-start(bf16[256,512]{1,0:T(8,128)(2,1)S(1)} %get-tuple-element.10), channel_id=1, source_target_pairs={{0,16},{1,17},{2,18},{3,19},{4,20},{5,21},{6,22},{7,23},{8,24},{9,... | collective-permute-start | bytes 786440 | tf_op jit(solution)/shard_map/ppermute | solution.py:12
  56.6 15.0 %collective-permute-start.2 = (bf16[256,512]{1,0:T(8,128)(2,1)S(1)}, bf16[256,512]{1,0:T(8,128)(2,1)S(1)}, u32[]{:S(2)}, u32[]{:S(2)}) collective-permute-start(bf16[256,512]{1,0:T(8,128)(2,1)S(1)} %fusion.1), channel_id=1, source_target_pairs={{0,1},{1,0},{2,3},{3,2},{4,5},{5,4},{6,7},{7,6},{8,9},{9,8},{10,11... | collective-permute-start | bytes 786440 | tf_op jit(solution)/shard_map/ppermute | solution.py:12
  71.9 11.5 %collective-permute-start.4 = (bf16[256,512]{0,1:T(8,128)(2,1)S(1)}, bf16[256,512]{0,1:T(8,128)(2,1)S(1)}, u32[]{:S(2)}, u32[]{:S(2)}) collective-permute-start(bf16[256,512]{0,1:T(8,128)(2,1)S(1)} %fusion.3), channel_id=1, source_target_pairs={{0,256},{32,288},{64,320},{96,352},{128,384},{160,416},{192,448},{... | collective-permute-start | bytes 786440 | tf_op jit(solution)/shard_map/ppermute | solution.py:12
  83.7 9.1 %collective-permute-start.5 = (bf16[256,512]{1,0:T(8,128)(2,1)S(1)}, bf16[256,512]{1,0:T(8,128)(2,1)S(1)}, u32[]{:S(2)}, u32[]{:S(2)}) collective-permute-start(bf16[256,512]{1,0:T(8,128)(2,1)S(1)} %fusion.4), channel_id=1, source_target_pairs={{0,1},{1,0},{2,3},{3,2},{4,5},{5,4},{6,7},{7,6},{8,9},{9,8},{10,11... | collective-permute-start | bytes 786440 | tf_op jit(solution)/shard_map/ppermute | solution.py:12

commit v5 on v2

--- a/solution.py
+++ b/solution.py
@@ -40,8 +40,8 @@
         panel = probes[chunk * rows:(chunk + 1) * rows]
         for level, (axis, bit) in enumerate(plan):
             own, cross = weights[level]
-            if level == 0:
-                step = (2**bit // 2) * (1 if chunk % 2 == 0 else -1)
+            if level == 0 and chunk % 2 == 1:
+                step = -(2**bit // 2)
                 other = shifted(shifted(panel, axis, step), axis, step)
             else:
                 other = from_partner(panel, axis, bit)

time: 95.9 us -> 109 us (1.14)
  the two profiles are of different devices: /device:TPU:120 before, /device:TPU:1 now
where the time goes in v5:
time: 109 us
  waiting for transfers between devices  57.6 us (53%)
  starting transfers between devices  39.8 us (37%)
  matrix products  6.12 us (6%)
  local copies, waits for them, and re-layouts  4.18 us (4%)
    ppermute x2, waiting for transfers between devices, shifted(): return lax.ppermute(value, axis, pairs)  47.6 us
    ppermute x5, starting transfers between devices, from_partner(): return lax.ppermute(value, axis, pairs)  30.9 us
    ppermute x5, waiting for transfers between devices, from_partner(): return lax.ppermute(value, axis, pairs)  10.1 us
    ppermute x2, starting transfers between devices, shifted(): return lax.ppermute(value, axis, pairs)  8.93 us
    dot_general x3, matrix products, permuted_columns(): jnp.dot(weights, onehot, preferred_element_type=jnp.float32)  2.28 us
  transfers between devices with their start and end apart: 7, of which 5 were waited for; matrix products, arithmetic and copies ran while one was open for 8% of the time, Pallas kernels for 0%

profile of v5, /device:TPU:1, one launch (start us, length us, event | category | flops | bytes accessed | tf_op | source)
XLA Modules:
  0.0 108.8 jit_solution(1297683106319545524)
XLA Ops:
  0.0 1.1 fusion.41
  1.1 16.3 %collective-permute-start = (bf16[256,512]{1,0:T(8,128)(2,1)S(1)}, bf16[256,512]{1,0:T(8,128)(2,1)S(1)}, u32[]{:S(2)}, u32[]{:S(2)}) collective-permute-start(bf16[256,512]{1,0:T(8,128)(2,1)S(1)} %get-tuple-element.11), channel_id=1, source_target_pairs={{0,16},{1,17},{2,18},{3,19},{4,20},{5,21},{6,22},{7,23},{8,24},{9,... | collective-permute-start | bytes 786440 | tf_op jit(solution)/shard_map/ppermute | solution.py:12
  17.3 1.9 %collective-permute-start.3 = (bf16[256,512]{1,0:T(8,128)(2,1)S(1)}, bf16[256,512]{1,0:T(8,128)(2,1)S(1)}, u32[]{:S(2)}, u32[]{:S(2)}) collective-permute-start(bf16[256,512]{1,0:T(8,128)(2,1)S(1)} %get-tuple-element.12), channel_id=1, source_target_pairs={{0,24},{1,25},{2,26},{3,27},{4,28},{5,29},{6,30},{7,31},{8,0},{9,1... | collective-permute-start | bytes 786440 | tf_op jit(solution)/shard_map/ppermute | solution.py:18
  19.3 0.8 fusion.42
  20.1 2.0 %slice_bitcast_fusion = (bf16[512,512]{1,0:T(8,128)(2,1)S(1)}, bf16[512,512]{1,0:T(8,128)(2,1)S(1)}, bf16[512,512]{1,0:T(8,128)(2,1)S(1)}, bf16[512,512]{1,0:T(8...) fusion(bf16[3,512,512]{2,1,0:T(8,128)(2,1)} %param.6, bf16[3,512,512]{2,1,0:T(8,128)(2,1)} %param.5), kind=kLoop, calls=%fused_computation.29 | loop fusion | bytes 6291456 | tf_op jit(solution)/shard_map/squeeze | solution.py:34
  22.1 0.8 convolution_convert_fusion.2
  22.9 0.3 copy-done
  23.2 0.3 fusion.34
  23.5 0.8 convolution_convert_fusion.1
  24.3 0.8 convolution_convert_fusion
  25.0 0.3 fusion.32
  25.4 38.7 %collective-permute-done.3 = bf16[256,512]{1,0:T(8,128)(2,1)S(1)} collective-permute-done((bf16[256,512]{1,0:T(8,128)(2,1)S(1)}, bf16[256,512]{1,0:T(8,128)(2,1)S(1)}, u32[]{:S(2)}, u32[]{:S(2)}) %collective-permute-start.3) | collective-permute-done | bytes 262176 | tf_op jit(solution)/shard_map/ppermute | solution.py:18
  64.1 7.0 %collective-permute-start.4 = (bf16[256,512]{1,0:T(8,128)(2,1)S(1)}, bf16[256,512]{1,0:T(8,128)(2,1)S(1)}, u32[]{:S(2)}, u32[]{:S(2)}) collective-permute-start(bf16[256,512]{1,0:T(8,128)(2,1)S(1)} %collective-permute-done.3), channel_id=1, source_target_pairs={{0,24},{1,25},{2,26},{3,27},{4,28},{5,29},{6,30},{7,31},{8,0},{9,1... | collective-permute-start | bytes 786440 | tf_op jit(solution)/shard_map/ppermute | solution.py:18
  71.1 0.3 fusion
  71.5 4.7 %collective-permute-start.1 = (bf16[256,512]{0,1:T(8,128)(2,1)S(1)}, bf16[256,512]{0,1:T(8,128)(2,1)S(1)}, u32[]{:S(2)}, u32[]{:S(2)}) collective-permute-start(bf16[256,512]{0,1:T(8,128)(2,1)S(1)} %bitcast.28), channel_id=1, source_target_pairs={{0,256},{32,288},{64,320},{96,352},{128,384},{160,416},{192,448},{... | collective-permute-start | bytes 786440 | tf_op jit(solution)/shard_map/ppermute | solution.py:12
  76.1 0.3 fusion.28
  76.4 8.9 %collective-permute-done.4 = bf16[256,512]{1,0:T(8,128)(2,1)S(1)} collective-permute-done((bf16[256,512]{1,0:T(8,128)(2,1)S(1)}, bf16[256,512]{1,0:T(8,128)(2,1)S(1)}, u32[]{:S(2)}, u32[]{:S(2)}) %collective-permute-start.4) | collective-permute-done | bytes 262176 | tf_op jit(solution)/shard_map/ppermute | solution.py:18
  85.3 0.3 fusion.3
  85.7 4.6 %collective-permute-start.5 = (bf16[256,512]{0,1:T(8,128)(2,1)S(1)}, bf16[256,512]{0,1:T(8,128)(2,1)S(1)}, u32[]{:S(2)}, u32[]{:S(2)}) collective-permute-start(bf16[256,512]{0,1:T(8,128)(2,1)S(1)} %bitcast.27), channel_id=1, source_target_pairs={{0,256},{32,288},{64,320},{96,352},{128,384},{160,416},{192,448},{... | collective-permute-start | bytes 786440 | tf_op jit(solution)/shard_map/ppermute | solution.py:12
  90.4 0.3 fusion.1
  90.7 0.3 fusion.26
  91.0 2.2 %collective-permute-start.2 = (bf16[256,512]{1,0:T(8,128)(2,1)S(1)}, bf16[256,512]{1,0:T(8,128)(2,1)S(1)}, u32[]{:S(2)}, u32[]{:S(2)}) collective-permute-start(bf16[256,512]{1,0:T(8,128)(2,1)S(1)} %fusion.1), channel_id=1, source_target_pairs={{0,1},{1,0},{2,3},{3,2},{4,5},{5,4},{6,7},{7,6},{8,9},{9,8},{10,11... | collective-permute-start | bytes 786440 | tf_op jit(solution)/shard_map/ppermute | solution.py:12
  93.2 0.3 fusion.22
  93.5 2.9 %collective-permute-done.5 = bf16[256,512]{0,1:T(8,128)(2,1)S(1)} collective-permute-done((bf16[256,512]{0,1:T(8,128)(2,1)S(1)}, bf16[256,512]{0,1:T(8,128)(2,1)S(1)}, u32[]{:S(2)}, u32[]{:S(2)}) %collective-permute-start.5) | collective-permute-done | bytes 262176 | tf_op jit(solution)/shard_map/ppermute | solution.py:12
  96.4 0.3 fusion.4
  96.7 3.1 %collective-permute-start.6 = (bf16[256,512]{1,0:T(8,128)(2,1)S(1)}, bf16[256,512]{1,0:T(8,128)(2,1)S(1)}, u32[]{:S(2)}, u32[]{:S(2)}) collective-permute-start(bf16[256,512]{1,0:T(8,128)(2,1)S(1)} %fusion.4), channel_id=1, source_target_pairs={{0,1},{1,0},{2,3},{3,2},{4,5},{5,4},{6,7},{7,6},{8,9},{9,8},{10,11... | collective-permute-start | bytes 786440 | tf_op jit(solution)/shard_map/ppermute | solution.py:12
  99.9 0.3 fusion.20
  100.2 2.0 %collective-permute-done.2 = bf16[256,512]{1,0:T(8,128)(2,1)S(1)} collective-permute-done((bf16[256,512]{1,0:T(8,128)(2,1)S(1)}, bf16[256,512]{1,0:T(8,128)(2,1)S(1)}, u32[]{:S(2)}, u32[]{:S(2)}) %collective-permute-start.2) | collective-permute-done | bytes 262176 | tf_op jit(solution)/shard_map/ppermute | solution.py:12
  102.1 0.3 fusion.2
  102.4 5.2 %collective-permute-done.6 = bf16[256,512]{1,0:T(8,128)(2,1)S(1)} collective-permute-done((bf16[256,512]{1,0:T(8,128)(2,1)S(1)}, bf16[256,512]{1,0:T(8,128)(2,1)S(1)}, u32[]{:S(2)}, u32[]{:S(2)}) %collective-permute-start.6) | collective-permute-done | bytes 262176 | tf_op jit(solution)/shard_map/ppermute | solution.py:12
  107.6 0.3 fusion.5
  108.0 0.8 pad_maximum_fusion
  (3 shorter events, 0.0 us)
Async XLA Ops:
  1.1 70.0 %collective-permute-start = (bf16[256,512]{1,0:T(8,128)(2,1)S(1)}, bf16[256,512]{1,0:T(8,128)(2,1)S(1)}, u32[]{:S(2)}, u32[]{:S(2)}) collective-permute-start(bf16[256,512]{1,0:T(8,128)(2,1)S(1)} %get-tuple-element.11), channel_id=1, source_target_pairs={{0,16},{1,17},{2,18},{3,19},{4,20},{5,21},{6,22},{7,23},{8,24},{9,... | collective-permute-start | bytes 786440 | tf_op jit(solution)/shard_map/ppermute | solution.py:12
  17.3 46.7 %collective-permute-start.3 = (bf16[256,512]{1,0:T(8,128)(2,1)S(1)}, bf16[256,512]{1,0:T(8,128)(2,1)S(1)}, u32[]{:S(2)}, u32[]{:S(2)}) collective-permute-start(bf16[256,512]{1,0:T(8,128)(2,1)S(1)} %get-tuple-element.12), channel_id=1, source_target_pairs={{0,24},{1,25},{2,26},{3,27},{4,28},{5,29},{6,30},{7,31},{8,0},{9,1... | collective-permute-start | bytes 786440 | tf_op jit(solution)/shard_map/ppermute | solution.py:18
  22.1 1.0 copy-start
  64.1 21.3 %collective-permute-start.4 = (bf16[256,512]{1,0:T(8,128)(2,1)S(1)}, bf16[256,512]{1,0:T(8,128)(2,1)S(1)}, u32[]{:S(2)}, u32[]{:S(2)}) collective-permute-start(bf16[256,512]{1,0:T(8,128)(2,1)S(1)} %collective-permute-done.3), channel_id=1, source_target_pairs={{0,24},{1,25},{2,26},{3,27},{4,28},{5,29},{6,30},{7,31},{8,0},{9,1... | collective-permute-start | bytes 786440 | tf_op jit(solution)/shard_map/ppermute | solution.py:18
  71.5 18.9 %collective-permute-start.1 = (bf16[256,512]{0,1:T(8,128)(2,1)S(1)}, bf16[256,512]{0,1:T(8,128)(2,1)S(1)}, u32[]{:S(2)}, u32[]{:S(2)}) collective-permute-start(bf16[256,512]{0,1:T(8,128)(2,1)S(1)} %bitcast.28), channel_id=1, source_target_pairs={{0,256},{32,288},{64,320},{96,352},{128,384},{160,416},{192,448},{... | collective-permute-start | bytes 786440 | tf_op jit(solution)/shard_map/ppermute | solution.py:12
  85.7 10.7 %collective-permute-start.5 = (bf16[256,512]{0,1:T(8,128)(2,1)S(1)}, bf16[256,512]{0,1:T(8,128)(2,1)S(1)}, u32[]{:S(2)}, u32[]{:S(2)}) collective-permute-start(bf16[256,512]{0,1:T(8,128)(2,1)S(1)} %bitcast.27), channel_id=1, source_target_pairs={{0,256},{32,288},{64,320},{96,352},{128,384},{160,416},{192,448},{... | collective-permute-start | bytes 786440 | tf_op jit(solution)/shard_map/ppermute | solution.py:12
  91.0 11.1 %collective-permute-start.2 = (bf16[256,512]{1,0:T(8,128)(2,1)S(1)}, bf16[256,512]{1,0:T(8,128)(2,1)S(1)}, u32[]{:S(2)}, u32[]{:S(2)}) collective-permute-start(bf16[256,512]{1,0:T(8,128)(2,1)S(1)} %fusion.1), channel_id=1, source_target_pairs={{0,1},{1,0},{2,3},{3,2},{4,5},{5,4},{6,7},{7,6},{8,9},{9,8},{10,11... | collective-permute-start | bytes 786440 | tf_op jit(solution)/shard_map/ppermute | solution.py:12
  96.7 10.9 %collective-permute-start.6 = (bf16[256,512]{1,0:T(8,128)(2,1)S(1)}, bf16[256,512]{1,0:T(8,128)(2,1)S(1)}, u32[]{:S(2)}, u32[]{:S(2)}) collective-permute-start(bf16[256,512]{1,0:T(8,128)(2,1)S(1)} %fusion.4), channel_id=1, source_target_pairs={{0,1},{1,0},{2,3},{3,2},{4,5},{5,4},{6,7},{7,6},{8,9},{9,8},{10,11... | collective-permute-start | bytes 786440 | tf_op jit(solution)/shard_map/ppermute | solution.py:12

commit v6 on v1

--- a/solution.py
+++ b/solution.py
@@ -29,9 +29,11 @@
         both = permuted_columns(both, level_perm[level])
         weights.append((both[:br], both[br:]))
     rows = probes.shape[0] // CHUNKS
+    panels = [probes[chunk * rows:(chunk + 1) * rows] for chunk in range(CHUNKS)]
+    weights, panels[1:] = lax.optimization_barrier((weights, panels[1:]))
     outs = []
     for chunk in range(CHUNKS):
-        panel = probes[chunk * rows:(chunk + 1) * rows]
+        panel = panels[chunk]
         for level, (axis, bit) in enumerate(plan):
             own, cross = weights[level]
             other = from_partner(panel, axis, bit)

time: 86 us -> 93.5 us (1.087)
  the two profiles are of different devices: /device:TPU:48 before, /device:TPU:8 now
where the time goes in v6:
time: 93.5 us; the launch traced here: 93.1 us
  waiting for transfers between devices  48.4 us (52%)
  starting transfers between devices  33.5 us (36%)
  matrix products  5.99 us (6%)
  local copies, waits for them, and re-layouts  4.13 us (4%)
    ppermute x6, waiting for transfers between devices, from_partner(): return lax.ppermute(value, axis, pairs)  48.4 us
    ppermute x6, starting transfers between devices, from_partner(): return lax.ppermute(value, axis, pairs)  33.5 us
    dot_general x3, matrix products, permuted_columns(): jnp.dot(weights, onehot, preferred_element_type=jnp.float32)  2.28 us
    squeeze x1, local copies, waits for them, and re-layouts, per_device(): both = jnp.concatenate([own_blocks[level], cross_blocks[level]], axis=0)  2.03 us
  transfers between devices with their start and end apart: 6, of which 4 were waited for; matrix products, arithmetic and copies ran while one was open for 9% of the time, Pallas kernels for 0%

profile of v6, /device:TPU:8, one launch (start us, length us, event | category | flops | bytes accessed | tf_op | source)
XLA Modules:
  0.0 93.1 jit_solution(16782730448564256326)
XLA Ops:
  0.0 1.1 %fusion.26 = (bf16[256,512]{1,0:T(8,128)(2,1)S(1)}, bf16[256,512]{1,0:T(8,128)(2,1)S(1)}) fusion(bf16[512,512]{1,0:T(8,128)(2,1)} %param.4), kind=kLoop, calls=%fused_computation.45 | loop fusion | bytes 1048576 | tf_op jit(solution)/shard_map/slice | solution.py:32
  1.1 15.7 %collective-permute-start = (bf16[256,512]{1,0:T(8,128)(2,1)S(1)}, bf16[256,512]{1,0:T(8,128)(2,1)S(1)}, u32[]{:S(2)}, u32[]{:S(2)}) collective-permute-start(bf16[256,512]{1,0:T(8,128)(2,1)S(1)} %get-tuple-element.31), channel_id=1, source_target_pairs={{0,16},{1,17},{2,18},{3,19},{4,20},{5,21},{6,22},{7,23},{8,24},{9,... | collective-permute-start | bytes 786440 | tf_op jit(solution)/shard_map/ppermute | solution.py:12
  16.8 0.8 fusion.27
  17.6 2.0 %slice_bitcast_fusion = (bf16[512,512]{1,0:T(8,128)(2,1)S(1)}, bf16[512,512]{1,0:T(8,128)(2,1)S(1)}, bf16[512,512]{1,0:T(8,128)(2,1)S(1)}, bf16[512,512]{1,0:T(8...) fusion(bf16[3,512,512]{2,1,0:T(8,128)(2,1)} %param.6, bf16[3,512,512]{2,1,0:T(8,128)(2,1)} %param.5), kind=kLoop, calls=%fused_computation.29 | loop fusion | bytes 6291456 | tf_op jit(solution)/shard_map/squeeze | solution.py:28
  19.7 0.8 convolution_convert_fusion
  20.4 0.1 fusion.23
  20.5 0.8 convolution_convert_fusion.1
  21.3 0.1 fusion.24
  21.3 0.8 convolution_convert_fusion.2
  22.1 0.1 fusion.25
  22.2 2.1 %collective-permute-start.3 = (bf16[256,512]{1,0:T(8,128)(2,1)S(1)}, bf16[256,512]{1,0:T(8,128)(2,1)S(1)}, u32[]{:S(2)}, u32[]{:S(2)}) collective-permute-start(bf16[256,512]{1,0:T(8,128)(2,1)S(1)} %get-tuple-element.18), channel_id=1, source_target_pairs={{0,16},{1,17},{2,18},{3,19},{4,20},{5,21},{6,22},{7,23},{8,24},{9,... | collective-permute-start | bytes 786440 | tf_op jit(solution)/shard_map/ppermute | solution.py:12
  24.3 0.3 fusion.21
  24.6 0.3 fusion.30
  24.9 0.4 fusion
  25.3 4.9 %collective-permute-start.1 = (bf16[256,512]{0,1:T(8,128)(2,1)S(1)}, bf16[256,512]{0,1:T(8,128)(2,1)S(1)}, u32[]{:S(2)}, u32[]{:S(2)}) collective-permute-start(bf16[256,512]{0,1:T(8,128)(2,1)S(1)} %bitcast.39), channel_id=1, source_target_pairs={{0,256},{32,288},{64,320},{96,352},{128,384},{160,416},{192,448},{... | collective-permute-start | bytes 786440 | tf_op jit(solution)/shard_map/ppermute | solution.py:12
  30.2 38.2 %collective-permute-done.3 = bf16[256,512]{1,0:T(8,128)(2,1)S(1)} collective-permute-done((bf16[256,512]{1,0:T(8,128)(2,1)S(1)}, bf16[256,512]{1,0:T(8,128)(2,1)S(1)}, u32[]{:S(2)}, u32[]{:S(2)}) %collective-permute-start.3) | collective-permute-done | bytes 262176 | tf_op jit(solution)/shard_map/ppermute | solution.py:12
  68.4 0.3 fusion.3
  68.7 0.3 fusion.28
  69.0 4.9 %collective-permute-start.4 = (bf16[256,512]{1,0:T(8,128)(2,1)S(1)}, bf16[256,512]{1,0:T(8,128)(2,1)S(1)}, u32[]{:S(2)}, u32[]{:S(2)}) collective-permute-start(bf16[256,512]{1,0:T(8,128)(2,1)S(1)} %fusion.3), channel_id=1, source_target_pairs={{0,256},{32,288},{64,320},{96,352},{128,384},{160,416},{192,448},{... | collective-permute-start | bytes 786440 | tf_op jit(solution)/shard_map/ppermute | solution.py:12
  74.0 0.3 fusion.31
  74.3 0.3 fusion.1
  74.6 2.5 %collective-permute-start.2 = (bf16[256,512]{1,0:T(8,128)(2,1)S(1)}, bf16[256,512]{1,0:T(8,128)(2,1)S(1)}, u32[]{:S(2)}, u32[]{:S(2)}) collective-permute-start(bf16[256,512]{1,0:T(8,128)(2,1)S(1)} %fusion.1), channel_id=1, source_target_pairs={{0,1},{1,0},{2,3},{3,2},{4,5},{5,4},{6,7},{7,6},{8,9},{9,8},{10,11... | collective-permute-start | bytes 786440 | tf_op jit(solution)/shard_map/ppermute | solution.py:12
  77.1 4.5 %collective-permute-done.4 = bf16[256,512]{1,0:T(8,128)(2,1)S(1)} collective-permute-done((bf16[256,512]{1,0:T(8,128)(2,1)S(1)}, bf16[256,512]{1,0:T(8,128)(2,1)S(1)}, u32[]{:S(2)}, u32[]{:S(2)}) %collective-permute-start.4) | collective-permute-done | bytes 262176 | tf_op jit(solution)/shard_map/ppermute | solution.py:12
  81.6 0.3 fusion.4
  81.9 0.3 fusion.29
  82.2 3.4 %collective-permute-start.5 = (bf16[256,512]{1,0:T(8,128)(2,1)S(1)}, bf16[256,512]{1,0:T(8,128)(2,1)S(1)}, u32[]{:S(2)}, u32[]{:S(2)}) collective-permute-start(bf16[256,512]{1,0:T(8,128)(2,1)S(1)} %fusion.4), channel_id=1, source_target_pairs={{0,1},{1,0},{2,3},{3,2},{4,5},{5,4},{6,7},{7,6},{8,9},{9,8},{10,11... | collective-permute-start | bytes 786440 | tf_op jit(solution)/shard_map/ppermute | solution.py:12
  85.6 0.3 fusion.32
  85.9 1.4 %collective-permute-done.2 = bf16[256,512]{1,0:T(8,128)(2,1)S(1)} collective-permute-done((bf16[256,512]{1,0:T(8,128)(2,1)S(1)}, bf16[256,512]{1,0:T(8,128)(2,1)S(1)}, u32[]{:S(2)}, u32[]{:S(2)}) %collective-permute-start.2) | collective-permute-done | bytes 262176 | tf_op jit(solution)/shard_map/ppermute | solution.py:12
  87.3 0.3 fusion.2
  87.6 4.4 %collective-permute-done.5 = bf16[256,512]{1,0:T(8,128)(2,1)S(1)} collective-permute-done((bf16[256,512]{1,0:T(8,128)(2,1)S(1)}, bf16[256,512]{1,0:T(8,128)(2,1)S(1)}, u32[]{:S(2)}, u32[]{:S(2)}) %collective-permute-start.5) | collective-permute-done | bytes 262176 | tf_op jit(solution)/shard_map/ppermute | solution.py:12
  92.0 0.3 fusion.5
  92.3 0.8 pad_maximum_fusion
  (4 shorter events, 0.0 us)
Async XLA Ops:
  1.1 23.9 %collective-permute-start = (bf16[256,512]{1,0:T(8,128)(2,1)S(1)}, bf16[256,512]{1,0:T(8,128)(2,1)S(1)}, u32[]{:S(2)}, u32[]{:S(2)}) collective-permute-start(bf16[256,512]{1,0:T(8,128)(2,1)S(1)} %get-tuple-element.31), channel_id=1, source_target_pairs={{0,16},{1,17},{2,18},{3,19},{4,20},{5,21},{6,22},{7,23},{8,24},{9,... | collective-permute-start | bytes 786440 | tf_op jit(solution)/shard_map/ppermute | solution.py:12
  22.1 2.2 %copy-start = (bf16[512,512]{1,0:T(8,128)(2,1)S(1)}, bf16[512,512]{1,0:T(8,128)(2,1)}, u32[]{:S(2)}) copy-start(bf16[512,512]{1,0:T(8,128)(2,1)} %param.4) | copy-start | bytes 1572868
  22.2 46.2 %collective-permute-start.3 = (bf16[256,512]{1,0:T(8,128)(2,1)S(1)}, bf16[256,512]{1,0:T(8,128)(2,1)S(1)}, u32[]{:S(2)}, u32[]{:S(2)}) collective-permute-start(bf16[256,512]{1,0:T(8,128)(2,1)S(1)} %get-tuple-element.18), channel_id=1, source_target_pairs={{0,16},{1,17},{2,18},{3,19},{4,20},{5,21},{6,22},{7,23},{8,24},{9,... | collective-permute-start | bytes 786440 | tf_op jit(solution)/shard_map/ppermute | solution.py:12
  25.3 49.0 %collective-permute-start.1 = (bf16[256,512]{0,1:T(8,128)(2,1)S(1)}, bf16[256,512]{0,1:T(8,128)(2,1)S(1)}, u32[]{:S(2)}, u32[]{:S(2)}) collective-permute-start(bf16[256,512]{0,1:T(8,128)(2,1)S(1)} %bitcast.39), channel_id=1, source_target_pairs={{0,256},{32,288},{64,320},{96,352},{128,384},{160,416},{192,448},{... | collective-permute-start | bytes 786440 | tf_op jit(solution)/shard_map/ppermute | solution.py:12
  69.0 12.6 %collective-permute-start.4 = (bf16[256,512]{1,0:T(8,128)(2,1)S(1)}, bf16[256,512]{1,0:T(8,128)(2,1)S(1)}, u32[]{:S(2)}, u32[]{:S(2)}) collective-permute-start(bf16[256,512]{1,0:T(8,128)(2,1)S(1)} %fusion.3), channel_id=1, source_target_pairs={{0,256},{32,288},{64,320},{96,352},{128,384},{160,416},{192,448},{... | collective-permute-start | bytes 786440 | tf_op jit(solution)/shard_map/ppermute | solution.py:12
  74.6 12.7 %collective-permute-start.2 = (bf16[256,512]{1,0:T(8,128)(2,1)S(1)}, bf16[256,512]{1,0:T(8,128)(2,1)S(1)}, u32[]{:S(2)}, u32[]{:S(2)}) collective-permute-start(bf16[256,512]{1,0:T(8,128)(2,1)S(1)} %fusion.1), channel_id=1, source_target_pairs={{0,1},{1,0},{2,3},{3,2},{4,5},{5,4},{6,7},{7,6},{8,9},{9,8},{10,11... | collective-permute-start | bytes 786440 | tf_op jit(solution)/shard_map/ppermute | solution.py:12
  82.2 9.8 %collective-permute-start.5 = (bf16[256,512]{1,0:T(8,128)(2,1)S(1)}, bf16[256,512]{1,0:T(8,128)(2,1)S(1)}, u32[]{:S(2)}, u32[]{:S(2)}) collective-permute-start(bf16[256,512]{1,0:T(8,128)(2,1)S(1)} %fusion.4), channel_id=1, source_target_pairs={{0,1},{1,0},{2,3},{3,2},{4,5},{5,4},{6,7},{7,6},{8,9},{9,8},{10,11... | collective-permute-start | bytes 786440 | tf_op jit(solution)/shard_map/ppermute | solution.py:12

commit v7 on v1

v7 whole, which is shorter than its diff:
```python
import jax
import jax.numpy as jnp
from jax import lax
from jax.sharding import PartitionSpec as P

CHUNKS = 2


def from_partner(value, axis, distance):
    mask = 2**distance
    pairs = [(source, source ^ mask) for source in range(lax.axis_size(axis))]
    return lax.ppermute(value, axis, pairs)


def from_diagonal(value, row_bit, col_bit):
    rows, cols = lax.axis_size("row"), lax.axis_size("col")
    pairs = [
        (r * cols + c, (r ^ 2**row_bit) * cols + (c ^ 2**col_bit)) for r in range(rows) for c in range(cols)
    ]
    return lax.ppermute(value, ("row", "col"), pairs)


def permuted_columns(weights, order):
    n = weights.shape[-1]
    onehot = (lax.broadcasted_iota(jnp.int32, (n, n), 0) == order[None, :]).astype(weights.dtype)
    return jnp.dot(weights, onehot, preferred_element_type=jnp.float32).astype(weights.dtype)


def split(product):
    high = product.astype(jnp.bfloat16)
    low = (product - high.astype(jnp.float32)).astype(jnp.bfloat16)
    return high, low


def times(panel, pair):
    high, low = pair
    total = jnp.dot(panel, high, preferred_element_type=jnp.float32)
    return total + jnp.dot(panel, low, preferred_element_type=jnp.float32)


def product(a, b):
    return jnp.dot(a, b, preferred_element_type=jnp.float32)


def per_device(probes, own_blocks, cross_blocks, level_perm):
    col_bits = lax.axis_size("col").bit_length() - 1
    row_bits = lax.axis_size("row").bit_length() - 1
    z_bit, hi_bit, lo_bit = col_bits - 1, row_bits - 1, 0
    br = own_blocks.shape[1]
    weights = []
    for level in range(3):
        both = jnp.concatenate([own_blocks[level], cross_blocks[level]], axis=0)
        both = permuted_columns(both, level_perm[level])
        weights.append((both[:br], both[br:]))
    (own0, cross0), (own1, cross1), (own2, cross2) = weights
    theirs = from_partner(jnp.stack([cross2, cross1, own2]), "col", lo_bit)
    k_self = split(product(own1, own2))
    k_diag = split(product(theirs[1], cross2))
    k_to_p = split(product(own1, theirs[0]))
    k_diag_p = split(product(theirs[1], theirs[2]))
    rows = probes.shape[0] // CHUNKS
    outs = []
    for chunk in range(CHUNKS):
        panel = probes[chunk * rows:(chunk + 1) * rows]
        other = from_partner(panel, "col", z_bit)
        total = jnp.dot(panel, own0, preferred_element_type=jnp.float32)
        total = total + jnp.dot(other, cross0, preferred_element_type=jnp.float32)
        panel = total.astype(jnp.bfloat16)
        diag = from_diagonal(panel, hi_bit, lo_bit)
        share = (times(panel, k_to_p) + times(diag, k_diag_p)).astype(jnp.bfloat16)
        received = from_partner(share, "col", lo_bit)
        total = times(panel, k_self) + times(diag, k_diag)
        outs.append((total + received.astype(jnp.float32)).astype(jnp.bfloat16))
    return jnp.concatenate(outs, axis=0)


def solution(mesh):
    placed = (
        P(None, ("row", "col")),
        P(None, ("row", "col"), None),
        P(None, ("row", "col"), None),
        P(None, ("row", "col")),
    )
    return jax.shard_map(
        per_device, mesh=mesh, in_specs=placed, out_specs=P(None, ("row", "col")), check_vma=False
    )
```

time: 86 us -> 90.7 us (1.055)
  the two profiles are of different devices: /device:TPU:48 before, /device:TPU:62 now
where the time goes in v7:
time: 90.7 us; the launch traced here: 90.3 us
  waiting for transfers between devices  42.4 us (47%)
  starting transfers between devices  31.7 us (35%)
  matrix products  10.6 us (12%)
  local copies, waits for them, and re-layouts  4.3 us (5%)
  other arithmetic  1 us (1%)
    ppermute x5, waiting for transfers between devices, from_partner(): return lax.ppermute(value, axis, pairs)  40 us
    ppermute x5, starting transfers between devices, from_partner(): return lax.ppermute(value, axis, pairs)  24.6 us
    ppermute x2, starting transfers between devices, from_diagonal(): return lax.ppermute(value, ('row', 'col'), pairs)  7.05 us
    dot_general x8, matrix products, times(): total = jnp.dot(panel, high, preferred_element_type=jnp.float32)  2.65 us
    dot_general x8, matrix products, times(): return total + jnp.dot(panel, low, preferred_element_type=jnp.float32)  2.57 us
    ppermute x2, waiting for transfers between devices, from_diagonal(): return lax.ppermute(value, ('row', 'col'), pairs)  2.34 us
    dot_general x3, matrix products, permuted_columns(): jnp.dot(weights, onehot, preferred_element_type=jnp.float32)  2.27 us
    squeeze x1, local copies, waits for them, and re-layouts, per_device(): both = jnp.concatenate([own_blocks[level], cross_blocks[level]], axis=0)  2.03 us
  transfers between devices with their start and end apart: 7, of which 5 were waited for; matrix products, arithmetic and copies ran while one was open for 15% of the time, Pallas kernels for 0%

profile of v7, /device:TPU:62, one launch (start us, length us, event | category | flops | bytes accessed | tf_op | source)
XLA Modules:
  0.0 90.3 jit_solution(7264501422744754610)
XLA Ops:
  0.0 1.1 %fusion.59 = (bf16[256,512]{1,0:T(8,128)(2,1)S(1)}, bf16[256,512]{1,0:T(8,128)(2,1)S(1)}) fusion(bf16[512,512]{1,0:T(8,128)(2,1)} %param.4), kind=kLoop, calls=%fused_computation.93 | loop fusion | bytes 1048576 | tf_op jit(solution)/shard_map/slice | solution.py:64
  1.1 14.8 %collective-permute-start = (bf16[256,512]{1,0:T(8,128)(2,1)S(1)}, bf16[256,512]{1,0:T(8,128)(2,1)S(1)}, u32[]{:S(2)}, u32[]{:S(2)}) collective-permute-start(bf16[256,512]{1,0:T(8,128)(2,1)S(1)} %get-tuple-element.13), channel_id=1, source_target_pairs={{0,16},{1,17},{2,18},{3,19},{4,20},{5,21},{6,22},{7,23},{8,24},{9,... | collective-permute-start | bytes 786440 | tf_op jit(solution)/shard_map/ppermute | solution.py:12
  15.9 1.9 %collective-permute-start.4 = (bf16[256,512]{1,0:T(8,128)(2,1)S(1)}, bf16[256,512]{1,0:T(8,128)(2,1)S(1)}, u32[]{:S(2)}, u32[]{:S(2)}) collective-permute-start(bf16[256,512]{1,0:T(8,128)(2,1)S(1)} %get-tuple-element.14), channel_id=1, source_target_pairs={{0,16},{1,17},{2,18},{3,19},{4,20},{5,21},{6,22},{7,23},{8,24},{9,... | collective-permute-start | bytes 786440 | tf_op jit(solution)/shard_map/ppermute | solution.py:12
  17.8 0.8 fusion.60
  18.6 2.0 %slice_bitcast_fusion.8 = (bf16[512,512]{1,0:T(8,128)(2,1)S(1)}, bf16[512,512]{1,0:T(8,128)(2,1)S(1)}, bf16[512,512]{1,0:T(8,128)(2,1)S(1)}, bf16[512,512]{1,0:T...) fusion(bf16[3,512,512]{2,1,0:T(8,128)(2,1)} %param.6, bf16[3,512,512]{2,1,0:T(8,128)(2,1)} %param.5), kind=kLoop, calls=%fused_computation.53 | loop fusion | bytes 6291456 | tf_op jit(solution)/shard_map/squeeze | solution.py:52
  20.7 0.8 convolution_convert_fusion.1
  21.5 0.8 convolution_convert_fusion
  22.5 2.7 %collective-permute-start.2 = (bf16[3,512,512]{2,1,0:T(8,128)(2,1)S(1)}, bf16[3,512,512]{2,1,0:T(8,128)(2,1)S(1)}, u32[]{:S(2)}, u32[]{:S(2)}) collective-permute-start(bf16[3,512,512]{2,1,0:T(8,128)(2,1)S(1)} %pad_maximum_fusion), channel_id=1, source_target_pairs={{0,1},{1,0},{2,3},{3,2},{4,5},{5,4},{6,7},{7,6},{8,9},{9,8},{10,11... | collective-permute-start | bytes 4718600 | tf_op jit(solution)/shard_map/ppermute | solution.py:12
  25.3 0.4 fusion.28
  25.7 0.8 convolution_convert_fusion.2
  26.7 0.3 fusion.34
  27.1 0.3 fusion.36
  27.4 34.5 %collective-permute-done.4 = bf16[256,512]{1,0:T(8,128)(2,1)S(1)} collective-permute-done((bf16[256,512]{1,0:T(8,128)(2,1)S(1)}, bf16[256,512]{1,0:T(8,128)(2,1)S(1)}, u32[]{:S(2)}, u32[]{:S(2)}) %collective-permute-start.4) | collective-permute-done | bytes 262176 | tf_op jit(solution)/shard_map/ppermute | solution.py:12
  61.9 0.3 fusion.10
  62.3 2.4 %collective-permute-start.5 = (bf16[256,512]{0,1:T(8,128)(2,1)S(1)}, bf16[256,512]{0,1:T(8,128)(2,1)S(1)}, u32[]{:S(2)}, u32[]{:S(2)}) collective-permute-start(bf16[256,512]{0,1:T(8,128)(2,1)S(1)} %bitcast.52), channel_id=1, source_target_pairs={{0,257},{1,256},{2,259},{3,258},{4,261},{5,260},{6,263},{7,262},{8... | collective-permute-start | bytes 786440 | tf_op jit(solution)/shard_map/ppermute | solution.py:20
  64.7 0.3 fusion.8
  65.0 4.7 %collective-permute-start.1 = (bf16[256,512]{0,1:T(8,128)(2,1)S(1)}, bf16[256,512]{0,1:T(8,128)(2,1)S(1)}, u32[]{:S(2)}, u32[]{:S(2)}) collective-permute-start(bf16[256,512]{0,1:T(8,128)(2,1)S(1)} %bitcast.51), channel_id=1, source_target_pairs={{0,257},{1,256},{2,259},{3,258},{4,261},{5,260},{6,263},{7,262},{8... | collective-permute-start | bytes 786440 | tf_op jit(solution)/shard_map/ppermute | solution.py:20
  69.7 0.3 fusion.53
  70.0 0.3 fusion.55
  70.4 0.3 convolution_add_fusion.3
  71.1 0.4 fusion.22
  72.2 0.4 fusion.21
  72.9 1.6 %collective-permute-done.5 = bf16[256,512]{0,1:T(8,128)(2,1)S(1)} collective-permute-done((bf16[256,512]{0,1:T(8,128)(2,1)S(1)}, bf16[256,512]{0,1:T(8,128)(2,1)S(1)}, u32[]{:S(2)}, u32[]{:S(2)}) %collective-permute-start.5) | collective-permute-done | bytes 262176 | tf_op jit(solution)/shard_map/ppermute | solution.py:20
  75.2 1.9 %collective-permute-start.6 = (bf16[256,512]{1,0:T(8,128)(2,1)S(1)}, bf16[256,512]{1,0:T(8,128)(2,1)S(1)}, u32[]{:S(2)}, u32[]{:S(2)}) collective-permute-start(bf16[256,512]{1,0:T(8,128)(2,1)S(1)} %fusion.7), channel_id=1, source_target_pairs={{0,1},{1,0},{2,3},{3,2},{4,5},{5,4},{6,7},{7,6},{8,9},{9,8},{10,11... | collective-permute-start | bytes 786440 | tf_op jit(solution)/shard_map/ppermute | solution.py:12
  77.4 0.7 collective-permute-done.1
  78.8 3.2 %collective-permute-start.3 = (bf16[256,512]{1,0:T(8,128)(2,1)S(1)}, bf16[256,512]{1,0:T(8,128)(2,1)S(1)}, u32[]{:S(2)}, u32[]{:S(2)}) collective-permute-start(bf16[256,512]{1,0:T(8,128)(2,1)S(1)} %fusion.6), channel_id=1, source_target_pairs={{0,1},{1,0},{2,3},{3,2},{4,5},{5,4},{6,7},{7,6},{8,9},{9,8},{10,11... | collective-permute-start | bytes 786440 | tf_op jit(solution)/shard_map/ppermute | solution.py:12
  82.0 0.4 fusion.26
  83.1 2.4 %collective-permute-done.6 = bf16[256,512]{1,0:T(8,128)(2,1)S(1)} collective-permute-done((bf16[256,512]{1,0:T(8,128)(2,1)S(1)}, bf16[256,512]{1,0:T(8,128)(2,1)S(1)}, u32[]{:S(2)}, u32[]{:S(2)}) %collective-permute-start.6) | collective-permute-done | bytes 262176 | tf_op jit(solution)/shard_map/ppermute | solution.py:12
  85.5 0.3 fusion.11
  85.8 3.2 %collective-permute-done.3 = bf16[256,512]{1,0:T(8,128)(2,1)S(1)} collective-permute-done((bf16[256,512]{1,0:T(8,128)(2,1)S(1)}, bf16[256,512]{1,0:T(8,128)(2,1)S(1)}, u32[]{:S(2)}, u32[]{:S(2)}) %collective-permute-start.3) | collective-permute-done | bytes 262176 | tf_op jit(solution)/shard_map/ppermute | solution.py:12
  89.1 0.3 fusion.9
  89.4 0.8 pad_maximum_fusion.1
  (18 shorter events, 4.1 us)
Async XLA Ops:
  1.1 63.6 %collective-permute-start = (bf16[256,512]{1,0:T(8,128)(2,1)S(1)}, bf16[256,512]{1,0:T(8,128)(2,1)S(1)}, u32[]{:S(2)}, u32[]{:S(2)}) collective-permute-start(bf16[256,512]{1,0:T(8,128)(2,1)S(1)} %get-tuple-element.13), channel_id=1, source_target_pairs={{0,16},{1,17},{2,18},{3,19},{4,20},{5,21},{6,22},{7,23},{8,24},{9,... | collective-permute-start | bytes 786440 | tf_op jit(solution)/shard_map/ppermute | solution.py:12
  15.9 46.0 %collective-permute-start.4 = (bf16[256,512]{1,0:T(8,128)(2,1)S(1)}, bf16[256,512]{1,0:T(8,128)(2,1)S(1)}, u32[]{:S(2)}, u32[]{:S(2)}) collective-permute-start(bf16[256,512]{1,0:T(8,128)(2,1)S(1)} %get-tuple-element.14), channel_id=1, source_target_pairs={{0,16},{1,17},{2,18},{3,19},{4,20},{5,21},{6,22},{7,23},{8,24},{9,... | collective-permute-start | bytes 786440 | tf_op jit(solution)/shard_map/ppermute | solution.py:12
  22.5 48.5 %collective-permute-start.2 = (bf16[3,512,512]{2,1,0:T(8,128)(2,1)S(1)}, bf16[3,512,512]{2,1,0:T(8,128)(2,1)S(1)}, u32[]{:S(2)}, u32[]{:S(2)}) collective-permute-start(bf16[3,512,512]{2,1,0:T(8,128)(2,1)S(1)} %pad_maximum_fusion), channel_id=1, source_target_pairs={{0,1},{1,0},{2,3},{3,2},{4,5},{5,4},{6,7},{7,6},{8,9},{9,8},{10,11... | collective-permute-start | bytes 4718600 | tf_op jit(solution)/shard_map/ppermute | solution.py:12
  25.7 1.0 %copy-start = (bf16[512,512]{1,0:T(8,128)(2,1)S(1)}, bf16[512,512]{1,0:T(8,128)(2,1)}, u32[]{:S(2)}) copy-start(bf16[512,512]{1,0:T(8,128)(2,1)} %param.4) | copy-start | bytes 1572868
  62.3 12.3 %collective-permute-start.5 = (bf16[256,512]{0,1:T(8,128)(2,1)S(1)}, bf16[256,512]{0,1:T(8,128)(2,1)S(1)}, u32[]{:S(2)}, u32[]{:S(2)}) collective-permute-start(bf16[256,512]{0,1:T(8,128)(2,1)S(1)} %bitcast.52), channel_id=1, source_target_pairs={{0,257},{1,256},{2,259},{3,258},{4,261},{5,260},{6,263},{7,262},{8... | collective-permute-start | bytes 786440 | tf_op jit(solution)/shard_map/ppermute | solution.py:20
  65.0 13.2 %collective-permute-start.1 = (bf16[256,512]{0,1:T(8,128)(2,1)S(1)}, bf16[256,512]{0,1:T(8,128)(2,1)S(1)}, u32[]{:S(2)}, u32[]{:S(2)}) collective-permute-start(bf16[256,512]{0,1:T(8,128)(2,1)S(1)} %bitcast.51), channel_id=1, source_target_pairs={{0,257},{1,256},{2,259},{3,258},{4,261},{5,260},{6,263},{7,262},{8... | collective-permute-start | bytes 786440 | tf_op jit(solution)/shard_map/ppermute | solution.py:20
  75.2 10.3 %collective-permute-start.6 = (bf16[256,512]{1,0:T(8,128)(2,1)S(1)}, bf16[256,512]{1,0:T(8,128)(2,1)S(1)}, u32[]{:S(2)}, u32[]{:S(2)}) collective-permute-start(bf16[256,512]{1,0:T(8,128)(2,1)S(1)} %fusion.7), channel_id=1, source_target_pairs={{0,1},{1,0},{2,3},{3,2},{4,5},{5,4},{6,7},{7,6},{8,9},{9,8},{10,11... | collective-permute-start | bytes 786440 | tf_op jit(solution)/shard_map/ppermute | solution.py:12
  78.8 10.3 %collective-permute-start.3 = (bf16[256,512]{1,0:T(8,128)(2,1)S(1)}, bf16[256,512]{1,0:T(8,128)(2,1)S(1)}, u32[]{:S(2)}, u32[]{:S(2)}) collective-permute-start(bf16[256,512]{1,0:T(8,128)(2,1)S(1)} %fusion.6), channel_id=1, source_target_pairs={{0,1},{1,0},{2,3},{3,2},{4,5},{5,4},{6,7},{7,6},{8,9},{9,8},{10,11... | collective-permute-start | bytes 786440 | tf_op jit(solution)/shard_map/ppermute | solution.py:12

commit v8 on v7

--- a/solution.py
+++ b/solution.py
@@ -63,6 +63,7 @@
     for chunk in range(CHUNKS):
         panel = probes[chunk * rows:(chunk + 1) * rows]
         other = from_partner(panel, "col", z_bit)
+        (k_self, k_diag, k_to_p, k_diag_p), other = lax.optimization_barrier(((k_self, k_diag, k_to_p, k_diag_p), other))
         total = jnp.dot(panel, own0, preferred_element_type=jnp.float32)
         total = total + jnp.dot(other, cross0, preferred_element_type=jnp.float32)
         panel = total.astype(jnp.bfloat16)

time: 90.7 us -> 90.6 us (level)
  the two profiles are of different devices: /device:TPU:62 before, /device:TPU:48 now
where the time goes in v8:
time: 90.6 us; the launch traced here: 90.2 us
  waiting for transfers between devices  43.6 us (48%)
  starting transfers between devices  31.8 us (35%)
  matrix products  10.6 us (12%)
  local copies, waits for them, and re-layouts  3 us (3%)
  other arithmetic  1 us (1%)
    ppermute x5, waiting for transfers between devices, from_partner(): return lax.ppermute(value, axis, pairs)  40.8 us
    ppermute x5, starting transfers between devices, from_partner(): return lax.ppermute(value, axis, pairs)  24.1 us
    ppermute x2, starting transfers between devices, from_diagonal(): return lax.ppermute(value, ('row', 'col'), pairs)  7.64 us
    ppermute x2, waiting for transfers between devices, from_diagonal(): return lax.ppermute(value, ('row', 'col'), pairs)  2.72 us
    dot_general x8, matrix products, times(): total = jnp.dot(panel, high, preferred_element_type=jnp.float32)  2.63 us
    dot_general x8, matrix products, times(): return total + jnp.dot(panel, low, preferred_element_type=jnp.float32)  2.52 us
    dot_general x3, matrix products, permuted_columns(): jnp.dot(weights, onehot, preferred_element_type=jnp.float32)  2.27 us
    squeeze x1, local copies, waits for them, and re-layouts, per_device(): both = jnp.concatenate([own_blocks[level], cross_blocks[level]], axis=0)  2.03 us
  transfers between devices with their start and end apart: 7, of which 6 were waited for; matrix products, arithmetic and copies ran while one was open for 10% of the time, Pallas kernels for 0%

profile of v8, /device:TPU:48, one launch (start us, length us, event | category | flops | bytes accessed | tf_op | source)
XLA Modules:
  0.0 90.2 jit_solution(3681210208524285617)
XLA Ops:
  0.0 0.8 fusion.42
  0.8 2.0 %slice_bitcast_fusion.8 = (bf16[512,512]{1,0:T(8,128)(2,1)S(1)}, bf16[512,512]{1,0:T(8,128)(2,1)S(1)}, bf16[512,512]{1,0:T(8,128)(2,1)S(1)}, bf16[512,512]{1,0:T...) fusion(bf16[3,512,512]{2,1,0:T(8,128)(2,1)} %param.6, bf16[3,512,512]{2,1,0:T(8,128)(2,1)} %param.5), kind=kLoop, calls=%fused_computation.55 | loop fusion | bytes 6291456 | tf_op jit(solution)/shard_map/squeeze | solution.py:52
  2.9 0.8 convolution_convert_fusion
  3.7 0.8 convolution_convert_fusion.1
  4.7 3.4 %collective-permute-start = (bf16[3,512,512]{2,1,0:T(8,128)(2,1)S(1)}, bf16[3,512,512]{2,1,0:T(8,128)(2,1)S(1)}, u32[]{:S(2)}, u32[]{:S(2)}) collective-permute-start(bf16[3,512,512]{2,1,0:T(8,128)(2,1)S(1)} %pad_maximum_fusion), channel_id=1, source_target_pairs={{0,1},{1,0},{2,3},{3,2},{4,5},{5,4},{6,7},{7,6},{8,9},{9,8},{10,11... | collective-permute-start | bytes 4718600 | tf_op jit(solution)/shard_map/ppermute | solution.py:12
  8.2 14.8 %collective-permute-start.1 = (bf16[256,512]{1,0:T(8,128)(2,1)S(1)}, bf16[256,512]{1,0:T(8,128)(2,1)S(1)}, u32[]{:S(2)}, u32[]{:S(2)}) collective-permute-start(bf16[256,512]{1,0:T(8,128)(2,1)S(1)} %get-tuple-element.58), channel_id=1, source_target_pairs={{0,16},{1,17},{2,18},{3,19},{4,20},{5,21},{6,22},{7,23},{8,24},{9,... | collective-permute-start | bytes 786440 | tf_op jit(solution)/shard_map/ppermute | solution.py:12
  23.0 1.9 %collective-permute-start.4 = (bf16[256,512]{1,0:T(8,128)(2,1)S(1)}, bf16[256,512]{1,0:T(8,128)(2,1)S(1)}, u32[]{:S(2)}, u32[]{:S(2)}) collective-permute-start(bf16[256,512]{1,0:T(8,128)(2,1)S(1)} %get-tuple-element.57), channel_id=1, source_target_pairs={{0,16},{1,17},{2,18},{3,19},{4,20},{5,21},{6,22},{7,23},{8,24},{9,... | collective-permute-start | bytes 786440 | tf_op jit(solution)/shard_map/ppermute | solution.py:12
  24.9 0.8 convolution_convert_fusion.2
  25.7 0.3 convolution_bitcast_fusion.1
  26.0 0.3 convolution_bitcast_fusion
  26.4 0.4 subtract_convert_fusion.3
  26.8 15.9 %collective-permute-done = bf16[3,512,512]{2,1,0:T(8,128)(2,1)S(1)} collective-permute-done((bf16[3,512,512]{2,1,0:T(8,128)(2,1)S(1)}, bf16[3,512,512]{2,1,0:T(8,128)(2,1)S(1)}, u32[]{:S(2)}, u32[]{:S(2)}) %collective-permute-start) | collective-permute-done | bytes 1572896 | tf_op jit(solution)/shard_map/ppermute | solution.py:12
  42.7 0.4 subtract_convert_fusion.1
  43.2 0.4 subtract_convert_fusion.2
  43.6 0.4 subtract_convert_fusion
  44.1 20.0 %collective-permute-done.1 = bf16[256,512]{1,0:T(8,128)(2,1)S(1)} collective-permute-done((bf16[256,512]{1,0:T(8,128)(2,1)S(1)}, bf16[256,512]{1,0:T(8,128)(2,1)S(1)}, u32[]{:S(2)}, u32[]{:S(2)}) %collective-permute-start.1) | collective-permute-done | bytes 262176 | tf_op jit(solution)/shard_map/ppermute | solution.py:12
  64.0 0.3 fusion.8
  64.4 4.0 %collective-permute-start.2 = (bf16[256,512]{0,1:T(8,128)(2,1)S(1)}, bf16[256,512]{0,1:T(8,128)(2,1)S(1)}, u32[]{:S(2)}, u32[]{:S(2)}) collective-permute-start(bf16[256,512]{0,1:T(8,128)(2,1)S(1)} %fusion.8), channel_id=1, source_target_pairs={{0,257},{1,256},{2,259},{3,258},{4,261},{5,260},{6,263},{7,262},{8... | collective-permute-start | bytes 786440 | tf_op jit(solution)/shard_map/ppermute | solution.py:20
  69.1 0.3 fusion.10
  69.4 3.6 %collective-permute-start.5 = (bf16[256,512]{0,1:T(8,128)(2,1)S(1)}, bf16[256,512]{0,1:T(8,128)(2,1)S(1)}, u32[]{:S(2)}, u32[]{:S(2)}) collective-permute-start(bf16[256,512]{0,1:T(8,128)(2,1)S(1)} %fusion.10), channel_id=1, source_target_pairs={{0,257},{1,256},{2,259},{3,258},{4,261},{5,260},{6,263},{7,262},{8... | collective-permute-start | bytes 786440 | tf_op jit(solution)/shard_map/ppermute | solution.py:20
  73.7 0.4 collective-permute-done.2
  74.4 0.3 convolution_add_fusion.5
  74.8 0.3 fusion.6
  75.1 2.1 %collective-permute-start.3 = (bf16[256,512]{1,0:T(8,128)(2,1)S(1)}, bf16[256,512]{1,0:T(8,128)(2,1)S(1)}, u32[]{:S(2)}, u32[]{:S(2)}) collective-permute-start(bf16[256,512]{1,0:T(8,128)(2,1)S(1)} %fusion.6), channel_id=1, source_target_pairs={{0,1},{1,0},{2,3},{3,2},{4,5},{5,4},{6,7},{7,6},{8,9},{9,8},{10,11... | collective-permute-start | bytes 786440 | tf_op jit(solution)/shard_map/ppermute | solution.py:12
  77.2 2.3 %collective-permute-done.5 = bf16[256,512]{0,1:T(8,128)(2,1)S(1)} collective-permute-done((bf16[256,512]{0,1:T(8,128)(2,1)S(1)}, bf16[256,512]{0,1:T(8,128)(2,1)S(1)}, u32[]{:S(2)}, u32[]{:S(2)}) %collective-permute-start.5) | collective-permute-done | bytes 262176 | tf_op jit(solution)/shard_map/ppermute | solution.py:20
  80.1 0.3 fusion.7
  80.5 1.9 %collective-permute-start.6 = (bf16[256,512]{1,0:T(8,128)(2,1)S(1)}, bf16[256,512]{1,0:T(8,128)(2,1)S(1)}, u32[]{:S(2)}, u32[]{:S(2)}) collective-permute-start(bf16[256,512]{1,0:T(8,128)(2,1)S(1)} %fusion.7), channel_id=1, source_target_pairs={{0,1},{1,0},{2,3},{3,2},{4,5},{5,4},{6,7},{7,6},{8,9},{9,8},{10,11... | collective-permute-start | bytes 786440 | tf_op jit(solution)/shard_map/ppermute | solution.py:12
  82.7 0.3 convolution_add_fusion.7
  83.9 0.3 fusion.9
  84.3 4.7 %collective-permute-done.6 = bf16[256,512]{1,0:T(8,128)(2,1)S(1)} collective-permute-done((bf16[256,512]{1,0:T(8,128)(2,1)S(1)}, bf16[256,512]{1,0:T(8,128)(2,1)S(1)}, u32[]{:S(2)}, u32[]{:S(2)}) %collective-permute-start.6) | collective-permute-done | bytes 262176 | tf_op jit(solution)/shard_map/ppermute | solution.py:12
  89.0 0.3 fusion.11
  89.4 0.8 pad_maximum_fusion.1
  (18 shorter events, 3.7 us)
Async XLA Ops:
  4.5 3.6 %copy-start = (bf16[512,512]{1,0:T(8,128)(2,1)S(1)}, bf16[512,512]{1,0:T(8,128)(2,1)}, u32[]{:S(2)}) copy-start(bf16[512,512]{1,0:T(8,128)(2,1)} %param.4) | copy-start | bytes 1572868
  4.7 38.0 %collective-permute-start = (bf16[3,512,512]{2,1,0:T(8,128)(2,1)S(1)}, bf16[3,512,512]{2,1,0:T(8,128)(2,1)S(1)}, u32[]{:S(2)}, u32[]{:S(2)}) collective-permute-start(bf16[3,512,512]{2,1,0:T(8,128)(2,1)S(1)} %pad_maximum_fusion), channel_id=1, source_target_pairs={{0,1},{1,0},{2,3},{3,2},{4,5},{5,4},{6,7},{7,6},{8,9},{9,8},{10,11... | collective-permute-start | bytes 4718600 | tf_op jit(solution)/shard_map/ppermute | solution.py:12
  8.2 55.9 %collective-permute-start.1 = (bf16[256,512]{1,0:T(8,128)(2,1)S(1)}, bf16[256,512]{1,0:T(8,128)(2,1)S(1)}, u32[]{:S(2)}, u32[]{:S(2)}) collective-permute-start(bf16[256,512]{1,0:T(8,128)(2,1)S(1)} %get-tuple-element.58), channel_id=1, source_target_pairs={{0,16},{1,17},{2,18},{3,19},{4,20},{5,21},{6,22},{7,23},{8,24},{9,... | collective-permute-start | bytes 786440 | tf_op jit(solution)/shard_map/ppermute | solution.py:12
  23.0 46.1 %collective-permute-start.4 = (bf16[256,512]{1,0:T(8,128)(2,1)S(1)}, bf16[256,512]{1,0:T(8,128)(2,1)S(1)}, u32[]{:S(2)}, u32[]{:S(2)}) collective-permute-start(bf16[256,512]{1,0:T(8,128)(2,1)S(1)} %get-tuple-element.57), channel_id=1, source_target_pairs={{0,16},{1,17},{2,18},{3,19},{4,20},{5,21},{6,22},{7,23},{8,24},{9,... | collective-permute-start | bytes 786440 | tf_op jit(solution)/shard_map/ppermute | solution.py:12
  64.4 9.7 %collective-permute-start.2 = (bf16[256,512]{0,1:T(8,128)(2,1)S(1)}, bf16[256,512]{0,1:T(8,128)(2,1)S(1)}, u32[]{:S(2)}, u32[]{:S(2)}) collective-permute-start(bf16[256,512]{0,1:T(8,128)(2,1)S(1)} %fusion.8), channel_id=1, source_target_pairs={{0,257},{1,256},{2,259},{3,258},{4,261},{5,260},{6,263},{7,262},{8... | collective-permute-start | bytes 786440 | tf_op jit(solution)/shard_map/ppermute | solution.py:20
  69.4 10.1 %collective-permute-start.5 = (bf16[256,512]{0,1:T(8,128)(2,1)S(1)}, bf16[256,512]{0,1:T(8,128)(2,1)S(1)}, u32[]{:S(2)}, u32[]{:S(2)}) collective-permute-start(bf16[256,512]{0,1:T(8,128)(2,1)S(1)} %fusion.10), channel_id=1, source_target_pairs={{0,257},{1,256},{2,259},{3,258},{4,261},{5,260},{6,263},{7,262},{8... | collective-permute-start | bytes 786440 | tf_op jit(solution)/shard_map/ppermute | solution.py:20
  75.1 8.8 %collective-permute-start.3 = (bf16[256,512]{1,0:T(8,128)(2,1)S(1)}, bf16[256,512]{1,0:T(8,128)(2,1)S(1)}, u32[]{:S(2)}, u32[]{:S(2)}) collective-permute-start(bf16[256,512]{1,0:T(8,128)(2,1)S(1)} %fusion.6), channel_id=1, source_target_pairs={{0,1},{1,0},{2,3},{3,2},{4,5},{5,4},{6,7},{7,6},{8,9},{9,8},{10,11... | collective-permute-start | bytes 786440 | tf_op jit(solution)/shard_map/ppermute | solution.py:12
  80.5 8.5 %collective-permute-start.6 = (bf16[256,512]{1,0:T(8,128)(2,1)S(1)}, bf16[256,512]{1,0:T(8,128)(2,1)S(1)}, u32[]{:S(2)}, u32[]{:S(2)}) collective-permute-start(bf16[256,512]{1,0:T(8,128)(2,1)S(1)} %fusion.7), channel_id=1, source_target_pairs={{0,1},{1,0},{2,3},{3,2},{4,5},{5,4},{6,7},{7,6},{8,9},{9,8},{10,11... | collective-permute-start | bytes 786440 | tf_op jit(solution)/shard_map/ppermute | solution.py:12

commit v9 on v1

--- a/solution.py
+++ b/solution.py
@@ -10,6 +10,20 @@
     mask = 2**distance
     pairs = [(source, source ^ mask) for source in range(lax.axis_size(axis))]
     return lax.ppermute(value, axis, pairs)
+
+
+def from_diagonal(value, row_bit, col_bit):
+    rows, cols = lax.axis_size("row"), lax.axis_size("col")
+    pairs = [
+        (r * cols + c, (r ^ 2**row_bit) * cols + (c ^ 2**col_bit)) for r in range(rows) for c in range(cols)
+    ]
+    return lax.ppermute(value, ("row", "col"), pairs)
+
+
+def combine(panel, partner, own, cross):
+    total = jnp.dot(panel, own, preferred_element_type=jnp.float32)
+    total = total + jnp.dot(partner, cross, preferred_element_type=jnp.float32)
+    return total.astype(jnp.bfloat16)
 
 
 def permuted_columns(weights, order):
@@ -28,17 +42,20 @@
         both = jnp.concatenate([own_blocks[level], cross_blocks[level]], axis=0)
         both = permuted_columns(both, level_perm[level])
         weights.append((both[:br], both[br:]))
+    (own0, cross0), (own1, cross1), (own2, cross2) = weights
+    z_bit, hi_bit, lo_bit = plan[0][1], plan[1][1], plan[2][1]
+    theirs = from_partner(jnp.stack([own1, cross1]), "col", lo_bit)
     rows = probes.shape[0] // CHUNKS
     outs = []
     for chunk in range(CHUNKS):
         panel = probes[chunk * rows:(chunk + 1) * rows]
-        for level, (axis, bit) in enumerate(plan):
-            own, cross = weights[level]
-            other = from_partner(panel, axis, bit)
-            total = jnp.dot(panel, own, preferred_element_type=jnp.float32)
-            total = total + jnp.dot(other, cross, preferred_element_type=jnp.float32)
-            panel = total.astype(jnp.bfloat16)
-        outs.append(panel)
+        panel = combine(panel, from_partner(panel, "col", z_bit), own0, cross0)
+        far = from_partner(panel, "row", hi_bit)
+        near = from_partner(panel, "col", lo_bit)
+        diag = from_diagonal(panel, hi_bit, lo_bit)
+        mine = combine(panel, far, own1, cross1)
+        partners = combine(near, diag, theirs[0], theirs[1])
+        outs.append(combine(mine, partners, own2, cross2))
     return jnp.concatenate(outs, axis=0)
 
 

time: 86 us -> 107 us (1.24)
  the two profiles are of different devices: /device:TPU:48 before, /device:TPU:36 now
where the time goes in v9:
time: 107 us; the launch traced here: 106 us
  starting transfers between devices  39.5 us (37%)
  waiting for transfers between devices  39.5 us (37%)
  matrix products  18.9 us (18%)
  local copies, waits for them, and re-layouts  4.97 us (5%)
  other arithmetic  2.85 us (3%)
    ppermute x7, waiting for transfers between devices, from_partner(): return lax.ppermute(value, axis, pairs)  39.5 us
    ppermute x7, starting transfers between devices, from_partner(): return lax.ppermute(value, axis, pairs)  34.7 us
    dot_general x6, matrix products, combine(): total = jnp.dot(panel, own, preferred_element_type=jnp.float32)  8.84 us
    dot_general x6, matrix products, combine(): total = total + jnp.dot(partner, cross, preferred_element_type=jnp.float32)  7.82 us
    ppermute x2, starting transfers between devices, from_diagonal(): return lax.ppermute(value, ('row', 'col'), pairs)  4.88 us
    dot_general x3, matrix products, permuted_columns(): jnp.dot(weights, onehot, preferred_element_type=jnp.float32)  2.27 us
  transfers between devices with their start and end apart: 9, of which 3 were waited for; matrix products, arithmetic and copies ran while one was open for 20% of the time, Pallas kernels for 0%

profile of v9, /device:TPU:36, one launch (start us, length us, event | category | flops | bytes accessed | tf_op | source)
XLA Modules:
  0.0 106.0 jit_solution(4889652640278992431)
XLA Ops:
  0.0 1.1 %fusion.47 = (bf16[256,512]{1,0:T(8,128)(2,1)S(1)}, bf16[256,512]{1,0:T(8,128)(2,1)S(1)}) fusion(bf16[512,512]{1,0:T(8,128)(2,1)} %param.4), kind=kLoop, calls=%fused_computation.71 | loop fusion | bytes 1048576 | tf_op jit(solution)/shard_map/slice | solution.py:51
  1.1 14.8 %collective-permute-start = (bf16[256,512]{1,0:T(8,128)(2,1)S(1)}, bf16[256,512]{1,0:T(8,128)(2,1)S(1)}, u32[]{:S(2)}, u32[]{:S(2)}) collective-permute-start(bf16[256,512]{1,0:T(8,128)(2,1)S(1)} %get-tuple-element.13), channel_id=1, source_target_pairs={{0,16},{1,17},{2,18},{3,19},{4,20},{5,21},{6,22},{7,23},{8,24},{9,... | collective-permute-start | bytes 786440 | tf_op jit(solution)/shard_map/ppermute | solution.py:12
  15.9 1.9 %collective-permute-start.5 = (bf16[256,512]{1,0:T(8,128)(2,1)S(1)}, bf16[256,512]{1,0:T(8,128)(2,1)S(1)}, u32[]{:S(2)}, u32[]{:S(2)}) collective-permute-start(bf16[256,512]{1,0:T(8,128)(2,1)S(1)} %get-tuple-element.14), channel_id=1, source_target_pairs={{0,16},{1,17},{2,18},{3,19},{4,20},{5,21},{6,22},{7,23},{8,24},{9,... | collective-permute-start | bytes 786440 | tf_op jit(solution)/shard_map/ppermute | solution.py:12
  17.8 0.8 fusion.48
  18.6 2.0 %slice_bitcast_fusion.2 = (bf16[512,512]{1,0:T(8,128)(2,1)S(1)}, bf16[512,512]{1,0:T(8,128)(2,1)S(1)}, bf16[512,512]{1,0:T(8,128)(2,1)S(1)}, bf16[512,512]{1,0:T...) fusion(bf16[3,512,512]{2,1,0:T(8,128)(2,1)} %param.6, bf16[3,512,512]{2,1,0:T(8,128)(2,1)} %param.5), kind=kLoop, calls=%fused_computation.38 | loop fusion | bytes 6291456 | tf_op jit(solution)/shard_map/squeeze | solution.py:42
  20.7 0.8 convolution_convert_fusion.1
  21.5 1.1 %pad_maximum_fusion = bf16[2,512,512]{2,1,0:T(8,128)(2,1)} fusion(bf16[1,512,512]{2,1,0:T(8,128)(2,1)S(1)} %get-tuple-element.12, bf16[1,512,512]{2,1,0:T(8,128)(2,1)S(1)} %get-tuple-element.11), kind=kLoop, calls=%fused_computation.30 | loop fusion | flops 524288 | bytes 2097152 | tf_op jit(solution)/shard_map/stack | solution.py:47
  22.6 3.1 %collective-permute-start.3 = (bf16[2,512,512]{2,1,0:T(8,128)(2,1)}, bf16[2,512,512]{2,1,0:T(8,128)(2,1)S(1)}, u32[]{:S(2)}, u32[]{:S(2)}) collective-permute-start(bf16[2,512,512]{2,1,0:T(8,128)(2,1)} %pad_maximum_fusion), channel_id=1, source_target_pairs={{0,1},{1,0},{2,3},{3,2},{4,5},{5,4},{6,7},{7,6},{8,9},{9,8},{10,11... | collective-permute-start | bytes 3145736 | tf_op jit(solution)/shard_map/ppermute | solution.py:12
  25.7 0.8 convolution_convert_fusion.2
  27.1 0.8 convolution_convert_fusion
  27.9 0.3 fusion.32
  28.2 33.7 %collective-permute-done.5 = bf16[256,512]{1,0:T(8,128)(2,1)S(1)} collective-permute-done((bf16[256,512]{1,0:T(8,128)(2,1)S(1)}, bf16[256,512]{1,0:T(8,128)(2,1)S(1)}, u32[]{:S(2)}, u32[]{:S(2)}) %collective-permute-start.5) | collective-permute-done | bytes 262176 | tf_op jit(solution)/shard_map/ppermute | solution.py:12
  61.9 0.3 fusion.4
  62.3 2.4 %collective-permute-start.8 = (bf16[256,512]{0,1:T(8,128)(2,1)S(1)}, bf16[256,512]{0,1:T(8,128)(2,1)}, u32[]{:S(2)}, u32[]{:S(2)}) collective-permute-start(bf16[256,512]{0,1:T(8,128)(2,1)S(1)} %bitcast.41), channel_id=1, source_target_pairs={{0,257},{1,256},{2,259},{3,258},{4,261},{5,260},{6,263},{7,262},{8... | collective-permute-start | bytes 786440 | tf_op jit(solution)/shard_map/ppermute | solution.py:20
  64.7 3.0 %collective-permute-start.7 = (bf16[256,512]{0,1:T(8,128)(2,1)S(1)}, bf16[256,512]{0,1:T(8,128)(2,1)}, u32[]{:S(2)}, u32[]{:S(2)}) collective-permute-start(bf16[256,512]{0,1:T(8,128)(2,1)S(1)} %bitcast.42), channel_id=1, source_target_pairs={{0,1},{1,0},{2,3},{3,2},{4,5},{5,4},{6,7},{7,6},{8,9},{9,8},{10,11... | collective-permute-start | bytes 786440 | tf_op jit(solution)/shard_map/ppermute | solution.py:12
  67.8 3.7 %collective-permute-start.6 = (bf16[256,512]{0,1:T(8,128)(2,1)S(1)}, bf16[256,512]{0,1:T(8,128)(2,1)S(1)}, u32[]{:S(2)}, u32[]{:S(2)}) collective-permute-start(bf16[256,512]{0,1:T(8,128)(2,1)S(1)} %bitcast.43), channel_id=1, source_target_pairs={{0,256},{32,288},{64,320},{96,352},{128,384},{160,416},{192,448},{... | collective-permute-start | bytes 786440 | tf_op jit(solution)/shard_map/ppermute | solution.py:12
  71.5 1.1 fusion
  72.6 1.1 %fusion.38 = f32[256,512]{1,0:T(8,128)} fusion(bf16[512,256]{1,0:T(8,128)(2,1)S(1)} %fusion.4, bf16[1024,512]{1,0:T(8,128)(2,1)S(1)} %convolution_convert_fusion.1), kind=kOutput, calls=%fused_computation.61 | convolution fusion | flops 134217728 | bytes 1310720 | tf_op jit(solution)/shard_map/dot_general | solution.py:24
  73.7 2.4 %collective-permute-start.4 = (bf16[256,512]{0,1:T(8,128)(2,1)}, bf16[256,512]{0,1:T(8,128)(2,1)}, u32[]{:S(2)}, u32[]{:S(2)}) collective-permute-start(bf16[256,512]{0,1:T(8,128)(2,1)} %bitcast.6), channel_id=1, source_target_pairs={{0,257},{1,256},{2,259},{3,258},{4,261},{5,260},{6,263},{7,262},{8... | collective-permute-start | bytes 786440 | tf_op jit(solution)/shard_map/ppermute | solution.py:20
  76.1 2.1 %fusion.40 = f32[256,512]{1,0:T(8,128)} fusion(bf16[512,256]{1,0:T(8,128)(2,1)} %fusion, bf16[1024,512]{1,0:T(8,128)(2,1)S(1)} %convolution_convert_fusion.1), kind=kOutput, calls=%fused_computation.64 | convolution fusion | flops 134217728 | bytes 1310720 | tf_op jit(solution)/shard_map/dot_general | solution.py:24
  78.2 2.0 %collective-permute-done.6 = bf16[256,512]{0,1:T(8,128)(2,1)S(1)} collective-permute-done((bf16[256,512]{0,1:T(8,128)(2,1)S(1)}, bf16[256,512]{0,1:T(8,128)(2,1)S(1)}, u32[]{:S(2)}, u32[]{:S(2)}) %collective-permute-start.6) | collective-permute-done | bytes 262176 | tf_op jit(solution)/shard_map/ppermute | solution.py:12
  80.2 0.7 copy-done.2
  80.9 3.8 %collective-permute-start.1 = (bf16[256,512]{0,1:T(8,128)(2,1)}, bf16[256,512]{0,1:T(8,128)(2,1)}, u32[]{:S(2)}, u32[]{:S(2)}) collective-permute-start(bf16[256,512]{0,1:T(8,128)(2,1)} %bitcast.6), channel_id=1, source_target_pairs={{0,256},{32,288},{64,320},{96,352},{128,384},{160,416},{192,448},{... | collective-permute-start | bytes 786440 | tf_op jit(solution)/shard_map/ppermute | solution.py:12
  84.8 2.5 %fusion.8 = f32[256,512]{1,0:T(8,128)} fusion(f32[256,512]{1,0:T(8,128)} %fusion.38, bf16[256,512]{0,1:T(8,128)(2,1)} %copy-done.2, bf16[1024,512]{1,0:T(8,128)(2,1)S(1)} %convolution_convert_fusion, bf16[1024,512]{1,0:T(8,128)(2,1)S(1)} %convolution_convert_fusion.1), kind=kOutput, calls=%fused_computation.19 | convolution fusion | flops 268697600 | bytes 2359296 | tf_op jit(solution)/shard_map/dot_general | solution.py:24
  87.3 3.8 %collective-permute-done.1 = bf16[256,512]{0,1:T(8,128)(2,1)} collective-permute-done((bf16[256,512]{0,1:T(8,128)(2,1)}, bf16[256,512]{0,1:T(8,128)(2,1)}, u32[]{:S(2)}, u32[]{:S(2)}) %collective-permute-start.1) | collective-permute-done | bytes 262176 | tf_op jit(solution)/shard_map/ppermute | solution.py:12
  91.0 4.2 %collective-permute-start.2 = (bf16[256,512]{0,1:T(8,128)(2,1)}, bf16[256,512]{0,1:T(8,128)(2,1)}, u32[]{:S(2)}, u32[]{:S(2)}) collective-permute-start(bf16[256,512]{0,1:T(8,128)(2,1)} %bitcast.6), channel_id=1, source_target_pairs={{0,1},{1,0},{2,3},{3,2},{4,5},{5,4},{6,7},{7,6},{8,9},{9,8},{10,11... | collective-permute-start | bytes 786440 | tf_op jit(solution)/shard_map/ppermute | solution.py:12
  95.3 2.5 %fusion.9 = f32[256,512]{1,0:T(8,128)} fusion(f32[256,512]{1,0:T(8,128)} %fusion.40, bf16[256,512]{0,1:T(8,128)(2,1)} %collective-permute-done.1, bf16[1024,512]{1,0:T(8,128)(2,1)S(1)} %convolution_convert_fusion, bf16[1024,512]{1,0:T(8,128)(2,1)S(1)} %convolution_convert_fusion.1), kind=kOutput, calls=%fused_computation.20 | convolution fusion | flops 268697600 | bytes 2359296 | tf_op jit(solution)/shard_map/dot_general | solution.py:24
  97.7 1.3 %fusion.22 = f32[256,512]{1,0:T(8,128)S(1)} fusion(bf16[256,512]{0,1:T(8,128)(2,1)} %collective-permute-done.8, bf16[2,512,512]{2,1,0:T(8,128)(2,1)S(1)} %collective-permute-done.3), kind=kOutput, calls=%fused_computation.46 | convolution fusion | flops 134217728 | bytes 1310720 | tf_op jit(solution)/shard_map/dot_general | solution.py:25
  99.0 1.7 %fusion.7 = bf16[256,512]{1,0:T(8,128)(2,1)S(1)} fusion(f32[256,512]{1,0:T(8,128)} %fusion.8, f32[256,512]{1,0:T(8,128)S(1)} %fusion.22, bf16[256,512]{0,1:T(8,128)(2,1)} %collective-permute-done.7, bf16[2,512,512]{2,1,0:T(8,128)(2,1)S(1)} %collective-permute-done.3, bf16[1024,512]{1,0:T(8,128)(2,1)S(1)} %convolution_convert_fusion), kind=kOutput, calls=%fused_computation.18 | convolution fusion | flops 268959744 | bytes 2621440 | tf_op jit(solution)/shard_map/dot_general | solution.py:25
  100.7 1.3 %fusion.23 = f32[256,512]{1,0:T(8,128)S(1)} fusion(bf16[256,512]{0,1:T(8,128)(2,1)} %collective-permute-done.4, bf16[2,512,512]{2,1,0:T(8,128)(2,1)S(1)} %collective-permute-done.3), kind=kOutput, calls=%fused_computation.47 | convolution fusion | flops 134217728 | bytes 1310720 | tf_op jit(solution)/shard_map/dot_general | solution.py:25
  102.0 2.2 %fusion.3 = bf16[256,512]{1,0:T(8,128)(2,1)} fusion(f32[256,512]{1,0:T(8,128)S(1)} %copy-done.1, f32[256,512]{1,0:T(8,128)S(1)} %fusion.23, bf16[256,512]{0,1:T(8,128)(2,1)} %collective-permute-done.2, bf16[2,512,512]{2,1,0:T(8,128)(2,1)S(1)} %collective-permute-done.3, bf16[1024,512]{1,0:T(8,128)(2,1)S(1)} %convolution_convert_fusion), kind=kOutput, calls=%fused_computation.14 | convolution fusion | flops 268959744 | bytes 2621440 | tf_op jit(solution)/shard_map/dot_general | solution.py:25
  104.2 1.8 %pad_maximum_fusion.1 = bf16[512,512]{1,0:T(8,128)(2,1)} fusion(bf16[256,512]{1,0:T(8,128)(2,1)S(1)} %fusion.7, bf16[256,512]{1,0:T(8,128)(2,1)} %fusion.3), kind=kLoop, calls=%fused_computation.36 | loop fusion | flops 1048576 | bytes 1048576 | tf_op jit(solution)/shard_map/concatenate | solution.py:59
  (13 shorter events, 0.7 us)
Async XLA Ops:
  1.1 70.4 %collective-permute-start = (bf16[256,512]{1,0:T(8,128)(2,1)S(1)}, bf16[256,512]{1,0:T(8,128)(2,1)S(1)}, u32[]{:S(2)}, u32[]{:S(2)}) collective-permute-start(bf16[256,512]{1,0:T(8,128)(2,1)S(1)} %get-tuple-element.13), channel_id=1, source_target_pairs={{0,16},{1,17},{2,18},{3,19},{4,20},{5,21},{6,22},{7,23},{8,24},{9,... | collective-permute-start | bytes 786440 | tf_op jit(solution)/shard_map/ppermute | solution.py:12
  15.9 46.0 %collective-permute-start.5 = (bf16[256,512]{1,0:T(8,128)(2,1)S(1)}, bf16[256,512]{1,0:T(8,128)(2,1)S(1)}, u32[]{:S(2)}, u32[]{:S(2)}) collective-permute-start(bf16[256,512]{1,0:T(8,128)(2,1)S(1)} %get-tuple-element.14), channel_id=1, source_target_pairs={{0,16},{1,17},{2,18},{3,19},{4,20},{5,21},{6,22},{7,23},{8,24},{9,... | collective-permute-start | bytes 786440 | tf_op jit(solution)/shard_map/ppermute | solution.py:12
  22.6 75.1 %collective-permute-start.3 = (bf16[2,512,512]{2,1,0:T(8,128)(2,1)}, bf16[2,512,512]{2,1,0:T(8,128)(2,1)S(1)}, u32[]{:S(2)}, u32[]{:S(2)}) collective-permute-start(bf16[2,512,512]{2,1,0:T(8,128)(2,1)} %pad_maximum_fusion), channel_id=1, source_target_pairs={{0,1},{1,0},{2,3},{3,2},{4,5},{5,4},{6,7},{7,6},{8,9},{9,8},{10,11... | collective-permute-start | bytes 3145736 | tf_op jit(solution)/shard_map/ppermute | solution.py:12
  25.7 1.0 copy-start
  62.3 35.5 %collective-permute-start.8 = (bf16[256,512]{0,1:T(8,128)(2,1)S(1)}, bf16[256,512]{0,1:T(8,128)(2,1)}, u32[]{:S(2)}, u32[]{:S(2)}) collective-permute-start(bf16[256,512]{0,1:T(8,128)(2,1)S(1)} %bitcast.41), channel_id=1, source_target_pairs={{0,257},{1,256},{2,259},{3,258},{4,261},{5,260},{6,263},{7,262},{8... | collective-permute-start | bytes 786440 | tf_op jit(solution)/shard_map/ppermute | solution.py:20
  64.7 34.3 %collective-permute-start.7 = (bf16[256,512]{0,1:T(8,128)(2,1)S(1)}, bf16[256,512]{0,1:T(8,128)(2,1)}, u32[]{:S(2)}, u32[]{:S(2)}) collective-permute-start(bf16[256,512]{0,1:T(8,128)(2,1)S(1)} %bitcast.42), channel_id=1, source_target_pairs={{0,1},{1,0},{2,3},{3,2},{4,5},{5,4},{6,7},{7,6},{8,9},{9,8},{10,11... | collective-permute-start | bytes 786440 | tf_op jit(solution)/shard_map/ppermute | solution.py:12
  67.8 12.5 %collective-permute-start.6 = (bf16[256,512]{0,1:T(8,128)(2,1)S(1)}, bf16[256,512]{0,1:T(8,128)(2,1)S(1)}, u32[]{:S(2)}, u32[]{:S(2)}) collective-permute-start(bf16[256,512]{0,1:T(8,128)(2,1)S(1)} %bitcast.43), channel_id=1, source_target_pairs={{0,256},{32,288},{64,320},{96,352},{128,384},{160,416},{192,448},{... | collective-permute-start | bytes 786440 | tf_op jit(solution)/shard_map/ppermute | solution.py:12
  73.7 27.1 %collective-permute-start.4 = (bf16[256,512]{0,1:T(8,128)(2,1)}, bf16[256,512]{0,1:T(8,128)(2,1)}, u32[]{:S(2)}, u32[]{:S(2)}) collective-permute-start(bf16[256,512]{0,1:T(8,128)(2,1)} %bitcast.6), channel_id=1, source_target_pairs={{0,257},{1,256},{2,259},{3,258},{4,261},{5,260},{6,263},{7,262},{8... | collective-permute-start | bytes 786440 | tf_op jit(solution)/shard_map/ppermute | solution.py:20
  80.2 0.7 copy-start.2
  80.9 10.1 %collective-permute-start.1 = (bf16[256,512]{0,1:T(8,128)(2,1)}, bf16[256,512]{0,1:T(8,128)(2,1)}, u32[]{:S(2)}, u32[]{:S(2)}) collective-permute-start(bf16[256,512]{0,1:T(8,128)(2,1)} %bitcast.6), channel_id=1, source_target_pairs={{0,256},{32,288},{64,320},{96,352},{128,384},{160,416},{192,448},{... | collective-permute-start | bytes 786440 | tf_op jit(solution)/shard_map/ppermute | solution.py:12
  91.0 11.0 %collective-permute-start.2 = (bf16[256,512]{0,1:T(8,128)(2,1)}, bf16[256,512]{0,1:T(8,128)(2,1)}, u32[]{:S(2)}, u32[]{:S(2)}) collective-permute-start(bf16[256,512]{0,1:T(8,128)(2,1)} %bitcast.6), channel_id=1, source_target_pairs={{0,1},{1,0},{2,3},{3,2},{4,5},{5,4},{6,7},{7,6},{8,9},{9,8},{10,11... | collective-permute-start | bytes 786440 | tf_op jit(solution)/shard_map/ppermute | solution.py:12
  99.0 3.0 %copy-start.1 = (f32[256,512]{1,0:T(8,128)S(1)}, f32[256,512]{1,0:T(8,128)}, u32[]{:S(2)}) copy-start(f32[256,512]{1,0:T(8,128)} %fusion.9) | copy-start | bytes 1572868

commit v10 on v1

--- a/solution.py
+++ b/solution.py
@@ -30,8 +30,10 @@
         weights.append((both[:br], both[br:]))
     rows = probes.shape[0] // CHUNKS
     outs = []
+    source = probes
     for chunk in range(CHUNKS):
-        panel = probes[chunk * rows:(chunk + 1) * rows]
+        panel = source[chunk * rows:(chunk + 1) * rows]
+        panel, source = lax.optimization_barrier((panel, source))
         for level, (axis, bit) in enumerate(plan):
             own, cross = weights[level]
             other = from_partner(panel, axis, bit)

time: 86 us -> 85.9 us (level)
    slice x1 -> x2, local copies, waits for them, and re-layouts: 1.06 us -> 1.94 us  [per_device(): panel = source[chunk * rows:(chunk + 1) * rows]]
  transfers between devices with their start and end apart: 6 -> 6, of which waited for: 4 -> 4; matrix products, arithmetic and copies ran while one was open for 10% -> 11% of each run, Pallas kernels for 0% -> 0%
where the time goes in v10:
time: 85.9 us; the launch traced here: 85.5 us
  waiting for transfers between devices  40.9 us (48%)
  starting transfers between devices  32.9 us (38%)
  matrix products  5.83 us (7%)
  local copies, waits for them, and re-layouts  4.79 us (6%)
    ppermute x6, waiting for transfers between devices, from_partner(): return lax.ppermute(value, axis, pairs)  40.9 us
    ppermute x6, starting transfers between devices, from_partner(): return lax.ppermute(value, axis, pairs)  32.9 us
    dot_general x3, matrix products, permuted_columns(): jnp.dot(weights, onehot, preferred_element_type=jnp.float32)  2.28 us
    squeeze x1, local copies, waits for them, and re-layouts, per_device(): both = jnp.concatenate([own_blocks[level], cross_blocks[level]], axis=0)  2.03 us
    slice x2, local copies, waits for them, and re-layouts, per_device(): panel = source[chunk * rows:(chunk + 1) * rows]  1.94 us
    dot_general x6, matrix products, per_device(): total = total + jnp.dot(other, cross, preferred_element_type=jnp.float32)  1.79 us
    dot_general x6, matrix products, per_device(): total = jnp.dot(panel, own, preferred_element_type=jnp.float32)  1.76 us
  transfers between devices with their start and end apart: 6, of which 4 were waited for; matrix products, arithmetic and copies ran while one was open for 11% of the time, Pallas kernels for 0%

profile of v10, /device:TPU:48, one launch (start us, length us, event | category | flops | bytes accessed | tf_op | source)
XLA Modules:
  0.0 85.5 jit_solution(8868003925369351135)
XLA Ops:
  0.0 1.0 %slice.51 = bf16[256,512]{1,0:T(8,128)(2,1)S(1)} slice(bf16[512,512]{1,0:T(8,128)(2,1)} %param.4), slice={[0:256], [0:512]} | slice | bytes 524288 | tf_op jit(solution)/shard_map/slice | solution.py:35
  1.0 14.8 %collective-permute-start = (bf16[256,512]{1,0:T(8,128)(2,1)S(1)}, bf16[256,512]{1,0:T(8,128)(2,1)S(1)}, u32[]{:S(2)}, u32[]{:S(2)}) collective-permute-start(bf16[256,512]{1,0:T(8,128)(2,1)S(1)} %slice.51), channel_id=1, source_target_pairs={{0,16},{1,17},{2,18},{3,19},{4,20},{5,21},{6,22},{7,23},{8,24},{9,... | collective-permute-start | bytes 786440 | tf_op jit(solution)/shard_map/ppermute | solution.py:12
  15.8 1.0 %slice.67 = bf16[256,512]{1,0:T(8,128)(2,1)S(1)} slice(bf16[512,512]{1,0:T(8,128)(2,1)} %param.4), slice={[256:512], [0:512]} | slice | bytes 524288 | tf_op jit(solution)/shard_map/slice | solution.py:35
  16.8 1.9 %collective-permute-start.3 = (bf16[256,512]{1,0:T(8,128)(2,1)S(1)}, bf16[256,512]{1,0:T(8,128)(2,1)S(1)}, u32[]{:S(2)}, u32[]{:S(2)}) collective-permute-start(bf16[256,512]{1,0:T(8,128)(2,1)S(1)} %slice.67), channel_id=1, source_target_pairs={{0,16},{1,17},{2,18},{3,19},{4,20},{5,21},{6,22},{7,23},{8,24},{9,... | collective-permute-start | bytes 786440 | tf_op jit(solution)/shard_map/ppermute | solution.py:12
  18.7 0.8 fusion.39
  19.5 2.0 %slice_bitcast_fusion = (bf16[512,512]{1,0:T(8,128)(2,1)S(1)}, bf16[512,512]{1,0:T(8,128)(2,1)S(1)}, bf16[512,512]{1,0:T(8,128)(2,1)S(1)}, bf16[512,512]{1,0:T(8...) fusion(bf16[3,512,512]{2,1,0:T(8,128)(2,1)} %param.6, bf16[3,512,512]{2,1,0:T(8,128)(2,1)} %param.5), kind=kLoop, calls=%fused_computation.29 | loop fusion | bytes 6291456 | tf_op jit(solution)/shard_map/squeeze | solution.py:28
  21.6 0.8 convolution_convert_fusion.2
  22.3 0.3 fusion.34
  22.6 0.8 convolution_convert_fusion.1
  23.4 0.8 convolution_convert_fusion
  24.2 0.3 fusion.32
  24.5 32.5 %collective-permute-done = bf16[256,512]{1,0:T(8,128)(2,1)S(1)} collective-permute-done((bf16[256,512]{1,0:T(8,128)(2,1)S(1)}, bf16[256,512]{1,0:T(8,128)(2,1)S(1)}, u32[]{:S(2)}, u32[]{:S(2)}) %collective-permute-start) | collective-permute-done | bytes 262176 | tf_op jit(solution)/shard_map/ppermute | solution.py:12
  56.9 0.3 fusion
  57.2 4.9 %collective-permute-start.1 = (bf16[256,512]{1,0:T(8,128)(2,1)S(1)}, bf16[256,512]{1,0:T(8,128)(2,1)S(1)}, u32[]{:S(2)}, u32[]{:S(2)}) collective-permute-start(bf16[256,512]{1,0:T(8,128)(2,1)S(1)} %fusion), channel_id=1, source_target_pairs={{0,256},{32,288},{64,320},{96,352},{128,384},{160,416},{192,448},{... | collective-permute-start | bytes 786440 | tf_op jit(solution)/shard_map/ppermute | solution.py:12
  62.2 0.0 collective-permute-done.3
  62.2 0.3 fusion.3
  62.5 0.3 fusion.28
  62.8 4.4 %collective-permute-start.4 = (bf16[256,512]{1,0:T(8,128)(2,1)S(1)}, bf16[256,512]{1,0:T(8,128)(2,1)S(1)}, u32[]{:S(2)}, u32[]{:S(2)}) collective-permute-start(bf16[256,512]{1,0:T(8,128)(2,1)S(1)} %fusion.3), channel_id=1, source_target_pairs={{0,256},{32,288},{64,320},{96,352},{128,384},{160,416},{192,448},{... | collective-permute-start | bytes 786440 | tf_op jit(solution)/shard_map/ppermute | solution.py:12
  67.2 0.3 fusion.26
  67.5 0.0 collective-permute-done.1
  67.5 0.3 fusion.1
  67.8 2.8 %collective-permute-start.2 = (bf16[256,512]{1,0:T(8,128)(2,1)S(1)}, bf16[256,512]{1,0:T(8,128)(2,1)S(1)}, u32[]{:S(2)}, u32[]{:S(2)}) collective-permute-start(bf16[256,512]{1,0:T(8,128)(2,1)S(1)} %fusion.1), channel_id=1, source_target_pairs={{0,1},{1,0},{2,3},{3,2},{4,5},{5,4},{6,7},{7,6},{8,9},{9,8},{10,11... | collective-permute-start | bytes 786440 | tf_op jit(solution)/shard_map/ppermute | solution.py:12
  70.7 3.6 %collective-permute-done.4 = bf16[256,512]{1,0:T(8,128)(2,1)S(1)} collective-permute-done((bf16[256,512]{1,0:T(8,128)(2,1)S(1)}, bf16[256,512]{1,0:T(8,128)(2,1)S(1)}, u32[]{:S(2)}, u32[]{:S(2)}) %collective-permute-start.4) | collective-permute-done | bytes 262176 | tf_op jit(solution)/shard_map/ppermute | solution.py:12
  74.3 0.3 fusion.4
  74.6 0.3 fusion.22
  74.9 4.0 %collective-permute-start.5 = (bf16[256,512]{1,0:T(8,128)(2,1)S(1)}, bf16[256,512]{1,0:T(8,128)(2,1)S(1)}, u32[]{:S(2)}, u32[]{:S(2)}) collective-permute-start(bf16[256,512]{1,0:T(8,128)(2,1)S(1)} %fusion.4), channel_id=1, source_target_pairs={{0,1},{1,0},{2,3},{3,2},{4,5},{5,4},{6,7},{7,6},{8,9},{9,8},{10,11... | collective-permute-start | bytes 786440 | tf_op jit(solution)/shard_map/ppermute | solution.py:12
  78.9 0.3 fusion.20
  79.2 1.4 %collective-permute-done.2 = bf16[256,512]{1,0:T(8,128)(2,1)S(1)} collective-permute-done((bf16[256,512]{1,0:T(8,128)(2,1)S(1)}, bf16[256,512]{1,0:T(8,128)(2,1)S(1)}, u32[]{:S(2)}, u32[]{:S(2)}) %collective-permute-start.2) | collective-permute-done | bytes 262176 | tf_op jit(solution)/shard_map/ppermute | solution.py:12
  80.6 0.3 fusion.2
  80.9 3.5 %collective-permute-done.5 = bf16[256,512]{1,0:T(8,128)(2,1)S(1)} collective-permute-done((bf16[256,512]{1,0:T(8,128)(2,1)S(1)}, bf16[256,512]{1,0:T(8,128)(2,1)S(1)}, u32[]{:S(2)}, u32[]{:S(2)}) %collective-permute-start.5) | collective-permute-done | bytes 262176 | tf_op jit(solution)/shard_map/ppermute | solution.py:12
  84.4 0.3 fusion.5
  84.7 0.8 pad_maximum_fusion
Async XLA Ops:
  1.0 55.9 %collective-permute-start = (bf16[256,512]{1,0:T(8,128)(2,1)S(1)}, bf16[256,512]{1,0:T(8,128)(2,1)S(1)}, u32[]{:S(2)}, u32[]{:S(2)}) collective-permute-start(bf16[256,512]{1,0:T(8,128)(2,1)S(1)} %slice.51), channel_id=1, source_target_pairs={{0,16},{1,17},{2,18},{3,19},{4,20},{5,21},{6,22},{7,23},{8,24},{9,... | collective-permute-start | bytes 786440 | tf_op jit(solution)/shard_map/ppermute | solution.py:12
  16.8 45.4 %collective-permute-start.3 = (bf16[256,512]{1,0:T(8,128)(2,1)S(1)}, bf16[256,512]{1,0:T(8,128)(2,1)S(1)}, u32[]{:S(2)}, u32[]{:S(2)}) collective-permute-start(bf16[256,512]{1,0:T(8,128)(2,1)S(1)} %slice.67), channel_id=1, source_target_pairs={{0,16},{1,17},{2,18},{3,19},{4,20},{5,21},{6,22},{7,23},{8,24},{9,... | collective-permute-start | bytes 786440 | tf_op jit(solution)/shard_map/ppermute | solution.py:12
  57.2 10.3 %collective-permute-start.1 = (bf16[256,512]{1,0:T(8,128)(2,1)S(1)}, bf16[256,512]{1,0:T(8,128)(2,1)S(1)}, u32[]{:S(2)}, u32[]{:S(2)}) collective-permute-start(bf16[256,512]{1,0:T(8,128)(2,1)S(1)} %fusion), channel_id=1, source_target_pairs={{0,256},{32,288},{64,320},{96,352},{128,384},{160,416},{192,448},{... | collective-permute-start | bytes 786440 | tf_op jit(solution)/shard_map/ppermute | solution.py:12
  62.8 11.5 %collective-permute-start.4 = (bf16[256,512]{1,0:T(8,128)(2,1)S(1)}, bf16[256,512]{1,0:T(8,128)(2,1)S(1)}, u32[]{:S(2)}, u32[]{:S(2)}) collective-permute-start(bf16[256,512]{1,0:T(8,128)(2,1)S(1)} %fusion.3), channel_id=1, source_target_pairs={{0,256},{32,288},{64,320},{96,352},{128,384},{160,416},{192,448},{... | collective-permute-start | bytes 786440 | tf_op jit(solution)/shard_map/ppermute | solution.py:12
  67.8 12.7 %collective-permute-start.2 = (bf16[256,512]{1,0:T(8,128)(2,1)S(1)}, bf16[256,512]{1,0:T(8,128)(2,1)S(1)}, u32[]{:S(2)}, u32[]{:S(2)}) collective-permute-start(bf16[256,512]{1,0:T(8,128)(2,1)S(1)} %fusion.1), channel_id=1, source_target_pairs={{0,1},{1,0},{2,3},{3,2},{4,5},{5,4},{6,7},{7,6},{8,9},{9,8},{10,11... | collective-permute-start | bytes 786440 | tf_op jit(solution)/shard_map/ppermute | solution.py:12
  74.9 9.4 %collective-permute-start.5 = (bf16[256,512]{1,0:T(8,128)(2,1)S(1)}, bf16[256,512]{1,0:T(8,128)(2,1)S(1)}, u32[]{:S(2)}, u32[]{:S(2)}) collective-permute-start(bf16[256,512]{1,0:T(8,128)(2,1)S(1)} %fusion.4), channel_id=1, source_target_pairs={{0,1},{1,0},{2,3},{3,2},{4,5},{5,4},{6,7},{7,6},{8,9},{9,8},{10,11... | collective-permute-start | bytes 786440 | tf_op jit(solution)/shard_map/ppermute | solution.py:12

commit v11 on v10

--- a/solution.py
+++ b/solution.py
@@ -41,7 +41,12 @@
             total = total + jnp.dot(other, cross, preferred_element_type=jnp.float32)
             panel = total.astype(jnp.bfloat16)
         outs.append(panel)
-    return jnp.concatenate(outs, axis=0)
+    result = jnp.zeros(probes.shape, probes.dtype)
+    for chunk, panel in enumerate(outs):
+        result = lax.dynamic_update_slice(result, panel, (chunk * rows, 0))
+        if chunk + 1 < CHUNKS:
+            result = lax.optimization_barrier(result)
+    return result
 
 
 def solution(mesh):

time: 85.9 us -> 85.7 us (level)
  transfers between devices with their start and end apart: 6 -> 6, of which waited for: 4 -> 4; matrix products, arithmetic and copies ran while one was open for 11% -> 12% of each run, Pallas kernels for 0% -> 0%
where the time goes in v11:
time: 85.7 us; the launch traced here: 85.4 us
  waiting for transfers between devices  40.1 us (47%)
  starting transfers between devices  32.9 us (38%)
  matrix products  6.54 us (8%)
  local copies, waits for them, and re-layouts  5.62 us (7%)
    ppermute x6, waiting for transfers between devices, from_partner(): return lax.ppermute(value, axis, pairs)  40.1 us
    ppermute x6, starting transfers between devices, from_partner(): return lax.ppermute(value, axis, pairs)  32.9 us
    dot_general x6, matrix products, per_device(): total = total + jnp.dot(other, cross, preferred_element_type=jnp.float32)  2.5 us
    dot_general x3, matrix products, permuted_columns(): jnp.dot(weights, onehot, preferred_element_type=jnp.float32)  2.28 us
    squeeze x1, local copies, waits for them, and re-layouts, per_device(): both = jnp.concatenate([own_blocks[level], cross_blocks[level]], axis=0)  2.03 us
    slice x2, local copies, waits for them, and re-layouts, per_device(): panel = source[chunk * rows:(chunk + 1) * rows]  1.94 us
    dot_general x6, matrix products, per_device(): total = jnp.dot(panel, own, preferred_element_type=jnp.float32)  1.76 us
  transfers between devices with their start and end apart: 6, of which 4 were waited for; matrix products, arithmetic and copies ran while one was open for 12% of the time, Pallas kernels for 0%

profile of v11, /device:TPU:48, one launch (start us, length us, event | category | flops | bytes accessed | tf_op | source)
XLA Modules:
  0.0 85.4 jit_solution(15009488183506129299)
XLA Ops:
  0.0 1.0 %slice.51 = bf16[256,512]{1,0:T(8,128)(2,1)S(1)} slice(bf16[512,512]{1,0:T(8,128)(2,1)} %param.4), slice={[0:256], [0:512]} | slice | bytes 524288 | tf_op jit(solution)/shard_map/slice | solution.py:35
  1.0 14.8 %collective-permute-start = (bf16[256,512]{1,0:T(8,128)(2,1)S(1)}, bf16[256,512]{1,0:T(8,128)(2,1)S(1)}, u32[]{:S(2)}, u32[]{:S(2)}) collective-permute-start(bf16[256,512]{1,0:T(8,128)(2,1)S(1)} %slice.51), channel_id=1, source_target_pairs={{0,16},{1,17},{2,18},{3,19},{4,20},{5,21},{6,22},{7,23},{8,24},{9,... | collective-permute-start | bytes 786440 | tf_op jit(solution)/shard_map/ppermute | solution.py:12
  15.8 1.0 %slice.67 = bf16[256,512]{1,0:T(8,128)(2,1)S(1)} slice(bf16[512,512]{1,0:T(8,128)(2,1)} %param.4), slice={[256:512], [0:512]} | slice | bytes 524288 | tf_op jit(solution)/shard_map/slice | solution.py:35
  16.8 1.9 %collective-permute-start.3 = (bf16[256,512]{1,0:T(8,128)(2,1)S(1)}, bf16[256,512]{1,0:T(8,128)(2,1)S(1)}, u32[]{:S(2)}, u32[]{:S(2)}) collective-permute-start(bf16[256,512]{1,0:T(8,128)(2,1)S(1)} %slice.67), channel_id=1, source_target_pairs={{0,16},{1,17},{2,18},{3,19},{4,20},{5,21},{6,22},{7,23},{8,24},{9,... | collective-permute-start | bytes 786440 | tf_op jit(solution)/shard_map/ppermute | solution.py:12
  18.7 0.8 fusion.40
  19.5 2.0 %slice_bitcast_fusion = (bf16[512,512]{1,0:T(8,128)(2,1)S(1)}, bf16[512,512]{1,0:T(8,128)(2,1)S(1)}, bf16[512,512]{1,0:T(8,128)(2,1)S(1)}, bf16[512,512]{1,0:T(8...) fusion(bf16[3,512,512]{2,1,0:T(8,128)(2,1)} %param.6, bf16[3,512,512]{2,1,0:T(8,128)(2,1)} %param.5), kind=kLoop, calls=%fused_computation.29 | loop fusion | bytes 6291456 | tf_op jit(solution)/shard_map/squeeze | solution.py:28
  21.6 0.8 convolution_convert_fusion.2
  22.3 0.3 fusion.35
  22.6 0.8 convolution_convert_fusion.1
  23.4 0.8 convolution_convert_fusion
  24.2 0.3 fusion.33
  24.5 32.5 %collective-permute-done = bf16[256,512]{1,0:T(8,128)(2,1)S(1)} collective-permute-done((bf16[256,512]{1,0:T(8,128)(2,1)S(1)}, bf16[256,512]{1,0:T(8,128)(2,1)S(1)}, u32[]{:S(2)}, u32[]{:S(2)}) %collective-permute-start) | collective-permute-done | bytes 262176 | tf_op jit(solution)/shard_map/ppermute | solution.py:12
  56.9 0.3 fusion
  57.2 4.9 %collective-permute-start.1 = (bf16[256,512]{1,0:T(8,128)(2,1)S(1)}, bf16[256,512]{1,0:T(8,128)(2,1)S(1)}, u32[]{:S(2)}, u32[]{:S(2)}) collective-permute-start(bf16[256,512]{1,0:T(8,128)(2,1)S(1)} %fusion), channel_id=1, source_target_pairs={{0,256},{32,288},{64,320},{96,352},{128,384},{160,416},{192,448},{... | collective-permute-start | bytes 786440 | tf_op jit(solution)/shard_map/ppermute | solution.py:12
  62.2 0.0 collective-permute-done.3
  62.2 0.3 fusion.3
  62.5 0.3 fusion.29
  62.8 4.4 %collective-permute-start.4 = (bf16[256,512]{1,0:T(8,128)(2,1)S(1)}, bf16[256,512]{1,0:T(8,128)(2,1)S(1)}, u32[]{:S(2)}, u32[]{:S(2)}) collective-permute-start(bf16[256,512]{1,0:T(8,128)(2,1)S(1)} %fusion.3), channel_id=1, source_target_pairs={{0,256},{32,288},{64,320},{96,352},{128,384},{160,416},{192,448},{... | collective-permute-start | bytes 786440 | tf_op jit(solution)/shard_map/ppermute | solution.py:12
  67.2 0.3 fusion.27
  67.5 0.0 collective-permute-done.1
  67.5 0.3 fusion.1
  67.8 2.8 %collective-permute-start.2 = (bf16[256,512]{1,0:T(8,128)(2,1)S(1)}, bf16[256,512]{1,0:T(8,128)(2,1)S(1)}, u32[]{:S(2)}, u32[]{:S(2)}) collective-permute-start(bf16[256,512]{1,0:T(8,128)(2,1)S(1)} %fusion.1), channel_id=1, source_target_pairs={{0,1},{1,0},{2,3},{3,2},{4,5},{5,4},{6,7},{7,6},{8,9},{9,8},{10,11... | collective-permute-start | bytes 786440 | tf_op jit(solution)/shard_map/ppermute | solution.py:12
  70.7 3.6 %collective-permute-done.4 = bf16[256,512]{1,0:T(8,128)(2,1)S(1)} collective-permute-done((bf16[256,512]{1,0:T(8,128)(2,1)S(1)}, bf16[256,512]{1,0:T(8,128)(2,1)S(1)}, u32[]{:S(2)}, u32[]{:S(2)}) %collective-permute-start.4) | collective-permute-done | bytes 262176 | tf_op jit(solution)/shard_map/ppermute | solution.py:12
  74.3 0.3 fusion.4
  74.6 0.3 fusion.23
  74.9 4.0 %collective-permute-start.5 = (bf16[256,512]{1,0:T(8,128)(2,1)S(1)}, bf16[256,512]{1,0:T(8,128)(2,1)S(1)}, u32[]{:S(2)}, u32[]{:S(2)}) collective-permute-start(bf16[256,512]{1,0:T(8,128)(2,1)S(1)} %fusion.4), channel_id=1, source_target_pairs={{0,1},{1,0},{2,3},{3,2},{4,5},{5,4},{6,7},{7,6},{8,9},{9,8},{10,11... | collective-permute-start | bytes 786440 | tf_op jit(solution)/shard_map/ppermute | solution.py:12
  78.9 0.3 fusion.21
  79.2 1.4 %collective-permute-done.2 = bf16[256,512]{1,0:T(8,128)(2,1)S(1)} collective-permute-done((bf16[256,512]{1,0:T(8,128)(2,1)S(1)}, bf16[256,512]{1,0:T(8,128)(2,1)S(1)}, u32[]{:S(2)}, u32[]{:S(2)}) %collective-permute-start.2) | collective-permute-done | bytes 262176 | tf_op jit(solution)/shard_map/ppermute | solution.py:12
  80.6 0.3 fusion.2
  80.9 0.8 dynamic_update_slice.6
  81.7 2.7 %collective-permute-done.5 = bf16[256,512]{1,0:T(8,128)(2,1)S(1)} collective-permute-done((bf16[256,512]{1,0:T(8,128)(2,1)S(1)}, bf16[256,512]{1,0:T(8,128)(2,1)S(1)}, u32[]{:S(2)}, u32[]{:S(2)}) %collective-permute-start.5) | collective-permute-done | bytes 262176 | tf_op jit(solution)/shard_map/ppermute | solution.py:12
  84.4 1.0 %fusion.6 = bf16[512,512]{1,0:T(8,128)(2,1)} fusion(bf16[512,512]{1,0:T(8,128)(2,1)} %dynamic_update_slice.6, f32[256,512]{1,0:T(8,128)S(1)} %fusion.21, bf16[256,512]{1,0:T(8,128)(2,1)S(1)} %collective-permute-done.5, bf16[1024,512]{1,0:T(8,128)(2,1)S(1)} %convolution_convert_fusion), kind=kOutput, calls=%fused_computation.15 | convolution fusion | flops 134479872 | bytes 1572864 | tf_op jit(solution)/shard_map/dot_general | solution.py:41
Async XLA Ops:
  1.0 55.9 %collective-permute-start = (bf16[256,512]{1,0:T(8,128)(2,1)S(1)}, bf16[256,512]{1,0:T(8,128)(2,1)S(1)}, u32[]{:S(2)}, u32[]{:S(2)}) collective-permute-start(bf16[256,512]{1,0:T(8,128)(2,1)S(1)} %slice.51), channel_id=1, source_target_pairs={{0,16},{1,17},{2,18},{3,19},{4,20},{5,21},{6,22},{7,23},{8,24},{9,... | collective-permute-start | bytes 786440 | tf_op jit(solution)/shard_map/ppermute | solution.py:12
  16.8 45.4 %collective-permute-start.3 = (bf16[256,512]{1,0:T(8,128)(2,1)S(1)}, bf16[256,512]{1,0:T(8,128)(2,1)S(1)}, u32[]{:S(2)}, u32[]{:S(2)}) collective-permute-start(bf16[256,512]{1,0:T(8,128)(2,1)S(1)} %slice.67), channel_id=1, source_target_pairs={{0,16},{1,17},{2,18},{3,19},{4,20},{5,21},{6,22},{7,23},{8,24},{9,... | collective-permute-start | bytes 786440 | tf_op jit(solution)/shard_map/ppermute | solution.py:12
  57.2 10.3 %collective-permute-start.1 = (bf16[256,512]{1,0:T(8,128)(2,1)S(1)}, bf16[256,512]{1,0:T(8,128)(2,1)S(1)}, u32[]{:S(2)}, u32[]{:S(2)}) collective-permute-start(bf16[256,512]{1,0:T(8,128)(2,1)S(1)} %fusion), channel_id=1, source_target_pairs={{0,256},{32,288},{64,320},{96,352},{128,384},{160,416},{192,448},{... | collective-permute-start | bytes 786440 | tf_op jit(solution)/shard_map/ppermute | solution.py:12
  62.8 11.5 %collective-permute-start.4 = (bf16[256,512]{1,0:T(8,128)(2,1)S(1)}, bf16[256,512]{1,0:T(8,128)(2,1)S(1)}, u32[]{:S(2)}, u32[]{:S(2)}) collective-permute-start(bf16[256,512]{1,0:T(8,128)(2,1)S(1)} %fusion.3), channel_id=1, source_target_pairs={{0,256},{32,288},{64,320},{96,352},{128,384},{160,416},{192,448},{... | collective-permute-start | bytes 786440 | tf_op jit(solution)/shard_map/ppermute | solution.py:12
  67.8 12.7 %collective-permute-start.2 = (bf16[256,512]{1,0:T(8,128)(2,1)S(1)}, bf16[256,512]{1,0:T(8,128)(2,1)S(1)}, u32[]{:S(2)}, u32[]{:S(2)}) collective-permute-start(bf16[256,512]{1,0:T(8,128)(2,1)S(1)} %fusion.1), channel_id=1, source_target_pairs={{0,1},{1,0},{2,3},{3,2},{4,5},{5,4},{6,7},{7,6},{8,9},{9,8},{10,11... | collective-permute-start | bytes 786440 | tf_op jit(solution)/shard_map/ppermute | solution.py:12
  74.9 9.4 %collective-permute-start.5 = (bf16[256,512]{1,0:T(8,128)(2,1)S(1)}, bf16[256,512]{1,0:T(8,128)(2,1)S(1)}, u32[]{:S(2)}, u32[]{:S(2)}) collective-permute-start(bf16[256,512]{1,0:T(8,128)(2,1)S(1)} %fusion.4), channel_id=1, source_target_pairs={{0,1},{1,0},{2,3},{3,2},{4,5},{5,4},{6,7},{7,6},{8,9},{9,8},{10,11... | collective-permute-start | bytes 786440 | tf_op jit(solution)/shard_map/ppermute | solution.py:12

commit v12 on v10

--- a/solution.py
+++ b/solution.py
@@ -36,8 +36,10 @@
         panel, source = lax.optimization_barrier((panel, source))
         for level, (axis, bit) in enumerate(plan):
             own, cross = weights[level]
+            total = jnp.dot(panel, own, preferred_element_type=jnp.float32)
+            if level > 0 and chunk + 1 < CHUNKS:
+                panel, total = lax.optimization_barrier((panel, total))
             other = from_partner(panel, axis, bit)
-            total = jnp.dot(panel, own, preferred_element_type=jnp.float32)
             total = total + jnp.dot(other, cross, preferred_element_type=jnp.float32)
             panel = total.astype(jnp.bfloat16)
         outs.append(panel)

time: 85.9 us -> 85.7 us (level)
  the two profiles are of different devices: /device:TPU:48 before, /device:TPU:40 now
where the time goes in v12:
time: 85.7 us; the launch traced here: 85.4 us
  waiting for transfers between devices  40.6 us (47%)
  starting transfers between devices  33.1 us (39%)
  matrix products  5.83 us (7%)
  local copies, waits for them, and re-layouts  4.79 us (6%)
    ppermute x6, waiting for transfers between devices, from_partner(): return lax.ppermute(value, axis, pairs)  40.6 us
    ppermute x6, starting transfers between devices, from_partner(): return lax.ppermute(value, axis, pairs)  33.1 us
    dot_general x3, matrix products, permuted_columns(): jnp.dot(weights, onehot, preferred_element_type=jnp.float32)  2.27 us
    squeeze x1, local copies, waits for them, and re-layouts, per_device(): both = jnp.concatenate([own_blocks[level], cross_blocks[level]], axis=0)  2.03 us
    slice x2, local copies, waits for them, and re-layouts, per_device(): panel = source[chunk * rows:(chunk + 1) * rows]  1.94 us
    dot_general x6, matrix products, per_device(): total = total + jnp.dot(other, cross, preferred_element_type=jnp.float32)  1.79 us
    dot_general x6, matrix products, per_device(): total = jnp.dot(panel, own, preferred_element_type=jnp.float32)  1.76 us
  transfers between devices with their start and end apart: 6, of which 5 were waited for; matrix products, arithmetic and copies ran while one was open for 11% of the time, Pallas kernels for 0%

profile of v12, /device:TPU:40, one launch (start us, length us, event | category | flops | bytes accessed | tf_op | source)
XLA Modules:
  0.0 85.4 jit_solution(8924128262744776370)
XLA Ops:
  0.0 1.0 %slice.51 = bf16[256,512]{1,0:T(8,128)(2,1)S(1)} slice(bf16[512,512]{1,0:T(8,128)(2,1)} %param.4), slice={[0:256], [0:512]} | slice | bytes 524288 | tf_op jit(solution)/shard_map/slice | solution.py:35
  1.0 14.8 %collective-permute-start = (bf16[256,512]{1,0:T(8,128)(2,1)S(1)}, bf16[256,512]{1,0:T(8,128)(2,1)S(1)}, u32[]{:S(2)}, u32[]{:S(2)}) collective-permute-start(bf16[256,512]{1,0:T(8,128)(2,1)S(1)} %slice.51), channel_id=1, source_target_pairs={{0,16},{1,17},{2,18},{3,19},{4,20},{5,21},{6,22},{7,23},{8,24},{9,... | collective-permute-start | bytes 786440 | tf_op jit(solution)/shard_map/ppermute | solution.py:12
  15.8 1.0 %slice.67 = bf16[256,512]{1,0:T(8,128)(2,1)S(1)} slice(bf16[512,512]{1,0:T(8,128)(2,1)} %param.4), slice={[256:512], [0:512]} | slice | bytes 524288 | tf_op jit(solution)/shard_map/slice | solution.py:35
  16.8 1.9 %collective-permute-start.3 = (bf16[256,512]{1,0:T(8,128)(2,1)S(1)}, bf16[256,512]{1,0:T(8,128)(2,1)S(1)}, u32[]{:S(2)}, u32[]{:S(2)}) collective-permute-start(bf16[256,512]{1,0:T(8,128)(2,1)S(1)} %slice.67), channel_id=1, source_target_pairs={{0,16},{1,17},{2,18},{3,19},{4,20},{5,21},{6,22},{7,23},{8,24},{9,... | collective-permute-start | bytes 786440 | tf_op jit(solution)/shard_map/ppermute | solution.py:12
  18.7 0.8 fusion.39
  19.5 2.0 %slice_bitcast_fusion = (bf16[512,512]{1,0:T(8,128)(2,1)S(1)}, bf16[512,512]{1,0:T(8,128)(2,1)S(1)}, bf16[512,512]{1,0:T(8,128)(2,1)S(1)}, bf16[512,512]{1,0:T(8...) fusion(bf16[3,512,512]{2,1,0:T(8,128)(2,1)} %param.6, bf16[3,512,512]{2,1,0:T(8,128)(2,1)} %param.5), kind=kLoop, calls=%fused_computation.29 | loop fusion | bytes 6291456 | tf_op jit(solution)/shard_map/squeeze | solution.py:28
  21.6 0.8 convolution_convert_fusion.2
  22.3 0.3 fusion.34
  22.6 0.8 convolution_convert_fusion.1
  23.4 0.8 convolution_convert_fusion
  24.2 0.3 fusion.32
  24.5 32.5 %collective-permute-done = bf16[256,512]{1,0:T(8,128)(2,1)S(1)} collective-permute-done((bf16[256,512]{1,0:T(8,128)(2,1)S(1)}, bf16[256,512]{1,0:T(8,128)(2,1)S(1)}, u32[]{:S(2)}, u32[]{:S(2)}) %collective-permute-start) | collective-permute-done | bytes 262176 | tf_op jit(solution)/shard_map/ppermute | solution.py:12
  56.9 0.3 fusion
  57.2 0.3 fusion.28
  57.5 4.9 %collective-permute-start.1 = (bf16[256,512]{1,0:T(8,128)(2,1)S(1)}, bf16[256,512]{1,0:T(8,128)(2,1)S(1)}, u32[]{:S(2)}, u32[]{:S(2)}) collective-permute-start(bf16[256,512]{1,0:T(8,128)(2,1)S(1)} %fusion), channel_id=1, source_target_pairs={{0,256},{32,288},{64,320},{96,352},{128,384},{160,416},{192,448},{... | collective-permute-start | bytes 786440 | tf_op jit(solution)/shard_map/ppermute | solution.py:12
  62.5 0.0 collective-permute-done.3
  62.5 0.3 fusion.3
  62.8 4.1 %collective-permute-start.4 = (bf16[256,512]{1,0:T(8,128)(2,1)S(1)}, bf16[256,512]{1,0:T(8,128)(2,1)S(1)}, u32[]{:S(2)}, u32[]{:S(2)}) collective-permute-start(bf16[256,512]{1,0:T(8,128)(2,1)S(1)} %fusion.3), channel_id=1, source_target_pairs={{0,256},{32,288},{64,320},{96,352},{128,384},{160,416},{192,448},{... | collective-permute-start | bytes 786440 | tf_op jit(solution)/shard_map/ppermute | solution.py:12
  66.9 0.3 fusion.26
  67.2 0.2 collective-permute-done.1
  67.5 0.3 fusion.1
  67.8 0.3 fusion.22
  68.1 3.4 %collective-permute-start.2 = (bf16[256,512]{1,0:T(8,128)(2,1)S(1)}, bf16[256,512]{1,0:T(8,128)(2,1)S(1)}, u32[]{:S(2)}, u32[]{:S(2)}) collective-permute-start(bf16[256,512]{1,0:T(8,128)(2,1)S(1)} %fusion.1), channel_id=1, source_target_pairs={{0,1},{1,0},{2,3},{3,2},{4,5},{5,4},{6,7},{7,6},{8,9},{9,8},{10,11... | collective-permute-start | bytes 786440 | tf_op jit(solution)/shard_map/ppermute | solution.py:12
  71.5 2.6 %collective-permute-done.4 = bf16[256,512]{1,0:T(8,128)(2,1)S(1)} collective-permute-done((bf16[256,512]{1,0:T(8,128)(2,1)S(1)}, bf16[256,512]{1,0:T(8,128)(2,1)S(1)}, u32[]{:S(2)}, u32[]{:S(2)}) %collective-permute-start.4) | collective-permute-done | bytes 262176 | tf_op jit(solution)/shard_map/ppermute | solution.py:12
  74.0 0.3 fusion.4
  74.3 3.9 %collective-permute-start.5 = (bf16[256,512]{1,0:T(8,128)(2,1)S(1)}, bf16[256,512]{1,0:T(8,128)(2,1)S(1)}, u32[]{:S(2)}, u32[]{:S(2)}) collective-permute-start(bf16[256,512]{1,0:T(8,128)(2,1)S(1)} %fusion.4), channel_id=1, source_target_pairs={{0,1},{1,0},{2,3},{3,2},{4,5},{5,4},{6,7},{7,6},{8,9},{9,8},{10,11... | collective-permute-start | bytes 786440 | tf_op jit(solution)/shard_map/ppermute | solution.py:12
  78.3 0.3 fusion.20
  78.6 1.7 %collective-permute-done.2 = bf16[256,512]{1,0:T(8,128)(2,1)S(1)} collective-permute-done((bf16[256,512]{1,0:T(8,128)(2,1)S(1)}, bf16[256,512]{1,0:T(8,128)(2,1)S(1)}, u32[]{:S(2)}, u32[]{:S(2)}) %collective-permute-start.2) | collective-permute-done | bytes 262176 | tf_op jit(solution)/shard_map/ppermute | solution.py:12
  80.3 0.3 fusion.2
  80.6 3.7 %collective-permute-done.5 = bf16[256,512]{1,0:T(8,128)(2,1)S(1)} collective-permute-done((bf16[256,512]{1,0:T(8,128)(2,1)S(1)}, bf16[256,512]{1,0:T(8,128)(2,1)S(1)}, u32[]{:S(2)}, u32[]{:S(2)}) %collective-permute-start.5) | collective-permute-done | bytes 262176 | tf_op jit(solution)/shard_map/ppermute | solution.py:12
  84.2 0.3 fusion.5
  84.5 0.8 pad_maximum_fusion
Async XLA Ops:
  1.0 55.9 %collective-permute-start = (bf16[256,512]{1,0:T(8,128)(2,1)S(1)}, bf16[256,512]{1,0:T(8,128)(2,1)S(1)}, u32[]{:S(2)}, u32[]{:S(2)}) collective-permute-start(bf16[256,512]{1,0:T(8,128)(2,1)S(1)} %slice.51), channel_id=1, source_target_pairs={{0,16},{1,17},{2,18},{3,19},{4,20},{5,21},{6,22},{7,23},{8,24},{9,... | collective-permute-start | bytes 786440 | tf_op jit(solution)/shard_map/ppermute | solution.py:12
  16.8 45.7 %collective-permute-start.3 = (bf16[256,512]{1,0:T(8,128)(2,1)S(1)}, bf16[256,512]{1,0:T(8,128)(2,1)S(1)}, u32[]{:S(2)}, u32[]{:S(2)}) collective-permute-start(bf16[256,512]{1,0:T(8,128)(2,1)S(1)} %slice.67), channel_id=1, source_target_pairs={{0,16},{1,17},{2,18},{3,19},{4,20},{5,21},{6,22},{7,23},{8,24},{9,... | collective-permute-start | bytes 786440 | tf_op jit(solution)/shard_map/ppermute | solution.py:12
  57.5 9.9 %collective-permute-start.1 = (bf16[256,512]{1,0:T(8,128)(2,1)S(1)}, bf16[256,512]{1,0:T(8,128)(2,1)S(1)}, u32[]{:S(2)}, u32[]{:S(2)}) collective-permute-start(bf16[256,512]{1,0:T(8,128)(2,1)S(1)} %fusion), channel_id=1, source_target_pairs={{0,256},{32,288},{64,320},{96,352},{128,384},{160,416},{192,448},{... | collective-permute-start | bytes 786440 | tf_op jit(solution)/shard_map/ppermute | solution.py:12
  62.8 11.3 %collective-permute-start.4 = (bf16[256,512]{1,0:T(8,128)(2,1)S(1)}, bf16[256,512]{1,0:T(8,128)(2,1)S(1)}, u32[]{:S(2)}, u32[]{:S(2)}) collective-permute-start(bf16[256,512]{1,0:T(8,128)(2,1)S(1)} %fusion.3), channel_id=1, source_target_pairs={{0,256},{32,288},{64,320},{96,352},{128,384},{160,416},{192,448},{... | collective-permute-start | bytes 786440 | tf_op jit(solution)/shard_map/ppermute | solution.py:12
  68.1 12.2 %collective-permute-start.2 = (bf16[256,512]{1,0:T(8,128)(2,1)S(1)}, bf16[256,512]{1,0:T(8,128)(2,1)S(1)}, u32[]{:S(2)}, u32[]{:S(2)}) collective-permute-start(bf16[256,512]{1,0:T(8,128)(2,1)S(1)} %fusion.1), channel_id=1, source_target_pairs={{0,1},{1,0},{2,3},{3,2},{4,5},{5,4},{6,7},{7,6},{8,9},{9,8},{10,11... | collective-permute-start | bytes 786440 | tf_op jit(solution)/shard_map/ppermute | solution.py:12
  74.3 9.9 %collective-permute-start.5 = (bf16[256,512]{1,0:T(8,128)(2,1)S(1)}, bf16[256,512]{1,0:T(8,128)(2,1)S(1)}, u32[]{:S(2)}, u32[]{:S(2)}) collective-permute-start(bf16[256,512]{1,0:T(8,128)(2,1)S(1)} %fusion.4), channel_id=1, source_target_pairs={{0,1},{1,0},{2,3},{3,2},{4,5},{5,4},{6,7},{7,6},{8,9},{9,8},{10,11... | collective-permute-start | bytes 786440 | tf_op jit(solution)/shard_map/ppermute | solution.py:12

commit v13 on v6

--- a/solution.py
+++ b/solution.py
@@ -3,7 +3,7 @@
 from jax import lax
 from jax.sharding import PartitionSpec as P
 
-CHUNKS = 2
+SPLIT = (3, 5)
 
 
 def from_partner(value, axis, distance):
@@ -28,15 +28,22 @@
         both = jnp.concatenate([own_blocks[level], cross_blocks[level]], axis=0)
         both = permuted_columns(both, level_perm[level])
         weights.append((both[:br], both[br:]))
-    rows = probes.shape[0] // CHUNKS
-    panels = [probes[chunk * rows:(chunk + 1) * rows] for chunk in range(CHUNKS)]
-    weights, panels[1:] = lax.optimization_barrier((weights, panels[1:]))
+    unit = probes.shape[0] // sum(SPLIT)
+    bounds = [unit * sum(SPLIT[:k]) for k in range(len(SPLIT) + 1)]
+    panels = []
+    source = probes
+    for chunk in range(len(SPLIT)):
+        panel, source = lax.optimization_barrier((source[bounds[chunk]:bounds[chunk + 1]], source))
+        panels.append(panel)
+    arrived = [from_partner(panel, *plan[0]) for panel in panels]
     outs = []
-    for chunk in range(CHUNKS):
+    for chunk in range(len(SPLIT)):
         panel = panels[chunk]
         for level, (axis, bit) in enumerate(plan):
             own, cross = weights[level]
-            other = from_partner(panel, axis, bit)
+            other = arrived[chunk] if level == 0 else from_partner(panel, axis, bit)
+            if level == 2 and chunk + 1 < len(SPLIT):
+                panel, arrived[chunk + 1] = lax.optimization_barrier((panel, arrived[chunk + 1]))
             total = jnp.dot(panel, own, preferred_element_type=jnp.float32)
             total = total + jnp.dot(other, cross, preferred_element_type=jnp.float32)
             panel = total.astype(jnp.bfloat16)

time: 93.5 us -> 89.4 us (0.956)
  the two profiles are of different devices: /device:TPU:8 before, /device:TPU:6 now
where the time goes in v13:
time: 89.4 us; the launch traced here: 89 us
  waiting for transfers between devices  48 us (54%)
  starting transfers between devices  29.4 us (33%)
  matrix products  5.82 us (7%)
  local copies, waits for them, and re-layouts  4.79 us (5%)
    ppermute x6, waiting for transfers between devices, from_partner(): return lax.ppermute(value, axis, pairs)  48 us
    ppermute x6, starting transfers between devices, from_partner(): return lax.ppermute(value, axis, pairs)  29.4 us
    dot_general x3, matrix products, permuted_columns(): jnp.dot(weights, onehot, preferred_element_type=jnp.float32)  2.28 us
    squeeze x1, local copies, waits for them, and re-layouts, per_device(): both = jnp.concatenate([own_blocks[level], cross_blocks[level]], axis=0)  2.03 us
    slice x2, local copies, waits for them, and re-layouts, per_device(): source[bounds[chunk]:bounds[chunk + 1]]  1.94 us
  transfers between devices with their start and end apart: 6, of which 5 were waited for; matrix products, arithmetic and copies ran while one was open for 10% of the time, Pallas kernels for 0%

profile of v13, /device:TPU:6, one launch (start us, length us, event | category | flops | bytes accessed | tf_op | source)
XLA Modules:
  0.0 89.0 jit_solution(16615652922185733778)
XLA Ops:
  0.0 0.9 %slice.51 = bf16[192,512]{1,0:T(8,128)(2,1)S(1)} slice(bf16[512,512]{1,0:T(8,128)(2,1)} %param.4), slice={[0:192], [0:512]} | slice | bytes 393216 | tf_op jit(solution)/shard_map/slice | solution.py:36
  0.9 15.7 %collective-permute-start = (bf16[192,512]{1,0:T(8,128)(2,1)S(1)}, bf16[192,512]{1,0:T(8,128)(2,1)S(1)}, u32[]{:S(2)}, u32[]{:S(2)}) collective-permute-start(bf16[192,512]{1,0:T(8,128)(2,1)S(1)} %slice.51), channel_id=1, source_target_pairs={{0,16},{1,17},{2,18},{3,19},{4,20},{5,21},{6,22},{7,23},{8,24},{9,... | collective-permute-start | bytes 589832 | tf_op jit(solution)/shard_map/ppermute | solution.py:12
  16.7 1.0 %slice.62 = bf16[320,512]{1,0:T(8,128)(2,1)S(1)} slice(bf16[512,512]{1,0:T(8,128)(2,1)} %param.4), slice={[192:512], [0:512]} | slice | bytes 655360 | tf_op jit(solution)/shard_map/slice | solution.py:36
  17.7 1.9 %collective-permute-start.2 = (bf16[320,512]{1,0:T(8,128)(2,1)S(1)}, bf16[320,512]{1,0:T(8,128)(2,1)S(1)}, u32[]{:S(2)}, u32[]{:S(2)}) collective-permute-start(bf16[320,512]{1,0:T(8,128)(2,1)S(1)} %slice.62), channel_id=1, source_target_pairs={{0,16},{1,17},{2,18},{3,19},{4,20},{5,21},{6,22},{7,23},{8,24},{9,... | collective-permute-start | bytes 983048 | tf_op jit(solution)/shard_map/ppermute | solution.py:12
  19.6 0.8 fusion.39
  20.4 2.0 %slice_bitcast_fusion = (bf16[512,512]{1,0:T(8,128)(2,1)S(1)}, bf16[512,512]{1,0:T(8,128)(2,1)S(1)}, bf16[512,512]{1,0:T(8,128)(2,1)S(1)}, bf16[512,512]{1,0:T(8...) fusion(bf16[3,512,512]{2,1,0:T(8,128)(2,1)} %param.6, bf16[3,512,512]{2,1,0:T(8,128)(2,1)} %param.5), kind=kLoop, calls=%fused_computation.29 | loop fusion | bytes 6291456 | tf_op jit(solution)/shard_map/squeeze | solution.py:28
  22.5 0.8 convolution_convert_fusion.2
  23.2 0.3 fusion.34
  23.5 0.3 fusion.32
  23.8 0.8 convolution_convert_fusion.1
  24.6 0.8 convolution_convert_fusion
  25.4 5.5 %collective-permute-done = bf16[192,512]{1,0:T(8,128)(2,1)S(1)} collective-permute-done((bf16[192,512]{1,0:T(8,128)(2,1)S(1)}, bf16[192,512]{1,0:T(8,128)(2,1)S(1)}, u32[]{:S(2)}, u32[]{:S(2)}) %collective-permute-start) | collective-permute-done | bytes 196640 | tf_op jit(solution)/shard_map/ppermute | solution.py:12
  30.9 0.3 fusion.3
  31.1 3.3 %collective-permute-start.1 = (bf16[192,512]{1,0:T(8,128)(2,1)S(1)}, bf16[192,512]{1,0:T(8,128)(2,1)S(1)}, u32[]{:S(2)}, u32[]{:S(2)}) collective-permute-start(bf16[192,512]{1,0:T(8,128)(2,1)S(1)} %fusion.3), channel_id=1, source_target_pairs={{0,256},{32,288},{64,320},{96,352},{128,384},{160,416},{192,448},{... | collective-permute-start | bytes 589832 | tf_op jit(solution)/shard_map/ppermute | solution.py:12
  34.4 0.3 fusion.28
  34.7 7.6 %collective-permute-done.1 = bf16[192,512]{1,0:T(8,128)(2,1)S(1)} collective-permute-done((bf16[192,512]{1,0:T(8,128)(2,1)S(1)}, bf16[192,512]{1,0:T(8,128)(2,1)S(1)}, u32[]{:S(2)}, u32[]{:S(2)}) %collective-permute-start.1) | collective-permute-done | bytes 196640 | tf_op jit(solution)/shard_map/ppermute | solution.py:12
  42.3 0.3 fusion.4
  42.6 2.7 %collective-permute-start.3 = (bf16[192,512]{1,0:T(8,128)(2,1)S(1)}, bf16[192,512]{1,0:T(8,128)(2,1)S(1)}, u32[]{:S(2)}, u32[]{:S(2)}) collective-permute-start(bf16[192,512]{1,0:T(8,128)(2,1)S(1)} %fusion.4), channel_id=1, source_target_pairs={{0,1},{1,0},{2,3},{3,2},{4,5},{5,4},{6,7},{7,6},{8,9},{9,8},{10,11... | collective-permute-start | bytes 589832 | tf_op jit(solution)/shard_map/ppermute | solution.py:12
  45.2 21.8 %collective-permute-done.2 = bf16[320,512]{1,0:T(8,128)(2,1)S(1)} collective-permute-done((bf16[320,512]{1,0:T(8,128)(2,1)S(1)}, bf16[320,512]{1,0:T(8,128)(2,1)S(1)}, u32[]{:S(2)}, u32[]{:S(2)}) %collective-permute-start.2) | collective-permute-done | bytes 327712 | tf_op jit(solution)/shard_map/ppermute | solution.py:12
  67.1 0.3 fusion
  67.4 3.3 %collective-permute-start.4 = (bf16[320,512]{1,0:T(8,128)(2,1)S(1)}, bf16[320,512]{1,0:T(8,128)(2,1)S(1)}, u32[]{:S(2)}, u32[]{:S(2)}) collective-permute-start(bf16[320,512]{1,0:T(8,128)(2,1)S(1)} %fusion), channel_id=1, source_target_pairs={{0,256},{32,288},{64,320},{96,352},{128,384},{160,416},{192,448},{... | collective-permute-start | bytes 983048 | tf_op jit(solution)/shard_map/ppermute | solution.py:12
  70.7 0.3 fusion.26
  71.1 0.0 collective-permute-done.3
  71.1 0.3 fusion.19
  71.3 7.2 %collective-permute-done.4 = bf16[320,512]{1,0:T(8,128)(2,1)S(1)} collective-permute-done((bf16[320,512]{1,0:T(8,128)(2,1)S(1)}, bf16[320,512]{1,0:T(8,128)(2,1)S(1)}, u32[]{:S(2)}, u32[]{:S(2)}) %collective-permute-start.4) | collective-permute-done | bytes 327712 | tf_op jit(solution)/shard_map/ppermute | solution.py:12
  78.6 0.3 fusion.1
  78.9 2.5 %collective-permute-start.5 = (bf16[320,512]{1,0:T(8,128)(2,1)S(1)}, bf16[320,512]{1,0:T(8,128)(2,1)S(1)}, u32[]{:S(2)}, u32[]{:S(2)}) collective-permute-start(bf16[320,512]{1,0:T(8,128)(2,1)S(1)} %fusion.1), channel_id=1, source_target_pairs={{0,1},{1,0},{2,3},{3,2},{4,5},{5,4},{6,7},{7,6},{8,9},{9,8},{10,11... | collective-permute-start | bytes 983048 | tf_op jit(solution)/shard_map/ppermute | solution.py:12
  81.4 0.3 fusion.5
  81.6 0.3 fusion.21
  82.0 5.9 %collective-permute-done.5 = bf16[320,512]{1,0:T(8,128)(2,1)S(1)} collective-permute-done((bf16[320,512]{1,0:T(8,128)(2,1)S(1)}, bf16[320,512]{1,0:T(8,128)(2,1)S(1)}, u32[]{:S(2)}, u32[]{:S(2)}) %collective-permute-start.5) | collective-permute-done | bytes 327712 | tf_op jit(solution)/shard_map/ppermute | solution.py:12
  87.9 0.3 fusion.2
  88.2 0.8 pad_maximum_fusion
Async XLA Ops:
  0.9 29.9 %collective-permute-start = (bf16[192,512]{1,0:T(8,128)(2,1)S(1)}, bf16[192,512]{1,0:T(8,128)(2,1)S(1)}, u32[]{:S(2)}, u32[]{:S(2)}) collective-permute-start(bf16[192,512]{1,0:T(8,128)(2,1)S(1)} %slice.51), channel_id=1, source_target_pairs={{0,16},{1,17},{2,18},{3,19},{4,20},{5,21},{6,22},{7,23},{8,24},{9,... | collective-permute-start | bytes 589832 | tf_op jit(solution)/shard_map/ppermute | solution.py:12
  17.7 49.4 %collective-permute-start.2 = (bf16[320,512]{1,0:T(8,128)(2,1)S(1)}, bf16[320,512]{1,0:T(8,128)(2,1)S(1)}, u32[]{:S(2)}, u32[]{:S(2)}) collective-permute-start(bf16[320,512]{1,0:T(8,128)(2,1)S(1)} %slice.62), channel_id=1, source_target_pairs={{0,16},{1,17},{2,18},{3,19},{4,20},{5,21},{6,22},{7,23},{8,24},{9,... | collective-permute-start | bytes 983048 | tf_op jit(solution)/shard_map/ppermute | solution.py:12
  31.1 11.2 %collective-permute-start.1 = (bf16[192,512]{1,0:T(8,128)(2,1)S(1)}, bf16[192,512]{1,0:T(8,128)(2,1)S(1)}, u32[]{:S(2)}, u32[]{:S(2)}) collective-permute-start(bf16[192,512]{1,0:T(8,128)(2,1)S(1)} %fusion.3), channel_id=1, source_target_pairs={{0,256},{32,288},{64,320},{96,352},{128,384},{160,416},{192,448},{... | collective-permute-start | bytes 589832 | tf_op jit(solution)/shard_map/ppermute | solution.py:12
  42.6 28.5 %collective-permute-start.3 = (bf16[192,512]{1,0:T(8,128)(2,1)S(1)}, bf16[192,512]{1,0:T(8,128)(2,1)S(1)}, u32[]{:S(2)}, u32[]{:S(2)}) collective-permute-start(bf16[192,512]{1,0:T(8,128)(2,1)S(1)} %fusion.4), channel_id=1, source_target_pairs={{0,1},{1,0},{2,3},{3,2},{4,5},{5,4},{6,7},{7,6},{8,9},{9,8},{10,11... | collective-permute-start | bytes 589832 | tf_op jit(solution)/shard_map/ppermute | solution.py:12
  67.4 11.2 %collective-permute-start.4 = (bf16[320,512]{1,0:T(8,128)(2,1)S(1)}, bf16[320,512]{1,0:T(8,128)(2,1)S(1)}, u32[]{:S(2)}, u32[]{:S(2)}) collective-permute-start(bf16[320,512]{1,0:T(8,128)(2,1)S(1)} %fusion), channel_id=1, source_target_pairs={{0,256},{32,288},{64,320},{96,352},{128,384},{160,416},{192,448},{... | collective-permute-start | bytes 983048 | tf_op jit(solution)/shard_map/ppermute | solution.py:12
  78.9 9.0 %collective-permute-start.5 = (bf16[320,512]{1,0:T(8,128)(2,1)S(1)}, bf16[320,512]{1,0:T(8,128)(2,1)S(1)}, u32[]{:S(2)}, u32[]{:S(2)}) collective-permute-start(bf16[320,512]{1,0:T(8,128)(2,1)S(1)} %fusion.1), channel_id=1, source_target_pairs={{0,1},{1,0},{2,3},{3,2},{4,5},{5,4},{6,7},{7,6},{8,9},{9,8},{10,11... | collective-permute-start | bytes 983048 | tf_op jit(solution)/shard_map/ppermute | solution.py:12
